TPU v7x, 128 devices: a whole 4x4x4 slice. The times are simulated.
128 devices in a mesh: group: 4 (over y_lo, core), fsdp: 32 (over y_hi, x, z).
Axes of the slice: x: 4, y: 4 (y_hi: 2, y_lo: 2; y = y_hi * 2 + y_lo), z: 4, core: 2. Of those that a mesh axis runs over, the one named last changes fastest.
Arguments:
- anchor: bfloat16 [8192, 1024], P('fsdp'), may hold values from -6 to 6
- pseudo_grads: bfloat16 [4, 8192, 1024], P('group', 'fsdp'), may hold values from -1.5 to 1.5
- outer_moment: float32 [8192, 1024], P('fsdp'), may hold values from -1.2 to 1.2
- adam_first: float32 [4, 8192, 1024], P('group', 'fsdp'), may hold values from -1.8 to 1.8
- adam_second: float32 [4, 8192, 1024], P('group', 'fsdp'), may hold values from 0.25 to 4
- inputs: bfloat16 [32768, 8192], P(('group', 'fsdp')), may hold values from -24 to 24
- key_cotangent: bfloat16 [32768, 1024], P(('group', 'fsdp')), may hold values from -6 to 6
Outputs:
- new_anchor: bfloat16 [8192, 1024], P('fsdp')
- new_moment: float32 [8192, 1024], P('fsdp')
- inner_weights: bfloat16 [4, 8192, 1024], P('group', 'fsdp')
- first_moment: float32 [4, 8192, 1024], P('group', 'fsdp')
- second_moment: float32 [4, 8192, 1024], P('group', 'fsdp')
- input_grad: bfloat16 [32768, 8192], P(('group', 'fsdp'))
All inputs are finite; a program needn't handle non-finite values.
Results may differ from a plain program's by a relative error of at most 0.012.
Values may be sent and summed in bfloat16 or wider, within the bound.
No kernel may reach another device: no remote copies, remote signals or barrier semaphores. Data moves between devices by JAX's collectives and lax.ppermute only.
A program may use at most 128 MiB of HBM per device.

v0:
```python
import jax
import jax.numpy as jnp
from jax import lax
from jax.sharding import PartitionSpec as P

OUTER_RATE = 0.7
MOMENTUM = 0.9
INNER_RATE = 0.05
BETA_ONE = 0.9
BETA_TWO = 0.95
ADAM_EPS = 1e-08
DECAY = 0.1
ADAM_STEP = 100


def per_device(anchor, pseudo_grads, outer_moment, adam_first, adam_second, inputs, key_cotangent):
    width = inputs.shape[1]
    scale = width ** (-0.5)
    workers = lax.axis_size("group")
    total = lax.psum(pseudo_grads[0].astype(jnp.float32).astype(jnp.bfloat16), "group").astype(
        jnp.float32
    )
    mean_delta = total / workers
    new_moment = MOMENTUM * outer_moment + mean_delta
    new_anchor = (
        anchor.astype(jnp.float32) - OUTER_RATE * (mean_delta + MOMENTUM * new_moment)
    ).astype(jnp.bfloat16)
    product = jnp.einsum(
        "tk,dk->td",
        key_cotangent,
        lax.all_gather(new_anchor, "fsdp", axis=0, tiled=True),
        preferred_element_type=jnp.float32,
    )
    input_grad = (product * scale).astype(jnp.bfloat16)
    grads = lax.psum_scatter(
        (
            jnp.einsum("td,tk->dk", inputs, key_cotangent, preferred_element_type=jnp.float32)
            * scale
        ).astype(jnp.bfloat16),
        "fsdp",
        scatter_dimension=0,
        tiled=True,
    ).astype(jnp.float32)
    correct_one = 1.0 - BETA_ONE**ADAM_STEP
    correct_two = 1.0 - BETA_TWO**ADAM_STEP
    first_moment = BETA_ONE * adam_first[0] + (1.0 - BETA_ONE) * grads
    second_moment = BETA_TWO * adam_second[0] + (1.0 - BETA_TWO) * grads * grads
    step_size = first_moment / correct_one / (jnp.sqrt(second_moment / correct_two) + ADAM_EPS)
    inner_weights = (
        new_anchor.astype(jnp.float32) * (1.0 - INNER_RATE * DECAY) - INNER_RATE * step_size
    ).astype(jnp.bfloat16)
    return (
        new_anchor,
        new_moment,
        inner_weights[None],
        first_moment[None],
        second_moment[None],
        input_grad,
    )


def solution(mesh):
    return jax.shard_map(
        per_device,
        mesh=mesh,
        in_specs=(
            P("fsdp", None),
            P("group", "fsdp", None),
            P("fsdp", None),
            P("group", "fsdp", None),
            P("group", "fsdp", None),
            P(("group", "fsdp"), None),
            P(("group", "fsdp"), None),
        ),
        out_specs=(
            P("fsdp", None),
            P("fsdp", None),
            P("group", "fsdp", None),
            P("group", "fsdp", None),
            P("group", "fsdp", None),
            P(("group", "fsdp"), None),
        ),
        check_vma=False,
    )
```

profile of v0, /device:TPU:6, one launch (start us, length us, event | category | flops | bytes accessed | tf_op | source)
XLA Modules:
  0.0 429.7 jit_solution(17225618997235193867)
XLA Ops:
  8.0 0.0 copy-start
  8.0 0.0 all-reduce.2.cloned.1.call-start
  8.1 0.7 all-reduce.2.cloned.1.call-update
  8.7 0.0 reduce-scatter.2.cloned.1.call-start
  8.8 0.2 copy-done
  9.0 10.5 %multiply_convert_fusion = bf16[8192,1024]{1,0:T(8,128)(2,1)} fusion(bf16[256,8192]{1,0:T(8,128)(2,1)} %param.12, bf16[256,1024]{1,0:T(8,128)(2,1)S(1)} %copy-done), kind=kOutput, calls=%fused_computation | convolution fusion | flops 4311744512 | bytes 21495808 | tf_op jit(solution)/shard_map/td,tk->dk/dot_general | solution.py:37
  19.5 0.0 copy-start.1
  19.5 0.0 copy-start.2
  19.5 0.0 copy-start.3
  19.5 0.0 reduce-scatter.2.cloned.1.call-update
  19.5 0.0 all-gather.2.cloned.1.call-start
  19.6 63.0 %all-reduce.2.cloned.1.call-done = bf16[256,1024]{1,0:T(8,128)(2,1)} async-done(((bf16[256,1024]{1,0:T(8,128)(2,1)}), bf16[256,1024]{1,0:T(8,128)(2,1)}) %all-reduce.2.cloned.1.call-update) | async-done | bytes 524304 | tf_op jit(solution)/shard_map/psum | solution.py:20
  82.6 156.5 %reduce-scatter.2.cloned.1.call-done = bf16[256,1024]{1,0:T(8,128)(2,1)} async-done(((bf16[8192,1024]{1,0:T(8,128)(2,1)}), bf16[256,1024]{1,0:T(8,128)(2,1)}) %reduce-scatter.2.cloned.1.call-update) | async-done | bytes 524304 | tf_op jit(solution)/shard_map/reduce_scatter | solution.py:35
  239.1 0.0 copy-done.1
  239.1 0.0 copy-done.2
  239.1 0.0 copy-done.3
  239.1 4.0 fusion.6
  243.0 0.0 all-gather.2.cloned.1.call-update
  243.0 160.7 %all-gather.2.cloned.1.call-done = bf16[8192,1024]{1,0:T(8,128)(2,1)} async-done(((bf16[256,1024]{1,0:T(8,128)(2,1)}), bf16[8192,1024]{1,0:T(8,128)(2,1)}) %all-gather.2.cloned.1.call-update) | async-done | bytes 16777232 | tf_op jit(solution)/shard_map/all_gather | solution.py:31
  403.7 12.3 %fusion.1 = bf16[256,8192]{0,1:T(8,128)(2,1)} fusion(bf16[8192,1024]{1,0:T(8,128)(2,1)} %all-gather.2.cloned.1.call-done, bf16[256,1024]{1,0:T(8,128)(2,1)S(1)} %copy-done), kind=kOutput, calls=%fused_computation.3 | convolution fusion | flops 4299161600 | bytes 21495808 | tf_op jit(solution)/shard_map/tk,dk->td/dot_general | solution.py:28
  416.0 6.3 %copy.13 = bf16[256,8192]{1,0:T(8,128)(2,1)} copy(bf16[256,8192]{0,1:T(8,128)(2,1)} %fusion.1) | data formatting | bytes 8388608
Async XLA Ops:
  8.0 1.0 copy-start
  8.0 74.6 %all-reduce.2.cloned.1.call-start = ((), (), s32[]{:S(2)}) async-start(), calls=%async_computation.1 | async-start | bytes 1048576 | tf_op jit(solution)/shard_map/psum | solution.py:20
  8.7 230.3 %reduce-scatter.2.cloned.1.call-start = ((), (), s32[]{:S(2)}) async-start(), calls=%async_computation.2 | async-start | bytes 17301504 | tf_op jit(solution)/shard_map/reduce_scatter | solution.py:35
  19.5 219.6 %copy-start.1 = (f32[1,256,1024]{2,1,0:T(8,128)S(1)}, f32[1,256,1024]{2,1,0:T(8,128)}, u32[]{:S(2)}) copy-start(f32[1,256,1024]{2,1,0:T(8,128)} %param.11) | copy-start | bytes 3145732
  19.5 219.6 %copy-start.2 = (f32[1,256,1024]{2,1,0:T(8,128)S(1)}, f32[1,256,1024]{2,1,0:T(8,128)}, u32[]{:S(2)}) copy-start(f32[1,256,1024]{2,1,0:T(8,128)} %param.10) | copy-start | bytes 3145732
  19.5 219.6 %copy-start.3 = (bf16[256,1024]{1,0:T(8,128)(2,1)S(1)}, bf16[256,1024]{1,0:T(8,128)(2,1)}, u32[]{:S(2)}) copy-start(bf16[256,1024]{1,0:T(8,128)(2,1)} %param.7) | copy-start | bytes 1572868
  19.5 384.2 %all-gather.2.cloned.1.call-start = ((), (), s32[]{:S(2)}) async-start(), calls=%async_computation.3 | async-start | bytes 17301504 | tf_op jit(solution)/shard_map/all_gather | solution.py:31
Sparse Core Ops, SparseCore 0:
  11.3 71.2 all-reduce.1
Sparse Core Ops, SparseCore 1:
  19.6 219.4 reduce-scatter.1
  243.1 160.5 all-gather.1
where the time goes:
time: 430 us
  waiting for transfers between devices  381 us (89%)
  matrix products  22.7 us (5%)
  between operations  15.5 us (4%)
  local copies, waits for them, and re-layouts  6.58 us (2%)
    all_gather x1, waiting for transfers between devices, per_device(): lax.all_gather(new_anchor, 'fsdp', axis=0, tiled=True)  161 us
    reduce_scatter x1, waiting for transfers between devices, per_device(): lax.psum_scatter((jnp.einsum('td,tk->dk', inputs, key_cotangent, preferre...  156 us
    psum x1, waiting for transfers between devices, per_device(): lax.psum(pseudo_grads[0].astype(jnp.float32).astype(jnp.bfloat16), 'group')  63 us
    dot_general x1, matrix products, per_device(): jnp.einsum('tk,dk->td', key_cotangent, lax.all_gather(new_anchor, 'fsdp',...  12.3 us
    dot_general x1, matrix products, per_device(): jnp.einsum('td,tk->dk', inputs, key_cotangent, preferred_element_type=jnp...  10.5 us
  transfers between devices with their start and end apart: 3, of which 3 were waited for; matrix products, arithmetic and copies ran while one was open for 2% of the time, Pallas kernels for 0%

commit v1 on v0

--- a/solution.py
+++ b/solution.py
@@ -17,30 +17,24 @@
     width = inputs.shape[1]
     scale = width ** (-0.5)
     workers = lax.axis_size("group")
-    total = lax.psum(pseudo_grads[0].astype(jnp.float32).astype(jnp.bfloat16), "group").astype(
-        jnp.float32
-    )
+
+    cot_full = lax.all_gather(key_cotangent, "fsdp", axis=0, tiled=True)
+    inputs_cols = lax.all_to_all(inputs, "fsdp", split_axis=1, concat_axis=0, tiled=True)
+
+    total = lax.psum(pseudo_grads[0], "group").astype(jnp.float32)
     mean_delta = total / workers
     new_moment = MOMENTUM * outer_moment + mean_delta
     new_anchor = (
         anchor.astype(jnp.float32) - OUTER_RATE * (mean_delta + MOMENTUM * new_moment)
     ).astype(jnp.bfloat16)
-    product = jnp.einsum(
-        "tk,dk->td",
-        key_cotangent,
-        lax.all_gather(new_anchor, "fsdp", axis=0, tiled=True),
-        preferred_element_type=jnp.float32,
+
+    product = jnp.einsum("tk,dk->td", cot_full, new_anchor, preferred_element_type=jnp.float32)
+    input_cols = (product * scale).astype(jnp.bfloat16)
+    input_grad = lax.all_to_all(input_cols, "fsdp", split_axis=0, concat_axis=1, tiled=True)
+
+    grads = (
+        jnp.einsum("td,tk->dk", inputs_cols, cot_full, preferred_element_type=jnp.float32) * scale
     )
-    input_grad = (product * scale).astype(jnp.bfloat16)
-    grads = lax.psum_scatter(
-        (
-            jnp.einsum("td,tk->dk", inputs, key_cotangent, preferred_element_type=jnp.float32)
-            * scale
-        ).astype(jnp.bfloat16),
-        "fsdp",
-        scatter_dimension=0,
-        tiled=True,
-    ).astype(jnp.float32)
     correct_one = 1.0 - BETA_ONE**ADAM_STEP
     correct_two = 1.0 - BETA_TWO**ADAM_STEP
     first_moment = BETA_ONE * adam_first[0] + (1.0 - BETA_ONE) * grads

time: 430 us -> 302 us (0.70)
  waiting for transfers between devices: 381 us -> 119 us
  blocking collectives: 0 us -> 124 us
  local copies, waits for them, and re-layouts: 6.58 us -> 20 us
    reduce_scatter x1 -> x0, waiting for transfers between devices: 156 us -> none  [per_device(): lax.psum_scatter((jnp.einsum('td,tk->dk', inputs, key_cotangent, preferre...]
    all_to_all x0 -> x2, blocking collectives: none -> 124 us  [the longest x1 67.9 us: per_device(): lax.all_to_all(inputs, 'fsdp', split_axis=1, concat_axis=0, tiled=True)]
    psum x1, waiting for transfers between devices: 63 us -> 0.01 us  [per_device(): total = lax.psum(pseudo_grads[0], 'group').astype(jnp.float32)]
    all_gather x1, waiting for transfers between devices: 161 us -> 118 us  [per_device(): cot_full = lax.all_gather(key_cotangent, 'fsdp', axis=0, tiled=True)]
    all_to_all x0 -> x2, local copies, waits for them, and re-layouts: none -> 7.26 us  [the longest x1 6.76 us: per_device(): lax.all_to_all(inputs, 'fsdp', split_axis=1, concat_axis=0, tiled=True)]
    unnamed x9 -> x10, local copies, waits for them, and re-layouts: 6.58 us -> 12.7 us
  transfers between devices with their start and end apart: 3 -> 2, of which waited for: 3 -> 1; matrix products, arithmetic and copies ran while one was open for 2% -> 4% of each run, Pallas kernels for 0% -> 0%
where the time goes in v1:
time: 302 us
  blocking collectives  124 us (41%)
  waiting for transfers between devices  119 us (39%)
  matrix products  22.8 us (8%)
  local copies, waits for them, and re-layouts  20 us (7%)
  between operations  15.5 us (5%)
    all_gather x1, waiting for transfers between devices, per_device(): cot_full = lax.all_gather(key_cotangent, 'fsdp', axis=0, tiled=True)  118 us
    all_to_all x1, blocking collectives, per_device(): lax.all_to_all(inputs, 'fsdp', split_axis=1, concat_axis=0, tiled=True)  67.9 us
    all_to_all x1, blocking collectives, per_device(): lax.all_to_all(input_cols, 'fsdp', split_axis=0, concat_axis=1, tiled=True)  56.2 us
    dot_general x1, matrix products, per_device(): jnp.einsum('td,tk->dk', inputs_cols, cot_full, preferred_element_type=jnp...  14.5 us
    unnamed x10, local copies, waits for them, and re-layouts  12.7 us
    dot_general x1, matrix products, per_device(): jnp.einsum('tk,dk->td', cot_full, new_anchor, preferred_element_type=jnp....  8.35 us
    all_to_all x1, local copies, waits for them, and re-layouts, per_device(): lax.all_to_all(inputs, 'fsdp', split_axis=1, concat_axis=0, tiled=True)  6.76 us
  transfers between devices with their start and end apart: 2, of which 1 were waited for; matrix products, arithmetic and copies ran while one was open for 4% of the time, Pallas kernels for 0%

profile of v1, /device:TPU:6, one launch (start us, length us, event | category | flops | bytes accessed | tf_op | source)
XLA Modules:
  0.0 301.6 jit_solution(12922551793617736811)
XLA Ops:
  8.0 0.0 all-reduce.2.cloned.1.call-start
  8.0 0.7 all-reduce.2.cloned.1.call-update
  8.7 0.0 all-gather.2.cloned.1.call-start
  8.8 0.5 all-gather.2.cloned.1.call-update
  9.3 6.4 %copy.18 = bf16[256,8192]{0,1:T(8,128)(2,1)} copy(bf16[256,8192]{1,0:T(8,128)(2,1)} %param.12) | data formatting | bytes 8388608 | tf_op args[5]
  15.7 67.9 %all_to_all.38 = bf16[256,32,256]{0,2,1:T(8,128)(2,1)} all-to-all(bf16[256,32,256]{0,2,1:T(8,128)(2,1)} %bitcast.38), channel_id=1, replica_groups=mesh['group'=4,'fsdp'=32] {'fsdp'}, dimensions={1} | all-to-all | bytes 8388608 | tf_op jit(solution)/shard_map/all_to_all | solution.py:22
  83.6 0.0 copy-start
  83.6 0.0 copy-start.1
  83.6 0.0 copy-start.2
  83.6 6.8 %copy.19 = bf16[32,256,256]{2,1,0:T(8,128)(2,1)} copy(bf16[32,256,256]{1,2,0:T(8,128)(2,1)} %bitcast.35) | data formatting | bytes 8388608 | tf_op jit(solution)/shard_map/all_to_all | solution.py:22
  90.3 0.0 all-reduce.2.cloned.1.call-done
  90.3 118.0 %all-gather.2.cloned.1.call-done = bf16[8192,1024]{1,0:T(8,128)(2,1)} async-done(((bf16[256,1024]{1,0:T(8,128)(2,1)}), bf16[8192,1024]{1,0:T(8,128)(2,1)}) %all-gather.2.cloned.1.call-update) | async-done | bytes 16777232 | tf_op jit(solution)/shard_map/all_gather | solution.py:21
  208.3 0.0 copy-done
  208.3 0.0 copy-done.1
  208.4 0.0 copy-done.2
  208.4 14.5 %fusion.1 = (bf16[1,256,1024]{2,1,0:T(8,128)(2,1)}, bf16[256,1024]{1,0:T(8,128)(2,1)S(1)}, f32[256,1024]{1,0:T(8,128)}, f32[1,256,1024]{2,1,0:T(8,128)}, f32[1,256,1024]{2,1,0:T(8,128)}) fusion(f32[1,256,1024]{2,1,0:T(8,128)S(1)} %copy-done, f32[1,256,1024]{2,1,0:T(8,128)S(1)} %copy-done.1, bf16[256,1024]{1,0:T(8,128)(2,1)} %all-reduce.2.cloned.1.call-done, ...), kind=kOutput, calls=%fused_computation.9 | convolution fusion | flops 4302045184 | bytes 29360128 | tf_op jit(solution)/shard_map/td,tk->dk/dot_general | solution.py:36
  222.8 0.0 copy-start.3
  222.8 8.3 %fusion = bf16[256,8192]{1,0:T(8,128)(2,1)S(1)} fusion(bf16[256,1024]{1,0:T(8,128)(2,1)S(1)} %get-tuple-element.13, bf16[8192,1024]{1,0:T(8,128)(2,1)} %all-gather.2.cloned.1.call-done), kind=kOutput, calls=%fused_computation.1 | convolution fusion | flops 4299161600 | bytes 21495808 | tf_op jit(solution)/shard_map/tk,dk->td/dot_general | solution.py:31
  231.2 0.0 copy-done.3
  231.2 0.5 copy.24
  231.7 56.2 %all_to_all.39 = bf16[32,256,256]{1,2,0:T(8,128)(2,1)} all-to-all(bf16[32,256,256]{1,2,0:T(8,128)(2,1)S(1)} %bitcast.36), channel_id=1, replica_groups=mesh['group'=4,'fsdp'=32] {'fsdp'}, dimensions={0} | all-to-all | bytes 8388608 | tf_op jit(solution)/shard_map/all_to_all | solution.py:33
  287.9 6.3 %copy.21 = bf16[256,8192]{1,0:T(8,128)(2,1)} copy(bf16[256,8192]{0,1:T(8,128)(2,1)} %bitcast.37) | data formatting | bytes 8388608
Async XLA Ops:
  8.0 82.3 %all-reduce.2.cloned.1.call-start = ((), (), s32[]{:S(2)}) async-start(), calls=%async_computation.2 | async-start | bytes 1048576 | tf_op jit(solution)/shard_map/psum | solution.py:24
  8.7 199.6 %all-gather.2.cloned.1.call-start = ((), (), s32[]{:S(2)}) async-start(), calls=%async_computation.3 | async-start | bytes 17301504 | tf_op jit(solution)/shard_map/all_gather | solution.py:21
  83.6 124.8 %copy-start = (f32[1,256,1024]{2,1,0:T(8,128)S(1)}, f32[1,256,1024]{2,1,0:T(8,128)}, u32[]{:S(2)}) copy-start(f32[1,256,1024]{2,1,0:T(8,128)} %param.10) | copy-start | bytes 3145732
  83.6 124.8 %copy-start.1 = (f32[1,256,1024]{2,1,0:T(8,128)S(1)}, f32[1,256,1024]{2,1,0:T(8,128)}, u32[]{:S(2)}) copy-start(f32[1,256,1024]{2,1,0:T(8,128)} %param.11) | copy-start | bytes 3145732
  83.6 124.8 %copy-start.2 = (f32[256,1024]{1,0:T(8,128)S(1)}, f32[256,1024]{1,0:T(8,128)}, u32[]{:S(2)}) copy-start(f32[256,1024]{1,0:T(8,128)} %param.9) | copy-start | bytes 3145732
  222.8 8.4 %copy-start.3 = (bf16[256,1024]{1,0:T(8,128)(2,1)}, bf16[256,1024]{1,0:T(8,128)(2,1)S(1)}, u32[]{:S(2)}) copy-start(bf16[256,1024]{1,0:T(8,128)(2,1)S(1)} %get-tuple-element.13) | copy-start | bytes 1572868
Sparse Core Ops, SparseCore 0:
  11.3 73.7 all-reduce.1
Sparse Core Ops, SparseCore 1:
  12.4 195.9 all-gather.1

commit v2 on v1

v2 whole, which is shorter than its diff:
```python
import jax
import jax.numpy as jnp
from jax import lax
from jax.sharding import Mesh
from jax.sharding import PartitionSpec as P

OUTER_RATE = 0.7
MOMENTUM = 0.9
INNER_RATE = 0.05
BETA_ONE = 0.9
BETA_TWO = 0.95
ADAM_EPS = 1e-08
DECAY = 0.1
ADAM_STEP = 100

GROUP = ("y_lo", "core")
TEAMS = ("y_hi", "x")
TEAM = "z"
FSDP = TEAMS + (TEAM,)


def per_device(anchor, pseudo_grads, outer_moment, adam_first, adam_second, inputs, key_cotangent):
    tok, width = inputs.shape
    rows, kv = anchor.shape
    scale = width ** (-0.5)
    workers = lax.axis_size(GROUP)
    teams = lax.axis_size(TEAMS)
    team = lax.axis_size(TEAM)

    cot_team = lax.all_gather(key_cotangent, TEAM, axis=0, tiled=True)
    inputs_part = lax.all_to_all(
        inputs.reshape(tok, teams, team, rows), TEAM, split_axis=2, concat_axis=0, tiled=True
    ).reshape(team * tok, teams * rows)

    total = lax.psum(pseudo_grads[0], GROUP).astype(jnp.float32)
    mean_delta = total / workers
    new_moment = MOMENTUM * outer_moment + mean_delta
    new_anchor = (
        anchor.astype(jnp.float32) - OUTER_RATE * (mean_delta + MOMENTUM * new_moment)
    ).astype(jnp.bfloat16)
    new_anchor = lax.optimization_barrier(new_anchor)

    anchor_part = lax.all_gather(new_anchor, TEAMS, axis=0, tiled=True)
    product = jnp.einsum("tk,dk->td", cot_team, anchor_part, preferred_element_type=jnp.float32)
    input_part = (product * scale).astype(jnp.bfloat16)
    input_grad = lax.all_to_all(
        input_part.reshape(team, tok, teams, 1, rows), TEAM, split_axis=0, concat_axis=3, tiled=True
    ).reshape(tok, width)

    partial = (
        jnp.einsum("td,tk->dk", inputs_part, cot_team, preferred_element_type=jnp.float32) * scale
    ).astype(jnp.bfloat16)
    grads = lax.psum_scatter(partial, TEAMS, scatter_dimension=0, tiled=True).astype(jnp.float32)

    correct_one = 1.0 - BETA_ONE**ADAM_STEP
    correct_two = 1.0 - BETA_TWO**ADAM_STEP
    first_moment = BETA_ONE * adam_first[0] + (1.0 - BETA_ONE) * grads
    second_moment = BETA_TWO * adam_second[0] + (1.0 - BETA_TWO) * grads * grads
    step_size = first_moment / correct_one / (jnp.sqrt(second_moment / correct_two) + ADAM_EPS)
    inner_weights = (
        new_anchor.astype(jnp.float32) * (1.0 - INNER_RATE * DECAY) - INNER_RATE * step_size
    ).astype(jnp.bfloat16)
    return (
        new_anchor,
        new_moment,
        inner_weights[None],
        first_moment[None],
        second_moment[None],
        input_grad,
    )


def physical_mesh(mesh):
    groups = mesh.shape["group"]
    shards = mesh.shape["fsdp"]
    cores = 2
    y_hi = 2
    x = int(round((shards // y_hi) ** 0.5))
    devices = mesh.devices.reshape(groups // cores, cores, y_hi, x, shards // (y_hi * x))
    return Mesh(devices, GROUP + FSDP)


def solution(mesh):
    pmesh = physical_mesh(mesh)
    rows = P(FSDP, None)
    stacked = P(GROUP, FSDP, None)
    tokens = P(GROUP + FSDP, None)
    return jax.shard_map(
        per_device,
        mesh=pmesh,
        in_specs=(rows, stacked, rows, stacked, stacked, tokens, tokens),
        out_specs=(rows, rows, stacked, stacked, stacked, tokens),
        check_vma=False,
    )
```

time: 302 us -> 228 us (0.75)
  waiting for transfers between devices: 119 us -> 47 us
  blocking collectives: 124 us -> 105 us
  local copies, waits for them, and re-layouts: 20 us -> 35.2 us
  other arithmetic: 0 us -> 6.39 us
  matrix products: 22.8 us -> 17.7 us
    all_gather x1 -> x2, waiting for transfers between devices: 118 us -> 0.03 us  [the longest x1 0.03 us: per_device(): anchor_part = lax.all_gather(new_anchor, TEAMS, axis=0, tiled=True)]
    psum x1, waiting for transfers between devices: 0.01 us -> 42.2 us  [per_device(): total = lax.psum(pseudo_grads[0], GROUP).astype(jnp.float32)]
    reshape x0 -> x4, local copies, waits for them, and re-layouts: none -> 21.4 us  [the longest x2 10.9 us: per_device(): input_part.reshape(team, tok, teams, 1, rows)]
    all_to_all x2, blocking collectives: 124 us -> 105 us  [the longest x1 53.6 us: per_device(): lax.all_to_all(inputs.reshape(tok, teams, team, rows), TEAM, split_axis=2...]
    dot_general x2, matrix products: 22.8 us -> 17.7 us  [the longest x1 9.4 us: per_device(): jnp.einsum('td,tk->dk', inputs_part, cot_team, preferred_element_type=jnp...]
    all_to_all x2 -> x1, local copies, waits for them, and re-layouts: 7.26 us -> 2.24 us  [per_device(): lax.all_to_all(input_part.reshape(team, tok, teams, 1, rows), TEAM, split...]
    reduce_scatter x0 -> x1, waiting for transfers between devices: none -> 3.55 us  [per_device(): lax.psum_scatter(partial, TEAMS, scatter_dimension=0, tiled=True)]
    broadcast_in_dim x0 -> x1, other arithmetic: none -> 3.36 us  [per_device(): second_moment[None]]
  transfers between devices with their start and end apart: 2 -> 4, of which waited for: 1 -> 2; matrix products, arithmetic and copies ran while one was open for 4% -> 24% of each run, Pallas kernels for 0% -> 0%
where the time goes in v2:
time: 228 us; the launch traced here: 227 us
  blocking collectives  105 us (46%)
  waiting for transfers between devices  47 us (21%)
  local copies, waits for them, and re-layouts  35.2 us (15%)
  matrix products  17.7 us (8%)
  between operations  15.7 us (7%)
  other arithmetic  6.39 us (3%)
    all_to_all x1, blocking collectives, per_device(): lax.all_to_all(inputs.reshape(tok, teams, team, rows), TEAM, split_axis=2...  53.6 us
    all_to_all x1, blocking collectives, per_device(): lax.all_to_all(input_part.reshape(team, tok, teams, 1, rows), TEAM, split...  51 us
    psum x1, waiting for transfers between devices, per_device(): total = lax.psum(pseudo_grads[0], GROUP).astype(jnp.float32)  42.2 us
    unnamed x10, local copies, waits for them, and re-layouts  11.5 us
    reshape x2, local copies, waits for them, and re-layouts, per_device(): input_part.reshape(team, tok, teams, 1, rows)  10.9 us
    reshape x2, local copies, waits for them, and re-layouts, per_device(): inputs.reshape(tok, teams, team, rows)  10.5 us
    dot_general x1, matrix products, per_device(): jnp.einsum('td,tk->dk', inputs_part, cot_team, preferred_element_type=jnp...  9.4 us
    dot_general x1, matrix products, per_device(): jnp.einsum('tk,dk->td', cot_team, anchor_part, preferred_element_type=jnp...  8.29 us
  transfers between devices with their start and end apart: 4, of which 2 were waited for; matrix products, arithmetic and copies ran while one was open for 24% of the time, Pallas kernels for 0%

profile of v2, /device:TPU:6, one launch (start us, length us, event | category | flops | bytes accessed | tf_op | source)
XLA Modules:
  0.0 226.8 jit_solution(4523407411034527686)
XLA Ops:
  8.0 0.0 all-reduce.2.cloned.1.call-start
  8.0 0.7 all-reduce.2.cloned.1.call-update
  8.7 0.0 all-gather.3.cloned.1.call-start
  8.8 0.5 all-gather.3.cloned.1.call-update
  9.3 0.0 all-gather.5.cloned.1.call-start
  9.4 42.2 %all-reduce.2.cloned.1.call-done = bf16[256,1024]{1,0:T(8,128)(2,1)} async-done(((bf16[256,1024]{1,0:T(8,128)(2,1)}), bf16[256,1024]{1,0:T(8,128)(2,1)}) %all-reduce.2.cloned.1.call-update) | async-done | bytes 524304 | tf_op jit(solution)/shard_map/psum | solution.py:35
  51.6 3.0 %subtract_convert_fusion.1 = (bf16[256,1024]{1,0:T(8,128)(2,1)}, f32[256,1024]{1,0:T(8,128)}) fusion(bf16[256,1024]{1,0:T(8,128)(2,1)} %all-reduce.2.cloned.1.call-done, bf16[256,1024]{1,0:T(8,128)(2,1)} %param.7, f32[256,1024]{1,0:T(8,128)} %param.9), kind=kLoop, calls=%fused_computation.8 | loop fusion | flops 2621440 | bytes 3670016 | tf_op jit(solution)/shard_map/convert_element_type | solution.py:40
  54.6 0.0 all-gather.5.cloned.1.call-update
  54.6 0.0 reduce-scatter.2.cloned.1.call-start
  54.7 7.8 %reshape.30 = bf16[256,8,4,256]{3,2,1,0:T(4,128)(2,1)} reshape(bf16[256,8192]{1,0:T(8,128)(2,1)} %param.12) | data formatting | bytes 8388608 | tf_op jit(solution)/shard_map/reshape | solution.py:32
  62.5 2.7 %copy.18 = bf16[256,8,4,256]{3,1,0,2:T(8,128)(2,1)S(1)} copy(bf16[256,8,4,256]{3,2,1,0:T(4,128)(2,1)} %reshape.30) | data formatting | bytes 8388608 | tf_op jit(solution)/shard_map/reshape | solution.py:32
  65.2 53.6 %all_to_all.30 = bf16[256,8,4,256]{3,1,0,2:T(8,128)(2,1)S(1)} all-to-all(bf16[256,8,4,256]{3,1,0,2:T(8,128)(2,1)S(1)} %copy.18), channel_id=1, replica_groups=mesh['y_lo'=2,'core'=2,'y_hi'=2,'x'=4,'z'=4] {'z'}, dimensions={2} | all-to-all | bytes 8388608 | tf_op jit(solution)/shard_map/all_to_all | solution.py:31
  118.8 3.5 %copy.22 = bf16[128,8,8,256]{3,1,2,0:T(8,128)(2,1)} copy(bf16[128,8,8,256]{3,2,1,0:T(8,128)(2,1)S(1)} %bitcast.43) | data formatting | bytes 8388608
  122.3 0.0 all-gather.3.cloned.1.call-done
  122.3 9.4 %multiply_convert_fusion.1 = bf16[2048,1024]{1,0:T(8,128)(2,1)} fusion(bf16[1024,2048]{1,0:T(8,128)(2,1)} %bitcast.45, bf16[1024,1024]{1,0:T(8,128)(2,1)} %all-gather.3.cloned.1.call-done), kind=kOutput, calls=%fused_computation.1 | convolution fusion | flops 4299161600 | bytes 10485760 | tf_op jit(solution)/shard_map/td,tk->dk/dot_general | solution.py:51
  131.7 0.0 copy-start.3
  131.7 0.0 reduce-scatter.2.cloned.1.call-update
  131.7 0.0 all-gather.5.cloned.1.call-done
  131.7 1.5 copy-done.3
  133.3 8.3 %fusion = bf16[1024,2048]{0,1:T(8,128)(2,1)} fusion(bf16[2048,1024]{1,0:T(8,128)(2,1)} %all-gather.5.cloned.1.call-done, bf16[1024,1024]{1,0:T(8,128)(2,1)S(1)} %copy-done.3), kind=kOutput, calls=%fused_computation.2 | convolution fusion | flops 4299161600 | bytes 10485760 | tf_op jit(solution)/shard_map/tk,dk->td/dot_general | solution.py:44
  141.6 7.9 %reshape.32 = bf16[4,256,8,1,256]{1,0,4,2,3:T(4,128)(2,1)} reshape(bf16[1024,2048]{0,1:T(8,128)(2,1)} %fusion) | data formatting | bytes 8388608 | tf_op jit(solution)/shard_map/reshape | solution.py:47
  149.5 3.0 %copy.19 = bf16[4,256,8,1,256]{1,4,2,3,0:T(8,128)(2,1)S(1)} copy(bf16[4,256,8,1,256]{1,0,4,2,3:T(4,128)(2,1)} %reshape.32) | data formatting | bytes 8388608 | tf_op jit(solution)/shard_map/reshape | solution.py:47
  152.5 51.0 %all_to_all.31 = bf16[4,256,8,1,256]{1,4,2,3,0:T(8,128)(2,1)S(1)} all-to-all(bf16[4,256,8,1,256]{1,4,2,3,0:T(8,128)(2,1)S(1)} %copy.19), channel_id=1, replica_groups=mesh['y_lo'=2,'core'=2,'y_hi'=2,'x'=4,'z'=4] {'z'}, dimensions={0} | all-to-all | bytes 8388608 | tf_op jit(solution)/shard_map/all_to_all | solution.py:46
  203.5 2.2 copy.20
  205.7 0.0 copy-start
  205.7 0.0 copy-start.1
  205.7 6.5 %copy.21 = bf16[256,8192]{1,0:T(8,128)(2,1)} copy(bf16[256,8192]{0,1:T(8,128)(2,1)} %bitcast.44) | data formatting | bytes 8388608
  212.3 3.5 %reduce-scatter.2.cloned.1.call-done = bf16[256,1024]{1,0:T(8,128)(2,1)} async-done(((bf16[2048,1024]{1,0:T(8,128)(2,1)}), bf16[256,1024]{1,0:T(8,128)(2,1)}) %reduce-scatter.2.cloned.1.call-update) | async-done | bytes 524304 | tf_op jit(solution)/shard_map/reduce_scatter | solution.py:53
  215.8 0.0 copy-done
  215.8 0.0 copy-done.1
  215.8 0.0 copy-done.2
  215.8 3.4 %fusion.4 = (f32[1,256,1024]{2,1,0:T(8,128)}, bf16[1,256,1024]{2,1,0:T(8,128)(2,1)}, f32[1,256,1024]{2,1,0:T(8,128)}) fusion(bf16[256,1024]{1,0:T(8,128)(2,1)} %reduce-scatter.2.cloned.1.call-done, f32[1,256,1024]{2,1,0:T(8,128)S(1)} %copy-done.1, f32[1,256,1024]{2,1,0:T(8,128)S(1)} %copy-done.2, bf16[256,1024]{1,0:T(8,128)(2,1)S(1)} %copy-done), kind=kLoop, calls=%fused_computation.12 | loop fusion | flops 4456448 | bytes 5767168 | tf_op jit(solution)/shard_map/broadcast_in_dim | solution.py:68
  (1 shorter events, 0.0 us)
Async XLA Ops:
  8.0 43.6 %all-reduce.2.cloned.1.call-start = ((), (), s32[]{:S(2)}) async-start(), calls=%async_computation.3 | async-start | bytes 1048576 | tf_op jit(solution)/shard_map/psum | solution.py:35
  8.7 113.5 %all-gather.3.cloned.1.call-start = ((), (), s32[]{:S(2)}) async-start(), calls=%async_computation.4 | async-start | bytes 2621440 | tf_op jit(solution)/shard_map/all_gather | solution.py:30
  9.3 122.4 %all-gather.5.cloned.1.call-start = ((), (), s32[]{:S(2)}) async-start(), calls=%async_computation.6 | async-start | bytes 4718592 | tf_op jit(solution)/shard_map/all_gather | solution.py:43
  54.6 161.2 %reduce-scatter.2.cloned.1.call-start = ((), (), s32[]{:S(2)}) async-start(), calls=%async_computation.5 | async-start | bytes 4718592 | tf_op jit(solution)/shard_map/reduce_scatter | solution.py:53
  131.7 1.6 copy-start.3
  205.7 10.1 %copy-start = (bf16[256,1024]{1,0:T(8,128)(2,1)S(1)}, bf16[256,1024]{1,0:T(8,128)(2,1)}, u32[]{:S(2)}) copy-start(bf16[256,1024]{1,0:T(8,128)(2,1)} %get-tuple-element.12) | copy-start | bytes 1572868
  205.7 10.1 %copy-start.1 = (f32[1,256,1024]{2,1,0:T(8,128)S(1)}, f32[1,256,1024]{2,1,0:T(8,128)}, u32[]{:S(2)}) copy-start(f32[1,256,1024]{2,1,0:T(8,128)} %param.11) | copy-start | bytes 3145732
  205.7 10.1 %copy-start.2 = (f32[1,256,1024]{2,1,0:T(8,128)S(1)}, f32[1,256,1024]{2,1,0:T(8,128)}, u32[]{:S(2)}) copy-start(f32[1,256,1024]{2,1,0:T(8,128)} %param.10) | copy-start | bytes 3145732
Sparse Core Ops, SparseCore 0:
  11.3 40.2 all-reduce.1
Sparse Core Ops, SparseCore 1:
  10.9 33.1 all-gather.2
  54.7 70.8 all-gather.4
  131.8 84.0 reduce-scatter.1

commit v3 on v2

--- a/solution.py
+++ b/solution.py
@@ -32,7 +32,11 @@
         inputs.reshape(tok, teams, team, rows), TEAM, split_axis=2, concat_axis=0, tiled=True
     ).reshape(team * tok, teams * rows)
 
-    total = lax.psum(pseudo_grads[0], GROUP).astype(jnp.float32)
+    own = pseudo_grads[0]
+    pair = own.astype(jnp.float32) + lax.ppermute(own, "y_lo", perm=[(0, 1), (1, 0)]).astype(
+        jnp.float32
+    )
+    total = pair + lax.ppermute(pair, "core", perm=[(0, 1), (1, 0)])
     mean_delta = total / workers
     new_moment = MOMENTUM * outer_moment + mean_delta
     new_anchor = (
@@ -40,8 +44,17 @@
     ).astype(jnp.bfloat16)
     new_anchor = lax.optimization_barrier(new_anchor)
 
-    anchor_part = lax.all_gather(new_anchor, TEAMS, axis=0, tiled=True)
-    product = jnp.einsum("tk,dk->td", cot_team, anchor_part, preferred_element_type=jnp.float32)
+    half = kv // 2
+    core = lax.axis_index("core")
+    mine = lax.all_gather(
+        lax.dynamic_slice_in_dim(new_anchor, core * half, half, axis=1), TEAMS, axis=0, tiled=True
+    )
+    other = lax.ppermute(mine, "core", perm=[(0, 1), (1, 0)])
+    cot_mine = lax.dynamic_slice_in_dim(cot_team, core * half, half, axis=1)
+    cot_other = lax.dynamic_slice_in_dim(cot_team, (1 - core) * half, half, axis=1)
+    product = jnp.einsum(
+        "tk,dk->td", cot_mine, mine, preferred_element_type=jnp.float32
+    ) + jnp.einsum("tk,dk->td", cot_other, other, preferred_element_type=jnp.float32)
     input_part = (product * scale).astype(jnp.bfloat16)
     input_grad = lax.all_to_all(
         input_part.reshape(team, tok, teams, 1, rows), TEAM, split_axis=0, concat_axis=3, tiled=True

time: 228 us -> 203 us (0.89)
  blocking collectives: 105 us -> 52.3 us
  waiting for transfers between devices: 47 us -> 66.7 us
  starting transfers between devices: 0.17 us -> 7.44 us
    all_to_all x1 -> x0, blocking collectives: 53.6 us -> none  [per_device(): lax.all_to_all(inputs.reshape(tok, teams, team, rows), TEAM, split_axis=2...]
    all_to_all x0 -> x1, waiting for transfers between devices: none -> 46.6 us  [per_device(): lax.all_to_all(inputs.reshape(tok, teams, team, rows), TEAM, split_axis=2...]
    psum x1 -> x0, waiting for transfers between devices: 42.2 us -> none  [per_device(): total = lax.psum(pseudo_grads[0], GROUP).astype(jnp.float32)]
    ppermute x0 -> x3, waiting for transfers between devices: none -> 12.3 us  [the longest x1 12.3 us: per_device(): lax.ppermute(own, 'y_lo', perm=[(0, 1), (1, 0)]).astype(jnp.float32)]
    reshape x2 -> x0, local copies, waits for them, and re-layouts: 10.9 us -> none  [per_device(): input_part.reshape(team, tok, teams, 1, rows)]
    all_to_all x0 -> x1, starting transfers between devices: none -> 5.43 us  [per_device(): lax.all_to_all(inputs.reshape(tok, teams, team, rows), TEAM, split_axis=2...]
    all_to_all x1, local copies, waits for them, and re-layouts: 2.24 us -> 7.53 us  [per_device(): lax.all_to_all(input_part.reshape(team, tok, teams, 1, rows), TEAM, split...]
    reduce_scatter x1, waiting for transfers between devices: 3.55 us -> 7.06 us  [per_device(): lax.psum_scatter(partial, TEAMS, scatter_dimension=0, tiled=True)]
  transfers between devices with their start and end apart: 4 -> 7, of which waited for: 2 -> 3; matrix products, arithmetic and copies ran while one was open for 24% -> 28% of each run, Pallas kernels for 0% -> 0%
where the time goes in v3:
time: 203 us; the launch traced here: 202 us
  waiting for transfers between devices  66.7 us (33%)
  blocking collectives  52.3 us (26%)
  local copies, waits for them, and re-layouts  35.8 us (18%)
  matrix products  17.4 us (9%)
  between operations  13.8 us (7%)
  other arithmetic  8.23 us (4%)
  starting transfers between devices  7.44 us (4%)
    all_to_all x1, blocking collectives, per_device(): lax.all_to_all(input_part.reshape(team, tok, teams, 1, rows), TEAM, split...  52.3 us
    all_to_all x1, waiting for transfers between devices, per_device(): lax.all_to_all(inputs.reshape(tok, teams, team, rows), TEAM, split_axis=2...  46.6 us
    unnamed x17, local copies, waits for them, and re-layouts  14.9 us
    reshape x2, local copies, waits for them, and re-layouts, per_device(): inputs.reshape(tok, teams, team, rows)  12.6 us
    ppermute x1, waiting for transfers between devices, per_device(): lax.ppermute(own, 'y_lo', perm=[(0, 1), (1, 0)]).astype(jnp.float32)  12.3 us
    dot_general x1, matrix products, per_device(): jnp.einsum('td,tk->dk', inputs_part, cot_team, preferred_element_type=jnp...  9.42 us
    all_to_all x1, local copies, waits for them, and re-layouts, per_device(): lax.all_to_all(input_part.reshape(team, tok, teams, 1, rows), TEAM, split...  7.53 us
    reduce_scatter x1, waiting for transfers between devices, per_device(): lax.psum_scatter(partial, TEAMS, scatter_dimension=0, tiled=True)  7.06 us
  transfers between devices with their start and end apart: 7, of which 3 were waited for; matrix products, arithmetic and copies ran while one was open for 28% of the time, Pallas kernels for 0%

profile of v3, /device:TPU:6, one launch (start us, length us, event | category | flops | bytes accessed | tf_op | source)
XLA Modules:
  0.0 201.8 jit_solution(9180297639101641675)
XLA Ops:
  7.2 0.0 all-gather.3.cloned.1.call-start
  7.2 0.7 all-gather.3.cloned.1.call-update
  7.9 1.7 collective-permute-start
  9.6 12.3 %collective-permute-done = bf16[256,1024]{1,0:T(8,128)(2,1)S(1)} collective-permute-done((bf16[256,1024]{1,0:T(8,128)(2,1)}, bf16[256,1024]{1,0:T(8,128)(2,1)S(1)}, u32[]{:S(2)}, u32[]{:S(2)}) %collective-permute-start) | collective-permute-done | bytes 524320 | tf_op jit(solution)/shard_map/ppermute | solution.py:36
  21.9 2.2 %convert_add_fusion = f32[256,1024]{1,0:T(8,128)} fusion(bf16[256,1024]{1,0:T(8,128)(2,1)S(1)} %collective-permute-done, bf16[1,256,1024]{2,1,0:T(8,128)(2,1)} %param.8), kind=kLoop, calls=%fused_computation.13 | loop fusion | flops 786432 | bytes 2097152 | tf_op jit(solution)/shard_map/add | solution.py:36
  24.1 0.0 collective-permute-start.1
  24.1 7.8 %reshape.30 = bf16[256,8,4,256]{3,2,1,0:T(4,128)(2,1)} reshape(bf16[256,8192]{1,0:T(8,128)(2,1)} %param.12) | data formatting | bytes 8388608 | tf_op jit(solution)/shard_map/reshape | solution.py:32
  31.9 4.8 %copy.18 = bf16[256,8,4,256]{3,1,0,2:T(8,128)(2,1)} copy(bf16[256,8,4,256]{3,2,1,0:T(4,128)(2,1)} %reshape.30) | data formatting | bytes 8388608 | tf_op jit(solution)/shard_map/reshape | solution.py:32
  36.7 5.4 %all-to-all-start = ((bf16[256,8,4,256]{3,1,0,2:T(8,128)(2,1)}), bf16[256,8,4,256]{3,1,0,2:T(8,128)(2,1)}, u32[]{:S(2)}, u32[]{:S(2)}) async-start(bf16[256,8,4,256]{3,1,0,2:T(8,128)(2,1)} %copy.18), calls=%async_computation | async-start | bytes 8388608 | tf_op jit(solution)/shard_map/all_to_all | solution.py:31
  42.1 0.0 all-gather.5.cloned.1.call-start
  42.1 0.0 collective-permute-done.1
  42.1 2.7 %subtract_convert_fusion.1 = (bf16[256,1024]{1,0:T(8,128)(2,1)S(1)}, f32[256,1024]{1,0:T(8,128)}) fusion(bf16[256,1024]{1,0:T(8,128)(2,1)S(1)} %copy-done.5, f32[256,1024]{1,0:T(8,128)} %collective-permute-done.1, bf16[256,1024]{1,0:T(8,128)(2,1)S(1)} %collective-permute-done, bf16[1,256,1024]{2,1,0:T(8,128)(2,1)S(1)} %copy-done.1, f32[256,1024]{1,0:T(8,128)S(1)} %copy-done.2), kind=kLoop, calls=%fused_computation.10 | loop fusion | flops 3407872 | bytes 5242880 | tf_op jit(solution)/shard_map/convert_element_type | solution.py:44
  44.8 0.8 constant_dynamic-slice_fusion
  45.6 0.0 all-gather.5.cloned.1.call-update
  45.6 0.0 reduce-scatter.2.cloned.1.call-start
  45.6 46.6 %all-to-all-done = bf16[256,8,4,256]{3,1,0,2:T(8,128)(2,1)} async-done(((bf16[256,8,4,256]{3,1,0,2:T(8,128)(2,1)}), bf16[256,8,4,256]{3,1,0,2:T(8,128)(2,1)}, u32[]{:S(2)}, u32[]{:S(2)}) %all-to-all-start) | async-done | bytes 4194336 | tf_op jit(solution)/shard_map/all_to_all | solution.py:31
  92.3 5.7 %copy.22 = bf16[128,8,8,256]{3,1,2,0:T(8,128)(2,1)} copy(bf16[128,8,8,256]{3,2,1,0:T(8,128)(2,1)} %bitcast.17) | data formatting | bytes 8388608
  98.0 9.4 %multiply_convert_fusion.1 = bf16[2048,1024]{1,0:T(8,128)(2,1)} fusion(bf16[1024,2048]{1,0:T(8,128)(2,1)} %bitcast.53, bf16[1024,1024]{1,0:T(8,128)(2,1)} %all-gather.3.cloned.1.call-done), kind=kOutput, calls=%fused_computation.1 | convolution fusion | flops 4299161600 | bytes 10485760 | tf_op jit(solution)/shard_map/td,tk->dk/dot_general | solution.py:64
  107.4 0.0 reduce-scatter.2.cloned.1.call-update
  107.4 0.0 all-gather.5.cloned.1.call-done
  107.4 0.3 collective-permute-start.2
  107.7 1.3 copy-done.6
  109.0 4.0 %fusion.3 = f32[1024,2048]{1,0:T(8,128)S(1)} fusion(bf16[2048,512]{1,0:T(8,128)(2,1)} %all-gather.5.cloned.1.call-done, bf16[1024,1024]{1,0:T(8,128)(2,1)S(1)} %copy-done.6, s32[]{:T(128)S(6)} %select_n.7), kind=kOutput, calls=%fused_computation.7 | convolution fusion | flops 2147483648 | bytes 11534340 | tf_op jit(solution)/shard_map/tk,dk->td/dot_general | solution.py:55
  113.0 0.0 collective-permute-done.2
  113.0 4.0 %multiply_convert_fusion = bf16[1024,2048]{1,0:T(8,128)(2,1)S(1)} fusion(f32[1024,2048]{1,0:T(8,128)S(1)} %fusion.3, bf16[2048,512]{1,0:T(8,128)(2,1)} %collective-permute-done.2, bf16[1024,1024]{1,0:T(8,128)(2,1)S(1)} %copy-done.6, s32[]{:T(128)S(6)} %select_n.8), kind=kOutput, calls=%fused_computation | convolution fusion | flops 2153775104 | bytes 15728644 | tf_op jit(solution)/shard_map/tk,dk->td/dot_general | solution.py:57
  117.0 1.5 copy.23
  118.5 52.3 %all_to_all.30 = bf16[4,256,8,1,256]{4,2,1,3,0:T(8,128)(2,1)} all-to-all(bf16[4,256,8,1,256]{4,2,1,3,0:T(8,128)(2,1)S(1)} %bitcast.51), channel_id=1, replica_groups=mesh['y_lo'=2,'core'=2,'y_hi'=2,'x'=4,'z'=4] {'z'}, dimensions={0} | all-to-all | bytes 8388608 | tf_op jit(solution)/shard_map/all_to_all | solution.py:59
  170.8 7.5 %copy.20 = bf16[4,256,8,1,256]{1,4,0,2,3:T(8,128)(2,1)} copy(bf16[4,256,8,1,256]{4,2,1,3,0:T(8,128)(2,1)} %all_to_all.30) | data formatting | bytes 8388608 | tf_op jit(solution)/shard_map/all_to_all | solution.py:59
  178.3 6.5 %copy.21 = bf16[256,8192]{1,0:T(8,128)(2,1)} copy(bf16[256,8192]{0,1:T(8,128)(2,1)} %bitcast.52) | data formatting | bytes 8388608
  184.8 7.1 %reduce-scatter.2.cloned.1.call-done = bf16[256,1024]{1,0:T(8,128)(2,1)} async-done(((bf16[2048,1024]{1,0:T(8,128)(2,1)}), bf16[256,1024]{1,0:T(8,128)(2,1)}) %reduce-scatter.2.cloned.1.call-update) | async-done | bytes 524304 | tf_op jit(solution)/shard_map/reduce_scatter | solution.py:66
  191.9 0.0 copy-done.3
  191.9 3.4 %fusion.6 = (f32[1,256,1024]{2,1,0:T(8,128)}, bf16[1,256,1024]{2,1,0:T(8,128)(2,1)}, f32[1,256,1024]{2,1,0:T(8,128)}) fusion(bf16[256,1024]{1,0:T(8,128)(2,1)} %reduce-scatter.2.cloned.1.call-done, f32[1,256,1024]{2,1,0:T(8,128)S(1)} %copy-done.3, f32[1,256,1024]{2,1,0:T(8,128)S(1)} %copy-done.4, bf16[256,1024]{1,0:T(8,128)(2,1)S(1)} %get-tuple-element.12), kind=kLoop, calls=%fused_computation.15 | loop fusion | flops 4456448 | bytes 5767168 | tf_op jit(solution)/shard_map/broadcast_in_dim | solution.py:81
  (13 shorter events, 0.0 us)
Async XLA Ops:
  7.2 90.8 %all-gather.3.cloned.1.call-start = ((), (), s32[]{:S(2)}) async-start(), calls=%async_computation.3 | async-start | bytes 2621440 | tf_op jit(solution)/shard_map/all_gather | solution.py:30
  7.9 14.0 %collective-permute-start = (bf16[256,1024]{1,0:T(8,128)(2,1)}, bf16[256,1024]{1,0:T(8,128)(2,1)S(1)}, u32[]{:S(2)}, u32[]{:S(2)}) collective-permute-start(bf16[256,1024]{1,0:T(8,128)(2,1)} %bitcast.55), channel_id=1, source_target_pairs={{0,64},{64,0},{1,65},{65,1},{2,66},{66,2},{3,67},{67,3},{4,68},{68... | collective-permute-start | bytes 1572872 | tf_op jit(solution)/shard_map/ppermute | solution.py:36
  24.1 18.0 %collective-permute-start.1 = (f32[256,1024]{1,0:T(8,128)}, f32[256,1024]{1,0:T(8,128)}, u32[]{:S(2)}, u32[]{:S(2)}) collective-permute-start(f32[256,1024]{1,0:T(8,128)} %convert_add_fusion), channel_id=1, source_target_pairs={{0,32},{32,0},{1,33},{33,1},{2,34},{34,2},{3,35},{35,3},{4,36},{36... | collective-permute-start | bytes 3145736 | tf_op jit(solution)/shard_map/ppermute | solution.py:39
  36.6 5.5 %copy-start.1 = (bf16[1,256,1024]{2,1,0:T(8,128)(2,1)S(1)}, bf16[1,256,1024]{2,1,0:T(8,128)(2,1)}, u32[]{:S(2)}) copy-start(bf16[1,256,1024]{2,1,0:T(8,128)(2,1)} %param.8) | copy-start | bytes 1572868
  36.6 5.5 %copy-start.2 = (f32[256,1024]{1,0:T(8,128)S(1)}, f32[256,1024]{1,0:T(8,128)}, u32[]{:S(2)}) copy-start(f32[256,1024]{1,0:T(8,128)} %param.9) | copy-start | bytes 3145732
  36.7 5.5 %copy-start.5 = (bf16[256,1024]{1,0:T(8,128)(2,1)S(1)}, bf16[256,1024]{1,0:T(8,128)(2,1)}, u32[]{:S(2)}) copy-start(bf16[256,1024]{1,0:T(8,128)(2,1)} %param.7) | copy-start | bytes 1572868
  36.7 55.6 %all-to-all-start = ((bf16[256,8,4,256]{3,1,0,2:T(8,128)(2,1)}), bf16[256,8,4,256]{3,1,0,2:T(8,128)(2,1)}, u32[]{:S(2)}, u32[]{:S(2)}) async-start(bf16[256,8,4,256]{3,1,0,2:T(8,128)(2,1)} %copy.18), calls=%async_computation | async-start | bytes 8388608 | tf_op jit(solution)/shard_map/all_to_all | solution.py:31
  42.1 65.4 %all-gather.5.cloned.1.call-start = ((), (), s32[]{:S(2)}) async-start(), calls=%async_computation.5 | async-start | bytes 2359296 | tf_op jit(solution)/shard_map/all_gather | solution.py:49
  44.8 147.1 %copy-start = (bf16[256,1024]{1,0:T(8,128)(2,1)}, bf16[256,1024]{1,0:T(8,128)(2,1)S(1)}, u32[]{:S(2)}) copy-start(bf16[256,1024]{1,0:T(8,128)(2,1)S(1)} %get-tuple-element.12) | copy-start | bytes 1572868
  45.6 146.3 %reduce-scatter.2.cloned.1.call-start = ((), (), s32[]{:S(2)}) async-start(), calls=%async_computation.4 | async-start | bytes 4718592 | tf_op jit(solution)/shard_map/reduce_scatter | solution.py:66
  107.4 1.6 copy-start.6
  107.4 5.5 %collective-permute-start.2 = (bf16[2048,512]{1,0:T(8,128)(2,1)}, bf16[2048,512]{1,0:T(8,128)(2,1)}, u32[]{:S(2)}, u32[]{:S(2)}) collective-permute-start(bf16[2048,512]{1,0:T(8,128)(2,1)} %all-gather.5.cloned.1.call-done), channel_id=1, source_target_pairs={{0,32},{32,0},{1,33},{33,1},{2,34},{34,2},{3,35},{35,3},{4,36},{36... | collective-permute-start | bytes 6291464 | tf_op jit(solution)/shard_map/ppermute | solution.py:52
  178.3 13.6 %copy-start.3 = (f32[1,256,1024]{2,1,0:T(8,128)S(1)}, f32[1,256,1024]{2,1,0:T(8,128)}, u32[]{:S(2)}) copy-start(f32[1,256,1024]{2,1,0:T(8,128)} %param.11) | copy-start | bytes 3145732
  178.3 13.6 %copy-start.4 = (f32[1,256,1024]{2,1,0:T(8,128)S(1)}, f32[1,256,1024]{2,1,0:T(8,128)}, u32[]{:S(2)}) copy-start(f32[1,256,1024]{2,1,0:T(8,128)} %param.10) | copy-start | bytes 3145732
Sparse Core Ops, SparseCore 0:
  9.6 33.2 all-gather.2
  45.9 56.7 all-gather.4
  107.5 84.3 reduce-scatter.1

commit v4 on v3

--- a/solution.py
+++ b/solution.py
@@ -27,10 +27,14 @@
     teams = lax.axis_size(TEAMS)
     team = lax.axis_size(TEAM)
 
-    cot_team = lax.all_gather(key_cotangent, TEAM, axis=0, tiled=True)
-    inputs_part = lax.all_to_all(
-        inputs.reshape(tok, teams, team, rows), TEAM, split_axis=2, concat_axis=0, tiled=True
-    ).reshape(team * tok, teams * rows)
+    chunks = kv // rows
+    cols = inputs.reshape(tok, teams, team, rows).transpose(2, 1, 0, 3)
+    cot_chunks = key_cotangent.reshape(tok, chunks, rows).transpose(1, 0, 2)
+    cot_chunks = jnp.broadcast_to(cot_chunks[None], (team,) + cot_chunks.shape)
+    sent = jnp.concatenate([cols, cot_chunks], axis=1)
+    got = lax.all_to_all(sent, TEAM, split_axis=0, concat_axis=0, tiled=True)
+    inputs_part = got[:, :teams]
+    cot_team = got[:, teams:].transpose(0, 2, 1, 3).reshape(team * tok, kv)
 
     own = pseudo_grads[0]
     pair = own.astype(jnp.float32) + lax.ppermute(own, "y_lo", perm=[(0, 1), (1, 0)]).astype(
@@ -55,14 +59,23 @@
     product = jnp.einsum(
         "tk,dk->td", cot_mine, mine, preferred_element_type=jnp.float32
     ) + jnp.einsum("tk,dk->td", cot_other, other, preferred_element_type=jnp.float32)
-    input_part = (product * scale).astype(jnp.bfloat16)
-    input_grad = lax.all_to_all(
-        input_part.reshape(team, tok, teams, 1, rows), TEAM, split_axis=0, concat_axis=3, tiled=True
-    ).reshape(tok, width)
+    input_part = (product * scale).astype(jnp.bfloat16).reshape(team, tok, teams * rows)
+    input_grad = (
+        lax.all_to_all(input_part, TEAM, split_axis=0, concat_axis=0, tiled=True)
+        .reshape(team, tok, teams, rows)
+        .transpose(1, 2, 0, 3)
+        .reshape(tok, width)
+    )
 
     partial = (
-        jnp.einsum("td,tk->dk", inputs_part, cot_team, preferred_element_type=jnp.float32) * scale
-    ).astype(jnp.bfloat16)
+        jnp.einsum(
+            "satr,stk->ark",
+            inputs_part,
+            cot_team.reshape(team, tok, kv),
+            preferred_element_type=jnp.float32,
+        )
+        * scale
+    ).astype(jnp.bfloat16).reshape(teams * rows, kv)
     grads = lax.psum_scatter(partial, TEAMS, scatter_dimension=0, tiled=True).astype(jnp.float32)
 
     correct_one = 1.0 - BETA_ONE**ADAM_STEP

time: 203 us -> 205 us (level)
  waiting for transfers between devices: 66.7 us -> 70.5 us
  matrix products: 17.4 us -> 14.8 us
    all_to_all x1 -> x0, local copies, waits for them, and re-layouts: 7.53 us -> none  [per_device(): lax.all_to_all(input_part.reshape(team, tok, teams, 1, rows), TEAM, split...]
    all_to_all x1, waiting for transfers between devices: 46.6 us -> 51.9 us  [per_device(): got = lax.all_to_all(sent, TEAM, split_axis=0, concat_axis=0, tiled=True)]
    unnamed x17 -> x15, local copies, waits for them, and re-layouts: 14.9 us -> 10.1 us
    transpose x0 -> x2, local copies, waits for them, and re-layouts: none -> 4.45 us  [per_device(): cot_team = got[:, teams:].transpose(0, 2, 1, 3).reshape(team * tok, kv)]
    reshape x2 -> x3, local copies, waits for them, and re-layouts: 12.6 us -> 16.5 us  [the longest x2 15.3 us: per_device(): input_grad = lax.all_to_all(input_part, TEAM, split_axis=0, concat_axis=0...]
    reduce_scatter x1, waiting for transfers between devices: 7.06 us -> 3.67 us  [per_device(): lax.psum_scatter(partial, TEAMS, scatter_dimension=0, tiled=True)]
    concatenate x0 -> x1, local copies, waits for them, and re-layouts: none -> 3.34 us  [per_device(): sent = jnp.concatenate([cols, cot_chunks], axis=1)]
    ppermute x1, waiting for transfers between devices: 0.01 us -> 2.77 us  [per_device(): total = pair + lax.ppermute(pair, 'core', perm=[(0, 1), (1, 0)])]
  transfers between devices with their start and end apart: 7 -> 6, of which waited for: 3 -> 4; matrix products, arithmetic and copies ran while one was open for 28% -> 21% of each run, Pallas kernels for 0% -> 0%
where the time goes in v4:
time: 205 us; the launch traced here: 204 us
  waiting for transfers between devices  70.5 us (34%)
  blocking collectives  52.5 us (26%)
  local copies, waits for them, and re-layouts  35.4 us (17%)
  matrix products  14.8 us (7%)
  between operations  14.2 us (7%)
  other arithmetic  9.1 us (4%)
  starting transfers between devices  7.31 us (4%)
    all_to_all x1, blocking collectives, per_device(): lax.all_to_all(input_part, TEAM, split_axis=0, concat_axis=0, tiled=True)  52.5 us
    all_to_all x1, waiting for transfers between devices, per_device(): got = lax.all_to_all(sent, TEAM, split_axis=0, concat_axis=0, tiled=True)  51.9 us
    reshape x2, local copies, waits for them, and re-layouts, per_device(): input_grad = lax.all_to_all(input_part, TEAM, split_axis=0, concat_axis=0...  15.3 us
    ppermute x1, waiting for transfers between devices, per_device(): lax.ppermute(own, 'y_lo', perm=[(0, 1), (1, 0)]).astype(jnp.float32)  12.1 us
    unnamed x15, local copies, waits for them, and re-layouts  10.1 us
    dot_general x1, matrix products, per_device(): jnp.einsum('satr,stk->ark', inputs_part, cot_team.reshape(team, tok, kv),...  8.4 us
    all_to_all x1, starting transfers between devices, per_device(): got = lax.all_to_all(sent, TEAM, split_axis=0, concat_axis=0, tiled=True)  5.44 us
    transpose x2, local copies, waits for them, and re-layouts, per_device(): cot_team = got[:, teams:].transpose(0, 2, 1, 3).reshape(team * tok, kv)  4.45 us
  transfers between devices with their start and end apart: 6, of which 4 were waited for; matrix products, arithmetic and copies ran while one was open for 21% of the time, Pallas kernels for 0%

profile of v4, /device:TPU:6, one launch (start us, length us, event | category | flops | bytes accessed | tf_op | source)
XLA Modules:
  0.0 203.8 jit_solution(4895531283479782979)
XLA Ops:
  7.2 1.2 copy.35
  8.4 6.4 %copy.27 = bf16[256,8192]{0,1:T(8,128)(2,1)} copy(bf16[256,8192]{1,0:T(8,128)(2,1)} %param.12) | data formatting | bytes 8388608 | tf_op args[5]
  14.8 0.2 broadcast_in_dim.15
  15.0 2.7 %pad_maximum_fusion = bf16[4,12,256,256]{2,3,0,1:T(8,128)(2,1)S(1)} fusion(bf16[4,4,256,256]{2,3,0,1:T(8,128)(2,1)S(1)} %broadcast_in_dim.15, bf16[4,8,256,256]{2,3,0,1:T(8,128)(2,1)} %bitcast.67), kind=kLoop, calls=%fused_computation.3 | loop fusion | flops 3145728 | bytes 12582912 | tf_op jit(solution)/shard_map/concatenate | solution.py:34
  17.7 3.3 %copy.29 = bf16[4,12,256,256]{2,3,1,0:T(8,128)(2,1)} copy(bf16[4,12,256,256]{2,3,0,1:T(8,128)(2,1)S(1)} %pad_maximum_fusion) | data formatting | bytes 12582912 | tf_op jit(solution)/shard_map/concatenate | solution.py:34
  21.1 5.4 %all-to-all-start = ((bf16[4,12,256,256]{2,3,1,0:T(8,128)(2,1)}), bf16[4,12,256,256]{2,3,1,0:T(8,128)(2,1)}, u32[]{:S(2)}, u32[]{:S(2)}) async-start(bf16[4,12,256,256]{2,3,1,0:T(8,128)(2,1)} %copy.29), calls=%async_computation | async-start | bytes 12582912 | tf_op jit(solution)/shard_map/all_to_all | solution.py:35
  26.5 1.7 collective-permute-start
  28.2 12.1 %collective-permute-done = bf16[256,1024]{1,0:T(8,128)(2,1)S(1)} collective-permute-done((bf16[256,1024]{1,0:T(8,128)(2,1)S(1)}, bf16[256,1024]{1,0:T(8,128)(2,1)S(1)}, u32[]{:S(2)}, u32[]{:S(2)}) %collective-permute-start) | collective-permute-done | bytes 524320 | tf_op jit(solution)/shard_map/ppermute | solution.py:40
  40.3 0.2 convert_add_fusion
  40.4 0.1 collective-permute-start.1
  40.5 2.8 %collective-permute-done.1 = f32[256,1024]{1,0:T(8,128)} collective-permute-done((f32[256,1024]{1,0:T(8,128)S(1)}, f32[256,1024]{1,0:T(8,128)}, u32[]{:S(2)}, u32[]{:S(2)}) %collective-permute-start.1) | collective-permute-done | bytes 1048608 | tf_op jit(solution)/shard_map/ppermute | solution.py:43
  43.3 2.8 %subtract_convert_fusion.1 = (bf16[256,1024]{1,0:T(8,128)(2,1)S(1)}, f32[256,1024]{1,0:T(8,128)}) fusion(bf16[256,1024]{1,0:T(8,128)(2,1)} %param.7, f32[256,1024]{1,0:T(8,128)} %collective-permute-done.1, bf16[256,1024]{1,0:T(8,128)(2,1)S(1)} %collective-permute-done, bf16[1,256,1024]{2,1,0:T(8,128)(2,1)S(1)} %copy-done.1, f32[256,1024]{1,0:T(8,128)S(1)} %copy-done.2), kind=kLoop, calls=%fused_computation.13 | loop fusion | flops 3407872 | bytes 5242880 | tf_op jit(solution)/shard_map/convert_element_type | solution.py:48
  46.2 0.8 constant_dynamic-slice_fusion
  46.9 0.0 all-gather.2.cloned.1.call-update
  46.9 0.0 reduce-scatter.2.cloned.1.call-start
  47.0 51.9 %all-to-all-done = bf16[4,12,256,256]{2,3,1,0:T(8,128)(2,1)} async-done(((bf16[4,12,256,256]{2,3,1,0:T(8,128)(2,1)}), bf16[4,12,256,256]{2,3,1,0:T(8,128)(2,1)}, u32[]{:S(2)}, u32[]{:S(2)}) %all-to-all-start) | async-done | bytes 6291488 | tf_op jit(solution)/shard_map/all_to_all | solution.py:35
  98.9 1.9 slice_bitcast_fusion
  100.8 8.4 %fusion = bf16[8,256,1024]{2,1,0:T(8,128)(2,1)} fusion(bf16[4,12,256,256]{2,3,1,0:T(8,128)(2,1)} %all-to-all-done, bf16[4,256,1024,1]{1,2,3,0:T(8,128)(2,1)S(1)} %bitcast.74), kind=kOutput, calls=%fused_computation.1 | convolution fusion | flops 4299161600 | bytes 12582912 | tf_op jit(solution)/shard_map/satr,stk->ark/dot_general | solution.py:71
  109.2 0.0 reduce-scatter.2.cloned.1.call-update
  109.3 0.0 all-gather.2.cloned.1.call-done
  109.3 0.1 collective-permute-start.2
  109.4 2.5 %copy.32 = bf16[4,256,4,256]{3,2,1,0:T(4,128)(2,1)} copy(bf16[4,256,4,256]{1,3,2,0:T(8,128)(2,1)S(1)} %get-tuple-element.8) | data formatting | bytes 4194304 | tf_op jit(solution)/shard_map/transpose | solution.py:37
  111.9 2.2 %copy.38 = bf16[128,8,4,256]{3,1,2,0:T(8,128)(2,1)S(1)} copy(bf16[128,8,4,256]{3,2,1,0:T(4,128)(2,1)} %bitcast.71) | data formatting | bytes 4194304
  114.2 2.4 %fusion.4 = f32[1024,2048]{1,0:T(8,128)S(1)} fusion(bf16[2048,512]{1,0:T(8,128)(2,1)S(1)} %copy-done.5, bf16[1024,1024]{1,0:T(8,128)(2,1)S(1)} %bitcast.76, s32[]{:T(128)S(6)} %select_n.7), kind=kOutput, calls=%fused_computation.10 | convolution fusion | flops 2147483648 | bytes 11534340 | tf_op jit(solution)/shard_map/tk,dk->td/dot_general | solution.py:59
  116.5 0.0 collective-permute-done.2
  116.5 4.1 %multiply_convert_fusion = bf16[1024,2048]{1,0:T(8,128)(2,1)S(1)} fusion(f32[1024,2048]{1,0:T(8,128)S(1)} %fusion.4, bf16[2048,512]{1,0:T(8,128)(2,1)} %collective-permute-done.2, bf16[1024,1024]{1,0:T(8,128)(2,1)S(1)} %bitcast.77, s32[]{:T(128)S(6)} %select_n.8), kind=kOutput, calls=%fused_computation.2 | convolution fusion | flops 2153775104 | bytes 15728644 | tf_op jit(solution)/shard_map/tk,dk->td/dot_general | solution.py:61
  120.6 52.5 %all_to_all.10 = bf16[4,256,2048]{2,1,0:T(8,128)(2,1)S(1)} all-to-all(bf16[4,256,2048]{2,1,0:T(8,128)(2,1)S(1)} %bitcast.73), channel_id=1, replica_groups=mesh['y_lo'=2,'core'=2,'y_hi'=2,'x'=4,'z'=4] {'z'}, dimensions={0} | all-to-all | bytes 8388608 | tf_op jit(solution)/shard_map/all_to_all | solution.py:64
  173.1 1.5 copy.39
  174.6 7.4 %copy.41 = bf16[4,256,8,256]{3,0,2,1:T(4,128)(2,1)} copy(bf16[4,256,8,256]{3,2,1,0:T(8,128)(2,1)S(1)} %bitcast.69) | data formatting | bytes 8388608 | tf_op jit(solution)/shard_map/reshape | solution.py:65
  182.0 7.9 %reshape.44 = bf16[256,8192]{1,0:T(8,128)(2,1)} reshape(bf16[256,8,4,256]{3,2,1,0:T(4,128)(2,1)} %bitcast.70) | data formatting | bytes 8388608 | tf_op jit(solution)/shard_map/reshape | solution.py:67
  189.9 3.7 %reduce-scatter.2.cloned.1.call-done = bf16[256,1024]{1,0:T(8,128)(2,1)} async-done(((bf16[2048,1024]{1,0:T(8,128)(2,1)}), bf16[256,1024]{1,0:T(8,128)(2,1)}) %reduce-scatter.2.cloned.1.call-update) | async-done | bytes 524304 | tf_op jit(solution)/shard_map/reduce_scatter | solution.py:79
  193.6 3.4 %fusion.7 = (f32[1,256,1024]{2,1,0:T(8,128)}, bf16[1,256,1024]{2,1,0:T(8,128)(2,1)}, f32[1,256,1024]{2,1,0:T(8,128)}) fusion(bf16[256,1024]{1,0:T(8,128)(2,1)} %reduce-scatter.2.cloned.1.call-done, f32[1,256,1024]{2,1,0:T(8,128)S(1)} %copy-done.3, f32[1,256,1024]{2,1,0:T(8,128)S(1)} %copy-done.4, bf16[256,1024]{1,0:T(8,128)(2,1)S(1)} %get-tuple-element.6), kind=kLoop, calls=%fused_computation.18 | loop fusion | flops 4456448 | bytes 5767168 | tf_op jit(solution)/shard_map/broadcast_in_dim | solution.py:94
  (13 shorter events, 0.0 us)
Async XLA Ops:
  21.1 5.5 %copy-start.1 = (bf16[1,256,1024]{2,1,0:T(8,128)(2,1)S(1)}, bf16[1,256,1024]{2,1,0:T(8,128)(2,1)}, u32[]{:S(2)}) copy-start(bf16[1,256,1024]{2,1,0:T(8,128)(2,1)} %param.8) | copy-start | bytes 1572868
  21.1 22.2 %copy-start.2 = (f32[256,1024]{1,0:T(8,128)S(1)}, f32[256,1024]{1,0:T(8,128)}, u32[]{:S(2)}) copy-start(f32[256,1024]{1,0:T(8,128)} %param.9) | copy-start | bytes 3145732
  21.1 77.8 %all-to-all-start = ((bf16[4,12,256,256]{2,3,1,0:T(8,128)(2,1)}), bf16[4,12,256,256]{2,3,1,0:T(8,128)(2,1)}, u32[]{:S(2)}, u32[]{:S(2)}) async-start(bf16[4,12,256,256]{2,3,1,0:T(8,128)(2,1)} %copy.29), calls=%async_computation | async-start | bytes 12582912 | tf_op jit(solution)/shard_map/all_to_all | solution.py:35
  26.5 82.8 %all-gather.2.cloned.1.call-start = ((), (), s32[]{:S(2)}) async-start(), calls=%async_computation.4 | async-start | bytes 2359296 | tf_op jit(solution)/shard_map/all_gather | solution.py:53
  26.5 13.7 %collective-permute-start = (bf16[256,1024]{1,0:T(8,128)(2,1)S(1)}, bf16[256,1024]{1,0:T(8,128)(2,1)S(1)}, u32[]{:S(2)}, u32[]{:S(2)}) collective-permute-start(bf16[256,1024]{1,0:T(8,128)(2,1)S(1)} %bitcast.78), channel_id=1, source_target_pairs={{0,64},{64,0},{1,65},{65,1},{2,66},{66,2},{3,67},{67,3},{4,68},{68... | collective-permute-start | bytes 1572872 | tf_op jit(solution)/shard_map/ppermute | solution.py:40
  40.4 2.9 %collective-permute-start.1 = (f32[256,1024]{1,0:T(8,128)S(1)}, f32[256,1024]{1,0:T(8,128)}, u32[]{:S(2)}, u32[]{:S(2)}) collective-permute-start(f32[256,1024]{1,0:T(8,128)S(1)} %convert_add_fusion), channel_id=1, source_target_pairs={{0,32},{32,0},{1,33},{33,1},{2,34},{34,2},{3,35},{35,3},{4,36},{36... | collective-permute-start | bytes 3145736 | tf_op jit(solution)/shard_map/ppermute | solution.py:43
  46.2 147.5 %copy-start = (bf16[256,1024]{1,0:T(8,128)(2,1)}, bf16[256,1024]{1,0:T(8,128)(2,1)S(1)}, u32[]{:S(2)}) copy-start(bf16[256,1024]{1,0:T(8,128)(2,1)S(1)} %get-tuple-element.6) | copy-start | bytes 1572868
  46.9 146.7 %reduce-scatter.2.cloned.1.call-start = ((), (), s32[]{:S(2)}) async-start(), calls=%async_computation.3 | async-start | bytes 4718592 | tf_op jit(solution)/shard_map/reduce_scatter | solution.py:79
  109.3 7.2 %collective-permute-start.2 = (bf16[2048,512]{1,0:T(8,128)(2,1)}, bf16[2048,512]{1,0:T(8,128)(2,1)}, u32[]{:S(2)}, u32[]{:S(2)}) collective-permute-start(bf16[2048,512]{1,0:T(8,128)(2,1)} %all-gather.2.cloned.1.call-done), channel_id=1, source_target_pairs={{0,32},{32,0},{1,33},{33,1},{2,34},{34,2},{3,35},{35,3},{4,36},{36... | collective-permute-start | bytes 6291464 | tf_op jit(solution)/shard_map/ppermute | solution.py:56
  111.9 2.2 %copy-start.5 = (bf16[2048,512]{1,0:T(8,128)(2,1)S(1)}, bf16[2048,512]{1,0:T(8,128)(2,1)}, u32[]{:S(2)}) copy-start(bf16[2048,512]{1,0:T(8,128)(2,1)} %all-gather.2.cloned.1.call-done) | copy-start | bytes 6291460
  182.0 11.6 %copy-start.3 = (f32[1,256,1024]{2,1,0:T(8,128)S(1)}, f32[1,256,1024]{2,1,0:T(8,128)}, u32[]{:S(2)}) copy-start(f32[1,256,1024]{2,1,0:T(8,128)} %param.11) | copy-start | bytes 3145732
  182.0 11.6 %copy-start.4 = (f32[1,256,1024]{2,1,0:T(8,128)S(1)}, f32[1,256,1024]{2,1,0:T(8,128)}, u32[]{:S(2)}) copy-start(f32[1,256,1024]{2,1,0:T(8,128)} %param.10) | copy-start | bytes 3145732
Sparse Core Ops, SparseCore 0:
  47.1 57.0 all-gather.1
  109.4 84.1 reduce-scatter.1

commit v5 on v4

--- a/solution.py
+++ b/solution.py
@@ -32,10 +32,6 @@
     cot_chunks = key_cotangent.reshape(tok, chunks, rows).transpose(1, 0, 2)
     cot_chunks = jnp.broadcast_to(cot_chunks[None], (team,) + cot_chunks.shape)
     sent = jnp.concatenate([cols, cot_chunks], axis=1)
-    got = lax.all_to_all(sent, TEAM, split_axis=0, concat_axis=0, tiled=True)
-    inputs_part = got[:, :teams]
-    cot_team = got[:, teams:].transpose(0, 2, 1, 3).reshape(team * tok, kv)
-
     own = pseudo_grads[0]
     pair = own.astype(jnp.float32) + lax.ppermute(own, "y_lo", perm=[(0, 1), (1, 0)]).astype(
         jnp.float32
@@ -46,7 +42,10 @@
     new_anchor = (
         anchor.astype(jnp.float32) - OUTER_RATE * (mean_delta + MOMENTUM * new_moment)
     ).astype(jnp.bfloat16)
-    new_anchor = lax.optimization_barrier(new_anchor)
+    sent, new_anchor = lax.optimization_barrier((sent, new_anchor))
+    got = lax.all_to_all(sent, TEAM, split_axis=0, concat_axis=0, tiled=True)
+    inputs_part = got[:, :teams]
+    cot_team = got[:, teams:].transpose(0, 2, 1, 3).reshape(team * tok, kv)
 
     half = kv // 2
     core = lax.axis_index("core")

time: 205 us -> 225 us (1.098)
  waiting for transfers between devices: 70.5 us -> 88.3 us
  other arithmetic: 9.1 us -> 11.8 us
    all_to_all x1, waiting for transfers between devices: 51.9 us -> 72.2 us  [per_device(): got = lax.all_to_all(sent, TEAM, split_axis=0, concat_axis=0, tiled=True)]
    concatenate x1 -> x0, local copies, waits for them, and re-layouts: 3.34 us -> none  [per_device(): sent = jnp.concatenate([cols, cot_chunks], axis=1)]
    optimization_barrier x0 -> x1, local copies, waits for them, and re-layouts: none -> 3.34 us  [per_device(): sent, new_anchor = lax.optimization_barrier((sent, new_anchor))]
    ppermute x1, waiting for transfers between devices: 2.77 us -> 0.01 us  [per_device(): total = pair + lax.ppermute(pair, 'core', perm=[(0, 1), (1, 0)])]
  transfers between devices with their start and end apart: 6 -> 6, of which waited for: 4 -> 3; matrix products, arithmetic and copies ran while one was open for 21% -> 22% of each run, Pallas kernels for 0% -> 0%
where the time goes in v5:
time: 225 us; the launch traced here: 224 us
  waiting for transfers between devices  88.3 us (39%)
  blocking collectives  52.5 us (23%)
  local copies, waits for them, and re-layouts  35.4 us (16%)
  matrix products  14.9 us (7%)
  between operations  14.2 us (6%)
  other arithmetic  11.8 us (5%)
  starting transfers between devices  7.1 us (3%)
    all_to_all x1, waiting for transfers between devices, per_device(): got = lax.all_to_all(sent, TEAM, split_axis=0, concat_axis=0, tiled=True)  72.2 us
    all_to_all x1, blocking collectives, per_device(): lax.all_to_all(input_part, TEAM, split_axis=0, concat_axis=0, tiled=True)  52.5 us
    reshape x2, local copies, waits for them, and re-layouts, per_device(): input_grad = lax.all_to_all(input_part, TEAM, split_axis=0, concat_axis=0...  15.3 us
    ppermute x1, waiting for transfers between devices, per_device(): lax.ppermute(own, 'y_lo', perm=[(0, 1), (1, 0)]).astype(jnp.float32)  12.3 us
    unnamed x15, local copies, waits for them, and re-layouts  10.1 us
    dot_general x1, matrix products, per_device(): jnp.einsum('satr,stk->ark', inputs_part, cot_team.reshape(team, tok, kv),...  8.4 us
    all_to_all x1, starting transfers between devices, per_device(): got = lax.all_to_all(sent, TEAM, split_axis=0, concat_axis=0, tiled=True)  5.31 us
  transfers between devices with their start and end apart: 6, of which 3 were waited for; matrix products, arithmetic and copies ran while one was open for 22% of the time, Pallas kernels for 0%

profile of v5, /device:TPU:6, one launch (start us, length us, event | category | flops | bytes accessed | tf_op | source)
XLA Modules:
  0.0 224.1 jit_solution(16482416428165816807)
XLA Ops:
  7.2 1.7 collective-permute-start
  8.8 12.3 %collective-permute-done = bf16[256,1024]{1,0:T(8,128)(2,1)S(1)} collective-permute-done((bf16[256,1024]{1,0:T(8,128)(2,1)}, bf16[256,1024]{1,0:T(8,128)(2,1)S(1)}, u32[]{:S(2)}, u32[]{:S(2)}) %collective-permute-start) | collective-permute-done | bytes 524320 | tf_op jit(solution)/shard_map/ppermute | solution.py:36
  21.1 2.4 %convert_add_fusion = f32[256,1024]{1,0:T(8,128)} fusion(bf16[256,1024]{1,0:T(8,128)(2,1)S(1)} %collective-permute-done, bf16[1,256,1024]{2,1,0:T(8,128)(2,1)} %param.8), kind=kLoop, calls=%fused_computation.16 | loop fusion | flops 786432 | bytes 2097152 | tf_op jit(solution)/shard_map/add | solution.py:36
  23.5 0.0 collective-permute-start.1
  23.5 1.2 copy.35
  24.8 6.4 %copy.27 = bf16[256,8192]{0,1:T(8,128)(2,1)} copy(bf16[256,8192]{1,0:T(8,128)(2,1)} %param.12) | data formatting | bytes 8388608 | tf_op args[5]
  31.1 0.2 broadcast_in_dim.15
  31.3 0.0 copy-start.1
  31.3 2.8 %pad_maximum_fusion = bf16[4,12,256,256]{2,3,0,1:T(8,128)(2,1)S(1)} fusion(bf16[4,4,256,256]{2,3,0,1:T(8,128)(2,1)S(1)} %broadcast_in_dim.15, bf16[4,8,256,256]{2,3,0,1:T(8,128)(2,1)} %bitcast.67), kind=kLoop, calls=%fused_computation.3 | loop fusion | flops 3145728 | bytes 12582912 | tf_op jit(solution)/shard_map/concatenate | solution.py:34
  34.1 0.0 collective-permute-done.1
  34.2 3.3 %subtract_convert_fusion.1 = (bf16[256,1024]{1,0:T(8,128)(2,1)S(1)}, f32[256,1024]{1,0:T(8,128)}) fusion(bf16[256,1024]{1,0:T(8,128)(2,1)} %param.7, f32[256,1024]{1,0:T(8,128)} %collective-permute-done.1, bf16[256,1024]{1,0:T(8,128)(2,1)} %copy-done.2, bf16[1,256,1024]{2,1,0:T(8,128)(2,1)S(1)} %copy-done.1, f32[256,1024]{1,0:T(8,128)} %param.9), kind=kLoop, calls=%fused_computation.13 | loop fusion | flops 3407872 | bytes 5242880 | tf_op jit(solution)/shard_map/convert_element_type | solution.py:44
  37.5 3.3 %copy.29 = bf16[4,12,256,256]{2,3,1,0:T(8,128)(2,1)} copy(bf16[4,12,256,256]{2,3,0,1:T(8,128)(2,1)S(1)} %pad_maximum_fusion) | data formatting | bytes 12582912 | tf_op jit(solution)/shard_map/optimization_barrier | solution.py:45
  40.8 5.3 %all-to-all-start = ((bf16[4,12,256,256]{2,3,1,0:T(8,128)(2,1)}), bf16[4,12,256,256]{2,3,1,0:T(8,128)(2,1)}, u32[]{:S(2)}, u32[]{:S(2)}) async-start(bf16[4,12,256,256]{2,3,1,0:T(8,128)(2,1)} %copy.29), calls=%async_computation | async-start | bytes 12582912 | tf_op jit(solution)/shard_map/all_to_all | solution.py:46
  46.1 0.7 constant_dynamic-slice_fusion
  46.9 0.0 all-gather.2.cloned.1.call-update
  46.9 0.0 reduce-scatter.2.cloned.1.call-start
  46.9 72.2 %all-to-all-done = bf16[4,12,256,256]{2,3,1,0:T(8,128)(2,1)} async-done(((bf16[4,12,256,256]{2,3,1,0:T(8,128)(2,1)}), bf16[4,12,256,256]{2,3,1,0:T(8,128)(2,1)}, u32[]{:S(2)}, u32[]{:S(2)}) %all-to-all-start) | async-done | bytes 6291488 | tf_op jit(solution)/shard_map/all_to_all | solution.py:46
  119.2 1.9 slice_bitcast_fusion
  121.1 8.4 %fusion = bf16[8,256,1024]{2,1,0:T(8,128)(2,1)} fusion(bf16[4,12,256,256]{2,3,1,0:T(8,128)(2,1)} %all-to-all-done, bf16[4,256,1024,1]{1,2,3,0:T(8,128)(2,1)S(1)} %bitcast.74), kind=kOutput, calls=%fused_computation.1 | convolution fusion | flops 4299161600 | bytes 12582912 | tf_op jit(solution)/shard_map/satr,stk->ark/dot_general | solution.py:70
  129.5 0.0 reduce-scatter.2.cloned.1.call-update
  129.5 0.0 all-gather.2.cloned.1.call-done
  129.6 0.1 collective-permute-start.2
  129.7 2.5 %copy.32 = bf16[4,256,4,256]{3,2,1,0:T(4,128)(2,1)} copy(bf16[4,256,4,256]{1,3,2,0:T(8,128)(2,1)S(1)} %get-tuple-element.12) | data formatting | bytes 4194304 | tf_op jit(solution)/shard_map/transpose | solution.py:48
  132.2 2.2 copy.38
  134.4 2.4 %fusion.4 = f32[1024,2048]{1,0:T(8,128)S(1)} fusion(bf16[2048,512]{1,0:T(8,128)(2,1)S(1)} %copy-done.5, bf16[1024,1024]{1,0:T(8,128)(2,1)S(1)} %bitcast.76, s32[]{:T(128)S(6)} %select_n.7), kind=kOutput, calls=%fused_computation.10 | convolution fusion | flops 2147483648 | bytes 11534340 | tf_op jit(solution)/shard_map/tk,dk->td/dot_general | solution.py:58
  136.8 4.1 %multiply_convert_fusion = bf16[1024,2048]{1,0:T(8,128)(2,1)S(1)} fusion(f32[1024,2048]{1,0:T(8,128)S(1)} %fusion.4, bf16[2048,512]{1,0:T(8,128)(2,1)} %collective-permute-done.2, bf16[1024,1024]{1,0:T(8,128)(2,1)S(1)} %bitcast.77, s32[]{:T(128)S(6)} %select_n.8), kind=kOutput, calls=%fused_computation.2 | convolution fusion | flops 2153775104 | bytes 15728644 | tf_op jit(solution)/shard_map/tk,dk->td/dot_general | solution.py:60
  140.9 52.5 %all_to_all.10 = bf16[4,256,2048]{2,1,0:T(8,128)(2,1)S(1)} all-to-all(bf16[4,256,2048]{2,1,0:T(8,128)(2,1)S(1)} %bitcast.73), channel_id=1, replica_groups=mesh['y_lo'=2,'core'=2,'y_hi'=2,'x'=4,'z'=4] {'z'}, dimensions={0} | all-to-all | bytes 8388608 | tf_op jit(solution)/shard_map/all_to_all | solution.py:63
  193.4 1.5 copy.39
  194.9 7.4 %copy.41 = bf16[4,256,8,256]{3,0,2,1:T(4,128)(2,1)} copy(bf16[4,256,8,256]{3,2,1,0:T(8,128)(2,1)S(1)} %bitcast.69) | data formatting | bytes 8388608 | tf_op jit(solution)/shard_map/reshape | solution.py:64
  202.3 7.9 %reshape.44 = bf16[256,8192]{1,0:T(8,128)(2,1)} reshape(bf16[256,8,4,256]{3,2,1,0:T(4,128)(2,1)} %bitcast.70) | data formatting | bytes 8388608 | tf_op jit(solution)/shard_map/reshape | solution.py:66
  210.2 3.7 %reduce-scatter.2.cloned.1.call-done = bf16[256,1024]{1,0:T(8,128)(2,1)} async-done(((bf16[2048,1024]{1,0:T(8,128)(2,1)}), bf16[256,1024]{1,0:T(8,128)(2,1)}) %reduce-scatter.2.cloned.1.call-update) | async-done | bytes 524304 | tf_op jit(solution)/shard_map/reduce_scatter | solution.py:78
  213.9 3.4 %fusion.7 = (f32[1,256,1024]{2,1,0:T(8,128)}, bf16[1,256,1024]{2,1,0:T(8,128)(2,1)}, f32[1,256,1024]{2,1,0:T(8,128)}) fusion(bf16[256,1024]{1,0:T(8,128)(2,1)} %reduce-scatter.2.cloned.1.call-done, f32[1,256,1024]{2,1,0:T(8,128)S(1)} %copy-done.3, f32[1,256,1024]{2,1,0:T(8,128)S(1)} %copy-done.4, bf16[256,1024]{1,0:T(8,128)(2,1)S(1)} %get-tuple-element.2), kind=kLoop, calls=%fused_computation.18 | loop fusion | flops 4456448 | bytes 5767168 | tf_op jit(solution)/shard_map/broadcast_in_dim | solution.py:93
  (13 shorter events, 0.0 us)
Async XLA Ops:
  7.2 14.0 %collective-permute-start = (bf16[256,1024]{1,0:T(8,128)(2,1)}, bf16[256,1024]{1,0:T(8,128)(2,1)S(1)}, u32[]{:S(2)}, u32[]{:S(2)}) collective-permute-start(bf16[256,1024]{1,0:T(8,128)(2,1)} %bitcast.78), channel_id=1, source_target_pairs={{0,64},{64,0},{1,65},{65,1},{2,66},{66,2},{3,67},{67,3},{4,68},{68... | collective-permute-start | bytes 1572872 | tf_op jit(solution)/shard_map/ppermute | solution.py:36
  21.1 2.4 %copy-start.2 = (bf16[256,1024]{1,0:T(8,128)(2,1)}, bf16[256,1024]{1,0:T(8,128)(2,1)S(1)}, u32[]{:S(2)}) copy-start(bf16[256,1024]{1,0:T(8,128)(2,1)S(1)} %collective-permute-done) | copy-start | bytes 1572868
  23.5 10.6 %collective-permute-start.1 = (f32[256,1024]{1,0:T(8,128)}, f32[256,1024]{1,0:T(8,128)}, u32[]{:S(2)}, u32[]{:S(2)}) collective-permute-start(f32[256,1024]{1,0:T(8,128)} %convert_add_fusion), channel_id=1, source_target_pairs={{0,32},{32,0},{1,33},{33,1},{2,34},{34,2},{3,35},{35,3},{4,36},{36... | collective-permute-start | bytes 3145736 | tf_op jit(solution)/shard_map/ppermute | solution.py:39
  31.3 2.8 %copy-start.1 = (bf16[1,256,1024]{2,1,0:T(8,128)(2,1)S(1)}, bf16[1,256,1024]{2,1,0:T(8,128)(2,1)}, u32[]{:S(2)}) copy-start(bf16[1,256,1024]{2,1,0:T(8,128)(2,1)} %param.8) | copy-start | bytes 1572868
  37.5 176.4 %copy-start = (bf16[256,1024]{1,0:T(8,128)(2,1)}, bf16[256,1024]{1,0:T(8,128)(2,1)S(1)}, u32[]{:S(2)}) copy-start(bf16[256,1024]{1,0:T(8,128)(2,1)S(1)} %get-tuple-element.2) | copy-start | bytes 1572868
  40.8 78.4 %all-to-all-start = ((bf16[4,12,256,256]{2,3,1,0:T(8,128)(2,1)}), bf16[4,12,256,256]{2,3,1,0:T(8,128)(2,1)}, u32[]{:S(2)}, u32[]{:S(2)}) async-start(bf16[4,12,256,256]{2,3,1,0:T(8,128)(2,1)} %copy.29), calls=%async_computation | async-start | bytes 12582912 | tf_op jit(solution)/shard_map/all_to_all | solution.py:46
  46.1 83.5 %all-gather.2.cloned.1.call-start = ((), (), s32[]{:S(2)}) async-start(), calls=%async_computation.4 | async-start | bytes 2359296 | tf_op jit(solution)/shard_map/all_gather | solution.py:52
  46.9 167.0 %reduce-scatter.2.cloned.1.call-start = ((), (), s32[]{:S(2)}) async-start(), calls=%async_computation.3 | async-start | bytes 4718592 | tf_op jit(solution)/shard_map/reduce_scatter | solution.py:78
  129.6 7.2 %collective-permute-start.2 = (bf16[2048,512]{1,0:T(8,128)(2,1)}, bf16[2048,512]{1,0:T(8,128)(2,1)}, u32[]{:S(2)}, u32[]{:S(2)}) collective-permute-start(bf16[2048,512]{1,0:T(8,128)(2,1)} %all-gather.2.cloned.1.call-done), channel_id=1, source_target_pairs={{0,32},{32,0},{1,33},{33,1},{2,34},{34,2},{3,35},{35,3},{4,36},{36... | collective-permute-start | bytes 6291464 | tf_op jit(solution)/shard_map/ppermute | solution.py:55
  132.2 2.2 %copy-start.5 = (bf16[2048,512]{1,0:T(8,128)(2,1)S(1)}, bf16[2048,512]{1,0:T(8,128)(2,1)}, u32[]{:S(2)}) copy-start(bf16[2048,512]{1,0:T(8,128)(2,1)} %all-gather.2.cloned.1.call-done) | copy-start | bytes 6291460
  202.3 11.6 %copy-start.3 = (f32[1,256,1024]{2,1,0:T(8,128)S(1)}, f32[1,256,1024]{2,1,0:T(8,128)}, u32[]{:S(2)}) copy-start(f32[1,256,1024]{2,1,0:T(8,128)} %param.11) | copy-start | bytes 3145732
  202.3 11.6 %copy-start.4 = (f32[1,256,1024]{2,1,0:T(8,128)S(1)}, f32[1,256,1024]{2,1,0:T(8,128)}, u32[]{:S(2)}) copy-start(f32[1,256,1024]{2,1,0:T(8,128)} %param.10) | copy-start | bytes 3145732
Sparse Core Ops, SparseCore 0:
  49.8 57.2 all-gather.1
  129.7 84.1 reduce-scatter.1

commit v6 on v4

--- a/solution.py
+++ b/solution.py
@@ -75,8 +75,13 @@
             preferred_element_type=jnp.float32,
         )
         * scale
-    ).astype(jnp.bfloat16).reshape(teams * rows, kv)
-    grads = lax.psum_scatter(partial, TEAMS, scatter_dimension=0, tiled=True).astype(jnp.float32)
+    ).astype(jnp.bfloat16)
+    grads = jnp.sum(
+        lax.all_to_all(partial, TEAMS, split_axis=0, concat_axis=0, tiled=True).astype(
+            jnp.float32
+        ),
+        axis=0,
+    )
 
     correct_one = 1.0 - BETA_ONE**ADAM_STEP
     correct_two = 1.0 - BETA_TWO**ADAM_STEP

time: 205 us -> 254 us (1.24)
  waiting for transfers between devices: 70.5 us -> 153 us
  blocking collectives: 52.5 us -> 0 us
  starting transfers between devices: 7.31 us -> 19.7 us
  other arithmetic: 9.1 us -> 12.5 us
    all_to_all x0 -> x2, waiting for transfers between devices: none -> 85.7 us  [the longest x1 45.5 us: per_device(): lax.all_to_all(partial, TEAMS, split_axis=0, concat_axis=0, tiled=True)]
    all_to_all x1 -> x0, blocking collectives: 52.5 us -> none  [per_device(): lax.all_to_all(input_part, TEAM, split_axis=0, concat_axis=0, tiled=True)]
    all_to_all x0 -> x2, starting transfers between devices: none -> 12.5 us  [the longest x1 7.4 us: per_device(): lax.all_to_all(partial, TEAMS, split_axis=0, concat_axis=0, tiled=True)]
    reduce_scatter x1 -> x0, waiting for transfers between devices: 3.67 us -> none  [per_device(): lax.psum_scatter(partial, TEAMS, scatter_dimension=0, tiled=True)]
    reduce_sum x0 -> x1, other arithmetic: none -> 3.29 us  [per_device(): jnp.sum(lax.all_to_all(partial, TEAMS, split_axis=0, concat_axis=0, tiled...]
  transfers between devices with their start and end apart: 6 -> 7, of which waited for: 4 -> 5; matrix products, arithmetic and copies ran while one was open for 21% -> 13% of each run, Pallas kernels for 0% -> 0%
where the time goes in v6:
time: 254 us; the launch traced here: 253 us
  waiting for transfers between devices  153 us (60%)
  local copies, waits for them, and re-layouts  37.4 us (15%)
  starting transfers between devices  19.7 us (8%)
  matrix products  16.7 us (7%)
  between operations  14.2 us (6%)
  other arithmetic  12.5 us (5%)
    all_to_all x1, waiting for transfers between devices, per_device(): got = lax.all_to_all(sent, TEAM, split_axis=0, concat_axis=0, tiled=True)  52 us
    all_to_all x1, waiting for transfers between devices, per_device(): lax.all_to_all(partial, TEAMS, split_axis=0, concat_axis=0, tiled=True)  45.5 us
    all_to_all x1, waiting for transfers between devices, per_device(): lax.all_to_all(input_part, TEAM, split_axis=0, concat_axis=0, tiled=True)  40.2 us
    reshape x2, local copies, waits for them, and re-layouts, per_device(): input_grad = lax.all_to_all(input_part, TEAM, split_axis=0, concat_axis=0...  15.1 us
    unnamed x15, local copies, waits for them, and re-layouts  12.3 us
    ppermute x1, waiting for transfers between devices, per_device(): lax.ppermute(own, 'y_lo', perm=[(0, 1), (1, 0)]).astype(jnp.float32)  12.1 us
    dot_general x1, matrix products, per_device(): jnp.einsum('satr,stk->ark', inputs_part, cot_team.reshape(team, tok, kv),...  8.32 us
    all_to_all x1, starting transfers between devices, per_device(): lax.all_to_all(partial, TEAMS, split_axis=0, concat_axis=0, tiled=True)  7.4 us
  transfers between devices with their start and end apart: 7, of which 5 were waited for; matrix products, arithmetic and copies ran while one was open for 13% of the time, Pallas kernels for 0%

profile of v6, /device:TPU:6, one launch (start us, length us, event | category | flops | bytes accessed | tf_op | source)
XLA Modules:
  0.0 253.0 jit_solution(985460826680274403)
XLA Ops:
  7.2 1.2 copy.35
  8.4 6.4 %copy.27 = bf16[256,8192]{0,1:T(8,128)(2,1)} copy(bf16[256,8192]{1,0:T(8,128)(2,1)} %param.12) | data formatting | bytes 8388608 | tf_op args[5]
  14.8 0.2 broadcast_in_dim.4
  15.0 2.7 %pad_maximum_fusion = bf16[4,12,256,256]{2,3,0,1:T(8,128)(2,1)S(1)} fusion(bf16[4,4,256,256]{2,3,0,1:T(8,128)(2,1)S(1)} %broadcast_in_dim.4, bf16[4,8,256,256]{2,3,0,1:T(8,128)(2,1)} %bitcast.67), kind=kLoop, calls=%fused_computation.4 | loop fusion | flops 3145728 | bytes 12582912 | tf_op jit(solution)/shard_map/concatenate | solution.py:34
  17.7 3.3 %copy.29 = bf16[4,12,256,256]{2,3,1,0:T(8,128)(2,1)} copy(bf16[4,12,256,256]{2,3,0,1:T(8,128)(2,1)S(1)} %pad_maximum_fusion) | data formatting | bytes 12582912 | tf_op jit(solution)/shard_map/concatenate | solution.py:34
  21.1 5.4 %all-to-all-start = ((bf16[4,12,256,256]{2,3,1,0:T(8,128)(2,1)}), bf16[4,12,256,256]{2,3,1,0:T(8,128)(2,1)}, u32[]{:S(2)}, u32[]{:S(2)}) async-start(bf16[4,12,256,256]{2,3,1,0:T(8,128)(2,1)} %copy.29), calls=%async_computation | async-start | bytes 12582912 | tf_op jit(solution)/shard_map/all_to_all | solution.py:35
  26.5 1.7 collective-permute-start
  28.2 12.1 %collective-permute-done = bf16[256,1024]{1,0:T(8,128)(2,1)S(1)} collective-permute-done((bf16[256,1024]{1,0:T(8,128)(2,1)S(1)}, bf16[256,1024]{1,0:T(8,128)(2,1)S(1)}, u32[]{:S(2)}, u32[]{:S(2)}) %collective-permute-start) | collective-permute-done | bytes 524320 | tf_op jit(solution)/shard_map/ppermute | solution.py:40
  40.3 0.2 convert_add_fusion
  40.4 0.1 collective-permute-start.1
  40.5 2.8 %collective-permute-done.1 = f32[256,1024]{1,0:T(8,128)} collective-permute-done((f32[256,1024]{1,0:T(8,128)S(1)}, f32[256,1024]{1,0:T(8,128)}, u32[]{:S(2)}, u32[]{:S(2)}) %collective-permute-start.1) | collective-permute-done | bytes 1048608 | tf_op jit(solution)/shard_map/ppermute | solution.py:43
  43.3 2.8 %subtract_convert_fusion = (bf16[256,1024]{1,0:T(8,128)(2,1)S(1)}, f32[256,1024]{1,0:T(8,128)}) fusion(bf16[256,1024]{1,0:T(8,128)(2,1)} %param.7, f32[256,1024]{1,0:T(8,128)} %collective-permute-done.1, bf16[256,1024]{1,0:T(8,128)(2,1)S(1)} %collective-permute-done, bf16[1,256,1024]{2,1,0:T(8,128)(2,1)S(1)} %copy-done.3, f32[256,1024]{1,0:T(8,128)S(1)} %copy-done.4), kind=kLoop, calls=%fused_computation.23 | loop fusion | flops 3407872 | bytes 5242880 | tf_op jit(solution)/shard_map/convert_element_type | solution.py:48
  46.1 0.8 constant_dynamic-slice_fusion
  46.9 0.0 all-gather.2.cloned.1.call-update
  46.9 52.0 %all-to-all-done = bf16[4,12,256,256]{2,3,1,0:T(8,128)(2,1)} async-done(((bf16[4,12,256,256]{2,3,1,0:T(8,128)(2,1)}), bf16[4,12,256,256]{2,3,1,0:T(8,128)(2,1)}, u32[]{:S(2)}, u32[]{:S(2)}) %all-to-all-start) | async-done | bytes 6291488 | tf_op jit(solution)/shard_map/all_to_all | solution.py:35
  98.9 1.9 slice_bitcast_fusion
  100.8 8.3 %fusion = bf16[8,256,1024]{2,1,0:T(8,128)(2,1)} fusion(bf16[4,12,256,256]{2,3,1,0:T(8,128)(2,1)} %all-to-all-done, bf16[4,256,1024,1]{1,2,3,0:T(8,128)(2,1)S(1)} %bitcast.72), kind=kOutput, calls=%fused_computation.1 | convolution fusion | flops 4299161600 | bytes 12582912 | tf_op jit(solution)/shard_map/satr,stk->ark/dot_general | solution.py:71
  109.2 7.4 %all-to-all-start.1 = ((bf16[8,256,1024]{2,1,0:T(8,128)(2,1)}), bf16[8,256,1024]{2,1,0:T(8,128)(2,1)}, u32[]{:S(2)}, u32[]{:S(2)}) async-start(bf16[8,256,1024]{2,1,0:T(8,128)(2,1)} %fusion), calls=%async_computation.1 | async-start | bytes 8388608 | tf_op jit(solution)/shard_map/all_to_all | solution.py:80
  116.6 2.5 copy.32
  119.1 2.2 copy.38
  121.4 2.4 fusion.12
  123.7 6.0 %multiply_convert_fusion = bf16[1024,2048]{1,0:T(8,128)(2,1)} fusion(f32[1024,2048]{1,0:T(8,128)S(1)} %fusion.12, bf16[2048,512]{1,0:T(8,128)(2,1)} %collective-permute-done.2, bf16[1024,1024]{1,0:T(8,128)(2,1)S(1)} %bitcast.75, s32[]{:T(128)S(6)} %select_n.8), kind=kOutput, calls=%fused_computation.2 | convolution fusion | flops 2153775104 | bytes 15728644 | tf_op jit(solution)/shard_map/tk,dk->td/dot_general | solution.py:61
  129.7 45.5 %all-to-all-done.1 = bf16[8,256,1024]{2,1,0:T(8,128)(2,1)} async-done(((bf16[8,256,1024]{2,1,0:T(8,128)(2,1)}), bf16[8,256,1024]{2,1,0:T(8,128)(2,1)}, u32[]{:S(2)}, u32[]{:S(2)}) %all-to-all-start.1) | async-done | bytes 4194336 | tf_op jit(solution)/shard_map/all_to_all | solution.py:80
  175.2 5.1 %all-to-all-start.2 = ((bf16[4,256,2048]{2,1,0:T(8,128)(2,1)}), bf16[4,256,2048]{2,1,0:T(8,128)(2,1)}, u32[]{:S(2)}, u32[]{:S(2)}) async-start(bf16[4,256,2048]{2,1,0:T(8,128)(2,1)} %bitcast.71), calls=%async_computation.2 | async-start | bytes 8388608 | tf_op jit(solution)/shard_map/all_to_all | solution.py:64
  180.3 0.0 copy-start.1
  180.4 3.3 %convert_reduce_fusion = f32[256,1024]{1,0:T(8,128)S(1)} fusion(bf16[8,256,1024]{2,1,0:T(8,128)(2,1)} %all-to-all-done.1), kind=kLoop, calls=%fused_computation.3 | loop fusion | flops 3932160 | bytes 5242880 | tf_op jit(solution)/shard_map/reduce_sum | solution.py:79
  183.7 1.9 fusion.8
  185.6 1.6 fusion.15
  187.2 40.2 %all-to-all-done.2 = bf16[4,256,2048]{2,1,0:T(8,128)(2,1)} async-done(((bf16[4,256,2048]{2,1,0:T(8,128)(2,1)}), bf16[4,256,2048]{2,1,0:T(8,128)(2,1)}, u32[]{:S(2)}, u32[]{:S(2)}) %all-to-all-start.2) | async-done | bytes 4194336 | tf_op jit(solution)/shard_map/all_to_all | solution.py:64
  227.4 3.7 %copy.39 = bf16[128,8,8,256]{3,2,1,0:T(8,128)(2,1)S(1)} copy(bf16[128,8,8,256]{3,1,2,0:T(8,128)(2,1)} %bitcast.29) | data formatting | bytes 8388608
  231.0 7.4 %copy.41 = bf16[4,256,8,256]{3,0,2,1:T(4,128)(2,1)} copy(bf16[4,256,8,256]{3,2,1,0:T(8,128)(2,1)S(1)} %bitcast.68) | data formatting | bytes 8388608 | tf_op jit(solution)/shard_map/reshape | solution.py:65
  238.4 7.7 %reshape.57 = bf16[256,8192]{1,0:T(8,128)(2,1)} reshape(bf16[256,8,4,256]{3,2,1,0:T(4,128)(2,1)} %bitcast.69) | data formatting | bytes 8388608 | tf_op jit(solution)/shard_map/reshape | solution.py:67
  (15 shorter events, 0.0 us)
Async XLA Ops:
  21.1 5.4 %copy-start.3 = (bf16[1,256,1024]{2,1,0:T(8,128)(2,1)S(1)}, bf16[1,256,1024]{2,1,0:T(8,128)(2,1)}, u32[]{:S(2)}) copy-start(bf16[1,256,1024]{2,1,0:T(8,128)(2,1)} %param.8) | copy-start | bytes 1572868
  21.1 22.2 %copy-start.4 = (f32[256,1024]{1,0:T(8,128)S(1)}, f32[256,1024]{1,0:T(8,128)}, u32[]{:S(2)}) copy-start(f32[256,1024]{1,0:T(8,128)} %param.9) | copy-start | bytes 3145732
  21.1 77.8 %all-to-all-start = ((bf16[4,12,256,256]{2,3,1,0:T(8,128)(2,1)}), bf16[4,12,256,256]{2,3,1,0:T(8,128)(2,1)}, u32[]{:S(2)}, u32[]{:S(2)}) async-start(bf16[4,12,256,256]{2,3,1,0:T(8,128)(2,1)} %copy.29), calls=%async_computation | async-start | bytes 12582912 | tf_op jit(solution)/shard_map/all_to_all | solution.py:35
  26.5 90.1 %all-gather.2.cloned.1.call-start = ((), (), s32[]{:S(2)}) async-start(), calls=%async_computation.3 | async-start | bytes 2359296 | tf_op jit(solution)/shard_map/all_gather | solution.py:53
  26.5 13.7 %collective-permute-start = (bf16[256,1024]{1,0:T(8,128)(2,1)S(1)}, bf16[256,1024]{1,0:T(8,128)(2,1)S(1)}, u32[]{:S(2)}, u32[]{:S(2)}) collective-permute-start(bf16[256,1024]{1,0:T(8,128)(2,1)S(1)} %bitcast.76), channel_id=1, source_target_pairs={{0,64},{64,0},{1,65},{65,1},{2,66},{66,2},{3,67},{67,3},{4,68},{68... | collective-permute-start | bytes 1572872 | tf_op jit(solution)/shard_map/ppermute | solution.py:40
  40.4 2.9 %collective-permute-start.1 = (f32[256,1024]{1,0:T(8,128)S(1)}, f32[256,1024]{1,0:T(8,128)}, u32[]{:S(2)}, u32[]{:S(2)}) collective-permute-start(f32[256,1024]{1,0:T(8,128)S(1)} %convert_add_fusion), channel_id=1, source_target_pairs={{0,32},{32,0},{1,33},{33,1},{2,34},{34,2},{3,35},{35,3},{4,36},{36... | collective-permute-start | bytes 3145736 | tf_op jit(solution)/shard_map/ppermute | solution.py:43
  46.1 139.4 %copy-start.2 = (bf16[256,1024]{1,0:T(8,128)(2,1)}, bf16[256,1024]{1,0:T(8,128)(2,1)S(1)}, u32[]{:S(2)}) copy-start(bf16[256,1024]{1,0:T(8,128)(2,1)S(1)} %get-tuple-element.6) | copy-start | bytes 1572868
  109.2 66.1 %all-to-all-start.1 = ((bf16[8,256,1024]{2,1,0:T(8,128)(2,1)}), bf16[8,256,1024]{2,1,0:T(8,128)(2,1)}, u32[]{:S(2)}, u32[]{:S(2)}) async-start(bf16[8,256,1024]{2,1,0:T(8,128)(2,1)} %fusion), calls=%async_computation.1 | async-start | bytes 8388608 | tf_op jit(solution)/shard_map/all_to_all | solution.py:80
  116.6 7.2 %collective-permute-start.2 = (bf16[2048,512]{1,0:T(8,128)(2,1)}, bf16[2048,512]{1,0:T(8,128)(2,1)}, u32[]{:S(2)}, u32[]{:S(2)}) collective-permute-start(bf16[2048,512]{1,0:T(8,128)(2,1)} %all-gather.2.cloned.1.call-done), channel_id=1, source_target_pairs={{0,32},{32,0},{1,33},{33,1},{2,34},{34,2},{3,35},{35,3},{4,36},{36... | collective-permute-start | bytes 6291464 | tf_op jit(solution)/shard_map/ppermute | solution.py:56
  119.1 2.2 copy-start.5
  175.2 52.1 %all-to-all-start.2 = ((bf16[4,256,2048]{2,1,0:T(8,128)(2,1)}), bf16[4,256,2048]{2,1,0:T(8,128)(2,1)}, u32[]{:S(2)}, u32[]{:S(2)}) async-start(bf16[4,256,2048]{2,1,0:T(8,128)(2,1)} %bitcast.71), calls=%async_computation.2 | async-start | bytes 8388608 | tf_op jit(solution)/shard_map/all_to_all | solution.py:64
  180.3 3.3 %copy-start = (f32[1,256,1024]{2,1,0:T(8,128)S(1)}, f32[1,256,1024]{2,1,0:T(8,128)}, u32[]{:S(2)}) copy-start(f32[1,256,1024]{2,1,0:T(8,128)} %param.11) | copy-start | bytes 3145732
  180.3 3.3 %copy-start.1 = (f32[1,256,1024]{2,1,0:T(8,128)S(1)}, f32[1,256,1024]{2,1,0:T(8,128)}, u32[]{:S(2)}) copy-start(f32[1,256,1024]{2,1,0:T(8,128)} %param.10) | copy-start | bytes 3145732
Sparse Core Ops, SparseCore 0:
  47.1 57.0 all-gather.1

commit v7 on v3

--- a/solution.py
+++ b/solution.py
@@ -42,28 +42,30 @@
     new_anchor = (
         anchor.astype(jnp.float32) - OUTER_RATE * (mean_delta + MOMENTUM * new_moment)
     ).astype(jnp.bfloat16)
-    new_anchor = lax.optimization_barrier(new_anchor)
+    new_anchor, cot_team = lax.optimization_barrier((new_anchor, cot_team))
 
     half = kv // 2
     core = lax.axis_index("core")
     mine = lax.all_gather(
-        lax.dynamic_slice_in_dim(new_anchor, core * half, half, axis=1), TEAMS, axis=0, tiled=True
+        lax.dynamic_slice_in_dim(new_anchor, core * half, half, axis=1), FSDP, axis=0, tiled=True
     )
     other = lax.ppermute(mine, "core", perm=[(0, 1), (1, 0)])
-    cot_mine = lax.dynamic_slice_in_dim(cot_team, core * half, half, axis=1)
-    cot_other = lax.dynamic_slice_in_dim(cot_team, (1 - core) * half, half, axis=1)
+    cot_mine = lax.dynamic_slice_in_dim(key_cotangent, core * half, half, axis=1)
+    cot_other = lax.dynamic_slice_in_dim(key_cotangent, (1 - core) * half, half, axis=1)
     product = jnp.einsum(
         "tk,dk->td", cot_mine, mine, preferred_element_type=jnp.float32
     ) + jnp.einsum("tk,dk->td", cot_other, other, preferred_element_type=jnp.float32)
-    input_part = (product * scale).astype(jnp.bfloat16)
-    input_grad = lax.all_to_all(
-        input_part.reshape(team, tok, teams, 1, rows), TEAM, split_axis=0, concat_axis=3, tiled=True
-    ).reshape(tok, width)
+    input_grad = (product * scale).astype(jnp.bfloat16)
 
     partial = (
         jnp.einsum("td,tk->dk", inputs_part, cot_team, preferred_element_type=jnp.float32) * scale
     ).astype(jnp.bfloat16)
-    grads = lax.psum_scatter(partial, TEAMS, scatter_dimension=0, tiled=True).astype(jnp.float32)
+    grads = jnp.sum(
+        lax.all_to_all(
+            partial.reshape(teams, rows, kv), TEAMS, split_axis=0, concat_axis=0, tiled=True
+        ).astype(jnp.float32),
+        axis=0,
+    )
 
     correct_one = 1.0 - BETA_ONE**ADAM_STEP
     correct_two = 1.0 - BETA_TWO**ADAM_STEP

time: 203 us -> 280 us (1.38)
  waiting for transfers between devices: 66.7 us -> 187 us
  blocking collectives: 52.3 us -> 0 us
  starting transfers between devices: 7.44 us -> 13.3 us
    all_gather x1, waiting for transfers between devices: 0.02 us -> 103 us  [per_device(): lax.all_gather(lax.dynamic_slice_in_dim(new_anchor, core * half, half, ax...]
    all_to_all x0 -> x1, waiting for transfers between devices: none -> 57.2 us  [per_device(): lax.all_to_all(partial.reshape(teams, rows, kv), TEAMS, split_axis=0, con...]
    all_to_all x1 -> x0, blocking collectives: 52.3 us -> none  [per_device(): lax.all_to_all(input_part.reshape(team, tok, teams, 1, rows), TEAM, split...]
    all_to_all x1, waiting for transfers between devices: 46.6 us -> 0.01 us  [per_device(): lax.all_to_all(inputs.reshape(tok, teams, team, rows), TEAM, split_axis=2...]
    all_gather x1, waiting for transfers between devices: 0.01 us -> 13.3 us  [per_device(): cot_team = lax.all_gather(key_cotangent, TEAM, axis=0, tiled=True)]
    all_to_all x1 -> x0, local copies, waits for them, and re-layouts: 7.53 us -> none  [per_device(): lax.all_to_all(input_part.reshape(team, tok, teams, 1, rows), TEAM, split...]
    reduce_scatter x1 -> x0, waiting for transfers between devices: 7.06 us -> none  [per_device(): lax.psum_scatter(partial, TEAMS, scatter_dimension=0, tiled=True)]
    all_to_all x0 -> x1, starting transfers between devices: none -> 6.54 us  [per_device(): lax.all_to_all(partial.reshape(teams, rows, kv), TEAMS, split_axis=0, con...]
  transfers between devices with their start and end apart: 7 -> 7, of which waited for: 3 -> 5; matrix products, arithmetic and copies ran while one was open for 28% -> 20% of each run, Pallas kernels for 0% -> 0%
where the time goes in v7:
time: 280 us; the launch traced here: 279 us
  waiting for transfers between devices  187 us (67%)
  local copies, waits for them, and re-layouts  35.8 us (13%)
  matrix products  18.8 us (7%)
  between operations  14.1 us (5%)
  starting transfers between devices  13.3 us (5%)
  other arithmetic  10.9 us (4%)
    all_gather x1, waiting for transfers between devices, per_device(): lax.all_gather(lax.dynamic_slice_in_dim(new_anchor, core * half, half, ax...  103 us
    all_to_all x1, waiting for transfers between devices, per_device(): lax.all_to_all(partial.reshape(teams, rows, kv), TEAMS, split_axis=0, con...  57.2 us
    unnamed x19, local copies, waits for them, and re-layouts  20.3 us
    all_gather x1, waiting for transfers between devices, per_device(): cot_team = lax.all_gather(key_cotangent, TEAM, axis=0, tiled=True)  13.3 us
    reshape x2, local copies, waits for them, and re-layouts, per_device(): inputs.reshape(tok, teams, team, rows)  12.5 us
    ppermute x1, waiting for transfers between devices, per_device(): lax.ppermute(own, 'y_lo', perm=[(0, 1), (1, 0)]).astype(jnp.float32)  12.1 us
    dot_general x1, matrix products, per_device(): jnp.einsum('tk,dk->td', cot_other, other, preferred_element_type=jnp.floa...  8.06 us
    all_to_all x1, starting transfers between devices, per_device(): lax.all_to_all(partial.reshape(teams, rows, kv), TEAMS, split_axis=0, con...  6.54 us
  transfers between devices with their start and end apart: 7, of which 5 were waited for; matrix products, arithmetic and copies ran while one was open for 20% of the time, Pallas kernels for 0%

profile of v7, /device:TPU:6, one launch (start us, length us, event | category | flops | bytes accessed | tf_op | source)
XLA Modules:
  0.0 279.4 jit_solution(10861435419062307790)
XLA Ops:
  7.2 0.7 all-gather.3.cloned.1.call-update
  7.9 1.2 copy.15
  9.2 1.7 collective-permute-start
  10.8 12.1 %collective-permute-done = bf16[256,1024]{0,1:T(8,128)(2,1)S(1)} collective-permute-done((bf16[256,1024]{0,1:T(8,128)(2,1)S(1)}, bf16[256,1024]{0,1:T(8,128)(2,1)S(1)}, u32[]{:S(2)}, u32[]{:S(2)}) %collective-permute-start) | collective-permute-done | bytes 524320 | tf_op jit(solution)/shard_map/ppermute | solution.py:36
  22.9 1.1 convert_add_fusion
  24.0 1.6 copy.16
  25.6 1.2 copy.14
  26.8 0.2 collective-permute-done.1
  27.0 2.6 multiply_add_fusion
  29.6 13.3 %all-gather.3.cloned.1.call-done = bf16[1024,1024]{1,0:T(8,128)(2,1)} async-done(((bf16[256,1024]{1,0:T(8,128)(2,1)}), bf16[1024,1024]{1,0:T(8,128)(2,1)}) %all-gather.3.cloned.1.call-update) | async-done | bytes 2097168 | tf_op jit(solution)/shard_map/all_gather | solution.py:30
  43.0 0.7 constant_dynamic-slice_fusion
  43.7 7.8 %reshape.43 = bf16[256,8,4,256]{3,2,1,0:T(4,128)(2,1)} reshape(bf16[256,8192]{1,0:T(8,128)(2,1)} %param.12) | data formatting | bytes 8388608 | tf_op jit(solution)/shard_map/reshape | solution.py:32
  51.5 4.7 %copy.18 = bf16[256,8,4,256]{3,1,0,2:T(8,128)(2,1)} copy(bf16[256,8,4,256]{3,2,1,0:T(4,128)(2,1)} %reshape.43) | data formatting | bytes 8388608 | tf_op jit(solution)/shard_map/reshape | solution.py:32
  56.2 5.0 %all-to-all-start = ((bf16[256,8,4,256]{3,1,0,2:T(8,128)(2,1)}), bf16[256,8,4,256]{3,1,0,2:T(8,128)(2,1)}, u32[]{:S(2)}, u32[]{:S(2)}) async-start(bf16[256,8,4,256]{3,1,0,2:T(8,128)(2,1)} %copy.18), calls=%async_computation | async-start | bytes 8388608 | tf_op jit(solution)/shard_map/all_to_all | solution.py:31
  61.2 103.1 %all-gather.5.cloned.1.call-done = bf16[8192,512]{0,1:T(8,128)(2,1)} async-done(((bf16[256,512]{0,1:T(8,128)(2,1)}), bf16[8192,512]{0,1:T(8,128)(2,1)}) %all-gather.5.cloned.1.call-update) | async-done | bytes 8388624 | tf_op jit(solution)/shard_map/all_gather | solution.py:49
  164.3 3.7 %copy.29 = bf16[128,8,8,256]{3,1,2,0:T(8,128)(2,1)S(1)} copy(bf16[128,8,8,256]{3,2,1,0:T(8,128)(2,1)} %bitcast.13) | data formatting | bytes 8388608
  168.0 4.9 %multiply_convert_fusion = bf16[1024,2048]{1,0:T(8,128)(2,1)S(1)} fusion(bf16[1024,1024]{1,0:T(8,128)(2,1)S(1)} %copy-done.3, bf16[1024,2048]{1,0:T(8,128)(2,1)S(1)} %bitcast.49), kind=kOutput, calls=%fused_computation.4 | convolution fusion | flops 4299161600 | bytes 10485760 | tf_op jit(solution)/shard_map/td,tk->dk/dot_general | solution.py:61
  172.9 2.3 copy.31
  175.2 6.5 %all-to-all-start.1 = ((bf16[8,256,1024]{1,2,0:T(8,128)(2,1)}), bf16[8,256,1024]{1,2,0:T(8,128)(2,1)}, u32[]{:S(2)}, u32[]{:S(2)}) async-start(bf16[8,256,1024]{1,2,0:T(8,128)(2,1)} %bitcast.47), calls=%async_computation.1 | async-start | bytes 8388608 | tf_op jit(solution)/shard_map/all_to_all | solution.py:64
  181.7 0.3 copy.17
  182.1 1.6 copy.21
  183.6 2.5 copy.23
  186.2 1.0 copy.22
  187.2 57.2 %all-to-all-done.1 = bf16[8,256,1024]{1,2,0:T(8,128)(2,1)} async-done(((bf16[8,256,1024]{1,2,0:T(8,128)(2,1)}), bf16[8,256,1024]{1,2,0:T(8,128)(2,1)}, u32[]{:S(2)}, u32[]{:S(2)}) %all-to-all-start.1) | async-done | bytes 4194336 | tf_op jit(solution)/shard_map/all_to_all | solution.py:64
  244.4 2.9 %convert_reduce_fusion = f32[256,1024]{0,1:T(8,128)S(1)} fusion(bf16[8,256,1024]{1,2,0:T(8,128)(2,1)} %all-to-all-done.1), kind=kLoop, calls=%fused_computation.3 | loop fusion | flops 3932160 | bytes 5242880 | tf_op jit(solution)/shard_map/reduce_sum | solution.py:63
  247.2 2.7 fusion.13
  249.9 2.0 copy.24
  252.0 1.6 fusion.9
  253.6 2.5 copy.25
  256.1 2.5 copy.26
  258.6 5.9 %fusion.15 = f32[256,8192]{1,0:T(8,128)S(1)} fusion(bf16[8192,512]{0,1:T(8,128)(2,1)} %all-gather.5.cloned.1.call-done, bf16[256,1024]{1,0:T(8,128)(2,1)} %param.13, s32[]{:T(128)S(6)} %select_n.7), kind=kOutput, calls=%fused_computation.27 | convolution fusion | flops 2147483648 | bytes 17039364 | tf_op jit(solution)/shard_map/tk,dk->td/dot_general | solution.py:55
  264.5 8.1 %fusion.1 = bf16[256,8192]{1,0:T(8,128)(2,1)} fusion(f32[256,8192]{1,0:T(8,128)S(1)} %fusion.15, bf16[8192,512]{0,1:T(8,128)(2,1)} %collective-permute-done.2, bf16[256,1024]{1,0:T(8,128)(2,1)S(1)} %copy-done.1, s32[]{:T(128)S(6)} %select_n.8), kind=kOutput, calls=%fused_computation.2 | convolution fusion | flops 2153775104 | bytes 21233668 | tf_op jit(solution)/shard_map/tk,dk->td/dot_general | solution.py:57
  (15 shorter events, 0.1 us)
Async XLA Ops:
  7.2 35.8 %all-gather.3.cloned.1.call-start = ((), (), s32[]{:S(2)}) async-start(), calls=%async_computation.2 | async-start | bytes 2621440 | tf_op jit(solution)/shard_map/all_gather | solution.py:30
  7.9 156.4 %all-gather.5.cloned.1.call-start = ((), (), s32[]{:S(2)}) async-start(), calls=%async_computation.3 | async-start | bytes 8650752 | tf_op jit(solution)/shard_map/all_gather | solution.py:49
  9.2 13.7 %collective-permute-start = (bf16[256,1024]{0,1:T(8,128)(2,1)S(1)}, bf16[256,1024]{0,1:T(8,128)(2,1)S(1)}, u32[]{:S(2)}, u32[]{:S(2)}) collective-permute-start(bf16[256,1024]{0,1:T(8,128)(2,1)S(1)} %bitcast.48), channel_id=1, source_target_pairs={{0,64},{64,0},{1,65},{65,1},{2,66},{66,2},{3,67},{67,3},{4,68},{68... | collective-permute-start | bytes 1572872 | tf_op jit(solution)/shard_map/ppermute | solution.py:36
  24.0 3.0 %collective-permute-start.1 = (f32[256,1024]{0,1:T(8,128)}, f32[256,1024]{0,1:T(8,128)}, u32[]{:S(2)}, u32[]{:S(2)}) collective-permute-start(f32[256,1024]{0,1:T(8,128)} %convert_add_fusion), channel_id=1, source_target_pairs={{0,32},{32,0},{1,33},{33,1},{2,34},{34,2},{3,35},{35,3},{4,36},{36... | collective-permute-start | bytes 3145736 | tf_op jit(solution)/shard_map/ppermute | solution.py:39
  29.6 156.5 %copy-start = (bf16[256,1024]{0,1:T(8,128)(2,1)}, bf16[256,1024]{0,1:T(8,128)(2,1)S(1)}, u32[]{:S(2)}) copy-start(bf16[256,1024]{0,1:T(8,128)(2,1)S(1)} %get-tuple-element.10) | copy-start | bytes 1572868
  56.2 111.8 %copy-start.3 = (bf16[1024,1024]{1,0:T(8,128)(2,1)S(1)}, bf16[1024,1024]{1,0:T(8,128)(2,1)}, u32[]{:S(2)}) copy-start(bf16[1024,1024]{1,0:T(8,128)(2,1)} %all-gather.3.cloned.1.call-done) | copy-start | bytes 6291460
  56.2 108.1 %all-to-all-start = ((bf16[256,8,4,256]{3,1,0,2:T(8,128)(2,1)}), bf16[256,8,4,256]{3,1,0,2:T(8,128)(2,1)}, u32[]{:S(2)}, u32[]{:S(2)}) async-start(bf16[256,8,4,256]{3,1,0,2:T(8,128)(2,1)} %copy.18), calls=%async_computation | async-start | bytes 8388608 | tf_op jit(solution)/shard_map/all_to_all | solution.py:31
  164.3 100.2 %collective-permute-start.2 = (bf16[8192,512]{0,1:T(8,128)(2,1)}, bf16[8192,512]{0,1:T(8,128)(2,1)}, u32[]{:S(2)}, u32[]{:S(2)}) collective-permute-start(bf16[8192,512]{0,1:T(8,128)(2,1)} %all-gather.5.cloned.1.call-done), channel_id=1, source_target_pairs={{0,32},{32,0},{1,33},{33,1},{2,34},{34,2},{3,35},{35,3},{4,36},{36... | collective-permute-start | bytes 25165832 | tf_op jit(solution)/shard_map/ppermute | solution.py:52
  172.9 8.8 %copy-start.2 = (f32[1,256,1024]{2,1,0:T(8,128)S(1)}, f32[1,256,1024]{2,1,0:T(8,128)}, u32[]{:S(2)}) copy-start(f32[1,256,1024]{2,1,0:T(8,128)} %param.10) | copy-start | bytes 3145732
  175.2 69.2 %all-to-all-start.1 = ((bf16[8,256,1024]{1,2,0:T(8,128)(2,1)}), bf16[8,256,1024]{1,2,0:T(8,128)(2,1)}, u32[]{:S(2)}, u32[]{:S(2)}) async-start(bf16[8,256,1024]{1,2,0:T(8,128)(2,1)} %bitcast.47), calls=%async_computation.1 | async-start | bytes 8388608 | tf_op jit(solution)/shard_map/all_to_all | solution.py:64
  258.6 5.9 %copy-start.1 = (bf16[256,1024]{1,0:T(8,128)(2,1)S(1)}, bf16[256,1024]{1,0:T(8,128)(2,1)}, u32[]{:S(2)}) copy-start(bf16[256,1024]{1,0:T(8,128)(2,1)} %param.13) | copy-start | bytes 1572868
Sparse Core Ops, SparseCore 0:
  9.6 33.2 all-gather.2
  46.3 117.9 all-gather.4

commit v8 on v3

--- a/solution.py
+++ b/solution.py
@@ -14,9 +14,9 @@
 ADAM_STEP = 100
 
 GROUP = ("y_lo", "core")
-TEAMS = ("y_hi", "x")
-TEAM = "z"
-FSDP = TEAMS + (TEAM,)
+FSDP = ("y_hi", "x", "z")
+TEAMS = "x"
+TEAM = ("y_hi", "z")
 
 
 def per_device(anchor, pseudo_grads, outer_moment, adam_first, adam_second, inputs, key_cotangent):
@@ -28,8 +28,11 @@
     team = lax.axis_size(TEAM)
 
     cot_team = lax.all_gather(key_cotangent, TEAM, axis=0, tiled=True)
+    hi = lax.axis_size("y_hi")
+    lo = lax.axis_size("z")
+    cols = inputs.reshape(tok, hi, teams, lo, rows).transpose(0, 2, 1, 3, 4)
     inputs_part = lax.all_to_all(
-        inputs.reshape(tok, teams, team, rows), TEAM, split_axis=2, concat_axis=0, tiled=True
+        cols.reshape(tok, teams, team, rows), TEAM, split_axis=2, concat_axis=0, tiled=True
     ).reshape(team * tok, teams * rows)
 
     own = pseudo_grads[0]
@@ -55,10 +58,13 @@
     product = jnp.einsum(
         "tk,dk->td", cot_mine, mine, preferred_element_type=jnp.float32
     ) + jnp.einsum("tk,dk->td", cot_other, other, preferred_element_type=jnp.float32)
-    input_part = (product * scale).astype(jnp.bfloat16)
-    input_grad = lax.all_to_all(
-        input_part.reshape(team, tok, teams, 1, rows), TEAM, split_axis=0, concat_axis=3, tiled=True
-    ).reshape(tok, width)
+    input_part = (product * scale).astype(jnp.bfloat16).reshape(team, tok, teams, rows)
+    input_grad = (
+        lax.all_to_all(input_part, TEAM, split_axis=0, concat_axis=0, tiled=True)
+        .reshape(hi, lo, tok, teams, rows)
+        .transpose(2, 0, 3, 1, 4)
+        .reshape(tok, width)
+    )
 
     partial = (
         jnp.einsum("td,tk->dk", inputs_part, cot_team, preferred_element_type=jnp.float32) * scale

time: 203 us -> 265 us (1.31)
  waiting for transfers between devices: 66.7 us -> 103 us
  local copies, waits for them, and re-layouts: 35.8 us -> 56.3 us
    all_gather x1, waiting for transfers between devices: 0.01 us -> 30.7 us  [per_device(): cot_team = lax.all_gather(key_cotangent, TEAM, axis=0, tiled=True)]
    reshape x2 -> x4, local copies, waits for them, and re-layouts: 12.6 us -> 27.8 us  [the longest x2 15.2 us: per_device(): input_grad = lax.all_to_all(input_part, TEAM, split_axis=0, concat_axis=0...]
    all_to_all x1, waiting for transfers between devices: 46.6 us -> 57 us  [per_device(): lax.all_to_all(cols.reshape(tok, teams, team, rows), TEAM, split_axis=2,...]
    transpose x0 -> x1, local copies, waits for them, and re-layouts: none -> 7.36 us  [per_device(): cols = inputs.reshape(tok, hi, teams, lo, rows).transpose(0, 2, 1, 3, 4)]
    reduce_scatter x1, waiting for transfers between devices: 7.06 us -> 0.01 us  [per_device(): lax.psum_scatter(partial, TEAMS, scatter_dimension=0, tiled=True)]
    unnamed x17 -> x12, local copies, waits for them, and re-layouts: 14.9 us -> 12.5 us
  transfers between devices with their start and end apart: 7 -> 7, of which waited for: 3 -> 4; matrix products, arithmetic and copies ran while one was open for 28% -> 28% of each run, Pallas kernels for 0% -> 0%
where the time goes in v8:
time: 265 us; the launch traced here: 263 us
  waiting for transfers between devices  103 us (39%)
  local copies, waits for them, and re-layouts  56.3 us (21%)
  blocking collectives  54 us (20%)
  matrix products  18.3 us (7%)
  between operations  13.8 us (5%)
  starting transfers between devices  10 us (4%)
  other arithmetic  7.56 us (3%)
    all_to_all x1, waiting for transfers between devices, per_device(): lax.all_to_all(cols.reshape(tok, teams, team, rows), TEAM, split_axis=2,...  57 us
    all_to_all x1, blocking collectives, per_device(): lax.all_to_all(input_part, TEAM, split_axis=0, concat_axis=0, tiled=True)  54 us
    all_gather x1, waiting for transfers between devices, per_device(): cot_team = lax.all_gather(key_cotangent, TEAM, axis=0, tiled=True)  30.7 us
    reshape x2, local copies, waits for them, and re-layouts, per_device(): input_grad = lax.all_to_all(input_part, TEAM, split_axis=0, concat_axis=0...  15.2 us
    unnamed x12, local copies, waits for them, and re-layouts  12.5 us
    ppermute x1, waiting for transfers between devices, per_device(): lax.ppermute(own, 'y_lo', perm=[(0, 1), (1, 0)]).astype(jnp.float32)  12.3 us
    dot_general x1, matrix products, per_device(): jnp.einsum('td,tk->dk', inputs_part, cot_team, preferred_element_type=jnp...  9.42 us
    all_to_all x1, starting transfers between devices, per_device(): lax.all_to_all(cols.reshape(tok, teams, team, rows), TEAM, split_axis=2,...  7.89 us
  transfers between devices with their start and end apart: 7, of which 4 were waited for; matrix products, arithmetic and copies ran while one was open for 28% of the time, Pallas kernels for 0%

profile of v8, /device:TPU:6, one launch (start us, length us, event | category | flops | bytes accessed | tf_op | source)
XLA Modules:
  0.0 263.4 jit_solution(15752528127165234368)
XLA Ops:
  7.2 0.0 all-gather.5.cloned.1.call-start
  7.2 1.7 collective-permute-start
  8.9 12.3 %collective-permute-done = bf16[256,1024]{1,0:T(8,128)(2,1)S(1)} collective-permute-done((bf16[256,1024]{1,0:T(8,128)(2,1)}, bf16[256,1024]{1,0:T(8,128)(2,1)S(1)}, u32[]{:S(2)}, u32[]{:S(2)}) %collective-permute-start) | collective-permute-done | bytes 524320 | tf_op jit(solution)/shard_map/ppermute | solution.py:39
  21.2 1.2 convert_add_fusion
  22.4 0.1 collective-permute-start.1
  22.5 2.6 %collective-permute-done.1 = f32[256,1024]{1,0:T(8,128)S(1)} collective-permute-done((f32[256,1024]{1,0:T(8,128)S(1)}, f32[256,1024]{1,0:T(8,128)S(1)}, u32[]{:S(2)}, u32[]{:S(2)}) %collective-permute-start.1) | collective-permute-done | bytes 1048608 | tf_op jit(solution)/shard_map/ppermute | solution.py:42
  25.1 3.0 %subtract_convert_fusion.1 = (bf16[256,1024]{1,0:T(8,128)(2,1)S(1)}, f32[256,1024]{1,0:T(8,128)}) fusion(bf16[256,1024]{1,0:T(8,128)(2,1)} %param.7, f32[256,1024]{1,0:T(8,128)S(1)} %collective-permute-done.1, bf16[256,1024]{1,0:T(8,128)(2,1)S(1)} %collective-permute-done, bf16[1,256,1024]{2,1,0:T(8,128)(2,1)} %param.8, f32[256,1024]{1,0:T(8,128)} %param.9), kind=kLoop, calls=%fused_computation.11 | loop fusion | flops 3407872 | bytes 5242880 | tf_op jit(solution)/shard_map/convert_element_type | solution.py:47
  28.1 0.8 constant_dynamic-slice_fusion
  28.9 0.0 all-gather.5.cloned.1.call-update
  28.9 0.0 all-gather.3.cloned.1.call-start
  28.9 0.7 all-gather.3.cloned.1.call-update
  29.6 6.4 %copy.20 = bf16[256,8192]{0,1:T(8,128)(2,1)} copy(bf16[256,8192]{1,0:T(8,128)(2,1)} %param.12) | data formatting | bytes 8388608 | tf_op args[5]
  36.0 7.4 %copy.21 = bf16[256,4,2,4,256]{4,0,3,2,1:T(8,128)(2,1)} copy(bf16[256,4,2,4,256]{0,4,3,1,2:T(8,128)(2,1)} %bitcast.53) | data formatting | bytes 8388608 | tf_op jit(solution)/shard_map/transpose | solution.py:33
  43.4 4.7 %copy.22 = bf16[256,4,8,256]{3,0,1,2:T(8,128)(2,1)} copy(bf16[256,4,8,256]{3,0,2,1:T(8,128)(2,1)} %bitcast.49) | data formatting | bytes 8388608 | tf_op jit(solution)/shard_map/reshape | solution.py:35
  48.0 7.9 %all-to-all-start = ((bf16[256,4,8,256]{3,0,1,2:T(8,128)(2,1)}), bf16[256,4,8,256]{3,0,1,2:T(8,128)(2,1)}, u32[]{:S(2)}, u32[]{:S(2)}) async-start(bf16[256,4,8,256]{3,0,1,2:T(8,128)(2,1)} %copy.22), calls=%async_computation | async-start | bytes 8388608 | tf_op jit(solution)/shard_map/all_to_all | solution.py:34
  55.9 0.0 reduce-scatter.2.cloned.1.call-start
  56.0 0.0 all-gather.5.cloned.1.call-done
  56.0 0.3 collective-permute-start.2
  56.3 57.0 %all-to-all-done = bf16[256,4,8,256]{3,0,1,2:T(8,128)(2,1)} async-done(((bf16[256,4,8,256]{3,0,1,2:T(8,128)(2,1)}), bf16[256,4,8,256]{3,0,1,2:T(8,128)(2,1)}, u32[]{:S(2)}, u32[]{:S(2)}) %all-to-all-start) | async-done | bytes 4194336 | tf_op jit(solution)/shard_map/all_to_all | solution.py:34
  113.3 7.8 %copy.23 = bf16[8,256,4,1,256]{1,0,4,2,3:T(8,128)(2,1)} copy(bf16[8,256,4,1,256]{4,1,2,0,3:T(8,128)(2,1)} %bitcast.6) | data formatting | bytes 8388608 | tf_op jit(solution)/shard_map/all_to_all | solution.py:34
  121.1 6.2 %copy.25 = bf16[128,8,8,256]{3,1,2,0:T(8,128)(2,1)} copy(bf16[128,8,8,256]{3,2,1,0:T(8,128)(2,1)} %bitcast.50) | data formatting | bytes 8388608
  127.3 30.7 %all-gather.3.cloned.1.call-done = bf16[2048,1024]{1,0:T(8,128)(2,1)} async-done(((bf16[256,1024]{1,0:T(8,128)(2,1)}), bf16[2048,1024]{1,0:T(8,128)(2,1)}) %all-gather.3.cloned.1.call-update) | async-done | bytes 4194320 | tf_op jit(solution)/shard_map/all_gather | solution.py:30
  158.0 9.4 %multiply_convert_fusion.1 = bf16[1024,1024]{1,0:T(8,128)(2,1)} fusion(bf16[2048,1024]{0,1:T(8,128)(2,1)} %bitcast.54, bf16[2048,1024]{1,0:T(8,128)(2,1)} %all-gather.3.cloned.1.call-done), kind=kOutput, calls=%fused_computation.2 | convolution fusion | flops 4297064448 | bytes 10485760 | tf_op jit(solution)/shard_map/td,tk->dk/dot_general | solution.py:70
  167.4 0.0 reduce-scatter.2.cloned.1.call-update
  167.5 4.2 %fusion.1 = f32[2048,1024]{1,0:T(8,128)S(1)} fusion(bf16[1024,512]{1,0:T(8,128)(2,1)S(1)} %copy-done.4, bf16[2048,1024]{1,0:T(8,128)(2,1)} %all-gather.3.cloned.1.call-done, s32[]{:T(128)S(6)} %select_n.7), kind=kOutput, calls=%fused_computation.4 | convolution fusion | flops 2147483648 | bytes 11534340 | tf_op jit(solution)/shard_map/tk,dk->td/dot_general | solution.py:58
  171.7 0.0 collective-permute-done.2
  171.7 4.7 %multiply_convert_fusion = bf16[2048,1024]{1,0:T(8,128)(2,1)} fusion(f32[2048,1024]{1,0:T(8,128)S(1)} %fusion.1, bf16[1024,512]{1,0:T(8,128)(2,1)S(1)} %collective-permute-done.2, bf16[2048,1024]{1,0:T(8,128)(2,1)S(1)} %copy-done.3, s32[]{:T(128)S(6)} %select_n.8), kind=kOutput, calls=%fused_computation | convolution fusion | flops 2153775104 | bytes 15728644 | tf_op jit(solution)/shard_map/tk,dk->td/dot_general | solution.py:60
  176.4 7.9 %reshape.38 = bf16[8,256,4,256]{3,2,1,0:T(4,128)(2,1)} reshape(bf16[2048,1024]{1,0:T(8,128)(2,1)} %multiply_convert_fusion) | data formatting | bytes 8388608 | tf_op jit(solution)/shard_map/reshape | solution.py:61
  184.3 54.0 %all_to_all.20 = bf16[8,256,4,256]{3,2,1,0:T(4,128)(2,1)S(1)} all-to-all(bf16[8,256,4,256]{3,2,1,0:T(4,128)(2,1)} %reshape.38), channel_id=1, replica_groups=mesh['y_lo'=2,'core'=2,'y_hi'=2,'x'=4,'z'=4] {'y_hi','z'}, dimensions={0} | all-to-all | bytes 8388608 | tf_op jit(solution)/shard_map/all_to_all | solution.py:63
  238.3 7.4 %copy.27 = bf16[2,4,256,4,256]{4,1,3,0,2:T(4,128)(2,1)} copy(bf16[2,4,256,4,256]{4,3,2,1,0:T(4,128)(2,1)S(1)} %bitcast.51) | data formatting | bytes 8388608 | tf_op jit(solution)/shard_map/reshape | solution.py:64
  245.6 7.9 %reshape.40 = bf16[256,8192]{1,0:T(8,128)(2,1)} reshape(bf16[256,2,4,4,256]{4,3,2,1,0:T(4,128)(2,1)} %bitcast.52) | data formatting | bytes 8388608 | tf_op jit(solution)/shard_map/reshape | solution.py:66
  253.5 3.4 %fusion.6 = (f32[1,256,1024]{2,1,0:T(8,128)}, bf16[1,256,1024]{2,1,0:T(8,128)(2,1)}, f32[1,256,1024]{2,1,0:T(8,128)}) fusion(bf16[256,1024]{1,0:T(8,128)(2,1)} %reduce-scatter.2.cloned.1.call-done, f32[1,256,1024]{2,1,0:T(8,128)S(1)} %copy-done.1, f32[1,256,1024]{2,1,0:T(8,128)S(1)} %copy-done.2, bf16[256,1024]{1,0:T(8,128)(2,1)S(1)} %get-tuple-element.6), kind=kLoop, calls=%fused_computation.16 | loop fusion | flops 4456448 | bytes 5767168 | tf_op jit(solution)/shard_map/broadcast_in_dim | solution.py:87
  (11 shorter events, 0.0 us)
Async XLA Ops:
  7.2 48.8 %all-gather.5.cloned.1.call-start = ((), (), s32[]{:S(2)}) async-start(), calls=%async_computation.5 | async-start | bytes 1310720 | tf_op jit(solution)/shard_map/all_gather | solution.py:52
  7.2 14.0 %collective-permute-start = (bf16[256,1024]{1,0:T(8,128)(2,1)}, bf16[256,1024]{1,0:T(8,128)(2,1)S(1)}, u32[]{:S(2)}, u32[]{:S(2)}) collective-permute-start(bf16[256,1024]{1,0:T(8,128)(2,1)} %bitcast.55), channel_id=1, source_target_pairs={{0,64},{64,0},{1,65},{65,1},{2,66},{66,2},{3,67},{67,3},{4,68},{68... | collective-permute-start | bytes 1572872 | tf_op jit(solution)/shard_map/ppermute | solution.py:39
  22.4 2.7 %collective-permute-start.1 = (f32[256,1024]{1,0:T(8,128)S(1)}, f32[256,1024]{1,0:T(8,128)S(1)}, u32[]{:S(2)}, u32[]{:S(2)}) collective-permute-start(f32[256,1024]{1,0:T(8,128)S(1)} %convert_add_fusion), channel_id=1, source_target_pairs={{0,32},{32,0},{1,33},{33,1},{2,34},{34,2},{3,35},{35,3},{4,36},{36... | collective-permute-start | bytes 3145736 | tf_op jit(solution)/shard_map/ppermute | solution.py:42
  28.1 225.4 %copy-start = (bf16[256,1024]{1,0:T(8,128)(2,1)}, bf16[256,1024]{1,0:T(8,128)(2,1)S(1)}, u32[]{:S(2)}) copy-start(bf16[256,1024]{1,0:T(8,128)(2,1)S(1)} %get-tuple-element.6) | copy-start | bytes 1572868
  28.9 129.1 %all-gather.3.cloned.1.call-start = ((), (), s32[]{:S(2)}) async-start(), calls=%async_computation.3 | async-start | bytes 4718592 | tf_op jit(solution)/shard_map/all_gather | solution.py:30
  48.0 65.2 %all-to-all-start = ((bf16[256,4,8,256]{3,0,1,2:T(8,128)(2,1)}), bf16[256,4,8,256]{3,0,1,2:T(8,128)(2,1)}, u32[]{:S(2)}, u32[]{:S(2)}) async-start(bf16[256,4,8,256]{3,0,1,2:T(8,128)(2,1)} %copy.22), calls=%async_computation | async-start | bytes 8388608 | tf_op jit(solution)/shard_map/all_to_all | solution.py:34
  55.9 197.6 %reduce-scatter.2.cloned.1.call-start = ((), (), s32[]{:S(2)}) async-start(), calls=%async_computation.4 | async-start | bytes 2621440 | tf_op jit(solution)/shard_map/reduce_scatter | solution.py:72
  56.0 115.7 %collective-permute-start.2 = (bf16[1024,512]{1,0:T(8,128)(2,1)}, bf16[1024,512]{1,0:T(8,128)(2,1)S(1)}, u32[]{:S(2)}, u32[]{:S(2)}) collective-permute-start(bf16[1024,512]{1,0:T(8,128)(2,1)} %all-gather.5.cloned.1.call-done), channel_id=1, source_target_pairs={{0,32},{32,0},{1,33},{33,1},{2,34},{34,2},{3,35},{35,3},{4,36},{36... | collective-permute-start | bytes 3145736 | tf_op jit(solution)/shard_map/ppermute | solution.py:55
  158.0 9.4 %copy-start.4 = (bf16[1024,512]{1,0:T(8,128)(2,1)S(1)}, bf16[1024,512]{1,0:T(8,128)(2,1)}, u32[]{:S(2)}) copy-start(bf16[1024,512]{1,0:T(8,128)(2,1)} %all-gather.5.cloned.1.call-done) | copy-start | bytes 3145732
  167.5 4.3 %copy-start.3 = (bf16[2048,1024]{1,0:T(8,128)(2,1)S(1)}, bf16[2048,1024]{1,0:T(8,128)(2,1)}, u32[]{:S(2)}) copy-start(bf16[2048,1024]{1,0:T(8,128)(2,1)} %all-gather.3.cloned.1.call-done) | copy-start | bytes 12582916
  245.6 7.9 %copy-start.1 = (f32[1,256,1024]{2,1,0:T(8,128)S(1)}, f32[1,256,1024]{2,1,0:T(8,128)}, u32[]{:S(2)}) copy-start(f32[1,256,1024]{2,1,0:T(8,128)} %param.11) | copy-start | bytes 3145732
  245.6 7.9 %copy-start.2 = (f32[1,256,1024]{2,1,0:T(8,128)S(1)}, f32[1,256,1024]{2,1,0:T(8,128)}, u32[]{:S(2)}) copy-start(f32[1,256,1024]{2,1,0:T(8,128)} %param.10) | copy-start | bytes 3145732
Sparse Core Ops, SparseCore 0:
  29.0 25.2 all-gather.4
  56.6 101.3 all-gather.2
  167.6 25.5 reduce-scatter.1

commit v9 on v3

--- a/solution.py
+++ b/solution.py
@@ -63,7 +63,15 @@
     partial = (
         jnp.einsum("td,tk->dk", inputs_part, cot_team, preferred_element_type=jnp.float32) * scale
     ).astype(jnp.bfloat16)
-    grads = lax.psum_scatter(partial, TEAMS, scatter_dimension=0, tiled=True).astype(jnp.float32)
+    halves = partial.reshape(lax.axis_size("y_hi"), -1, kv)
+    y = lax.axis_index("y_hi")
+    kept = lax.dynamic_index_in_dim(halves, y, axis=0, keepdims=False)
+    given = lax.dynamic_index_in_dim(halves, 1 - y, axis=0, keepdims=False)
+    paired = (
+        kept.astype(jnp.float32)
+        + lax.ppermute(given, "y_hi", perm=[(0, 1), (1, 0)]).astype(jnp.float32)
+    ).astype(jnp.bfloat16)
+    grads = lax.psum_scatter(paired, "x", scatter_dimension=0, tiled=True).astype(jnp.float32)
 
     correct_one = 1.0 - BETA_ONE**ADAM_STEP
     correct_two = 1.0 - BETA_TWO**ADAM_STEP

time: 203 us -> 244 us (1.20)
  waiting for transfers between devices: 66.7 us -> 147 us
  blocking collectives: 52.3 us -> 0 us
  starting transfers between devices: 7.44 us -> 15.2 us
  local copies, waits for them, and re-layouts: 35.8 us -> 40.1 us
  other arithmetic: 8.23 us -> 11.1 us
    all_to_all x1 -> x0, blocking collectives: 52.3 us -> none  [per_device(): lax.all_to_all(input_part.reshape(team, tok, teams, 1, rows), TEAM, split...]
    ppermute x0 -> x1, waiting for transfers between devices: none -> 42.1 us  [per_device(): lax.ppermute(given, 'y_hi', perm=[(0, 1), (1, 0)]).astype(jnp.float32)]
    all_to_all x0 -> x1, waiting for transfers between devices: none -> 34.7 us  [per_device(): lax.all_to_all(input_part.reshape(team, tok, teams, 1, rows), TEAM, split...]
    ppermute x1, waiting for transfers between devices: 12.3 us -> 0.01 us  [per_device(): lax.ppermute(own, 'y_lo', perm=[(0, 1), (1, 0)]).astype(jnp.float32)]
    all_to_all x1, waiting for transfers between devices: 46.6 us -> 52.6 us  [per_device(): lax.all_to_all(inputs.reshape(tok, teams, team, rows), TEAM, split_axis=2...]
    all_to_all x0 -> x1, starting transfers between devices: none -> 5.01 us  [per_device(): lax.all_to_all(input_part.reshape(team, tok, teams, 1, rows), TEAM, split...]
    all_gather x1, waiting for transfers between devices: 0.02 us -> 3.94 us  [per_device(): lax.all_gather(lax.dynamic_slice_in_dim(new_anchor, core * half, half, ax...]
    convert_element_type x0 -> x1, other arithmetic: none -> 3.89 us  [per_device(): paired = (kept.astype(jnp.float32) + lax.ppermute(given, 'y_hi', perm=[(0...]
  transfers between devices with their start and end apart: 7 -> 9, of which waited for: 3 -> 6; matrix products, arithmetic and copies ran while one was open for 28% -> 21% of each run, Pallas kernels for 0% -> 0%
where the time goes in v9:
time: 244 us; the launch traced here: 243 us
  waiting for transfers between devices  147 us (60%)
  local copies, waits for them, and re-layouts  40.1 us (16%)
  matrix products  15.9 us (7%)
  starting transfers between devices  15.2 us (6%)
  between operations  13.8 us (6%)
  other arithmetic  11.1 us (5%)
    all_to_all x1, waiting for transfers between devices, per_device(): lax.all_to_all(inputs.reshape(tok, teams, team, rows), TEAM, split_axis=2...  52.6 us
    ppermute x1, waiting for transfers between devices, per_device(): lax.ppermute(given, 'y_hi', perm=[(0, 1), (1, 0)]).astype(jnp.float32)  42.1 us
    all_to_all x1, waiting for transfers between devices, per_device(): lax.all_to_all(input_part.reshape(team, tok, teams, 1, rows), TEAM, split...  34.7 us
    unnamed x19, local copies, waits for them, and re-layouts  17.8 us
    reshape x2, local copies, waits for them, and re-layouts, per_device(): inputs.reshape(tok, teams, team, rows)  12.5 us
    reduce_scatter x1, waiting for transfers between devices, per_device(): lax.psum_scatter(paired, 'x', scatter_dimension=0, tiled=True)  10.1 us
    all_to_all x1, local copies, waits for them, and re-layouts, per_device(): lax.all_to_all(input_part.reshape(team, tok, teams, 1, rows), TEAM, split...  7.51 us
    dot_general x1, matrix products, per_device(): jnp.einsum('td,tk->dk', inputs_part, cot_team, preferred_element_type=jnp...  7.46 us
  transfers between devices with their start and end apart: 9, of which 6 were waited for; matrix products, arithmetic and copies ran while one was open for 21% of the time, Pallas kernels for 0%

profile of v9, /device:TPU:6, one launch (start us, length us, event | category | flops | bytes accessed | tf_op | source)
XLA Modules:
  0.0 243.3 jit_solution(14457614594959980693)
XLA Ops:
  7.2 0.0 all-gather.3.cloned.1.call-start
  7.2 0.7 all-gather.3.cloned.1.call-update
  7.9 1.7 collective-permute-start
  9.6 7.8 %reshape.35 = bf16[256,8,4,256]{3,2,1,0:T(4,128)(2,1)} reshape(bf16[256,8192]{1,0:T(8,128)(2,1)} %param.12) | data formatting | bytes 8388608 | tf_op jit(solution)/shard_map/reshape | solution.py:32
  17.4 4.7 %copy.18 = bf16[256,8,4,256]{3,1,0,2:T(8,128)(2,1)} copy(bf16[256,8,4,256]{3,2,1,0:T(4,128)(2,1)} %reshape.35) | data formatting | bytes 8388608 | tf_op jit(solution)/shard_map/reshape | solution.py:32
  22.1 5.4 %all-to-all-start = ((bf16[256,8,4,256]{3,1,0,2:T(8,128)(2,1)}), bf16[256,8,4,256]{3,1,0,2:T(8,128)(2,1)}, u32[]{:S(2)}, u32[]{:S(2)}) async-start(bf16[256,8,4,256]{3,1,0,2:T(8,128)(2,1)} %copy.18), calls=%async_computation | async-start | bytes 8388608 | tf_op jit(solution)/shard_map/all_to_all | solution.py:31
  27.6 1.1 convert_add_fusion.1
  28.7 3.0 %collective-permute-done.1 = f32[256,1024]{1,0:T(8,128)} collective-permute-done((f32[256,1024]{1,0:T(8,128)}, f32[256,1024]{1,0:T(8,128)}, u32[]{:S(2)}, u32[]{:S(2)}) %collective-permute-start.1) | collective-permute-done | bytes 1048608 | tf_op jit(solution)/shard_map/ppermute | solution.py:39
  31.7 2.7 %subtract_convert_fusion.1 = (bf16[256,1024]{1,0:T(8,128)(2,1)S(1)}, f32[256,1024]{1,0:T(8,128)}) fusion(bf16[256,1024]{1,0:T(8,128)(2,1)S(1)} %copy-done.6, f32[256,1024]{1,0:T(8,128)} %collective-permute-done.1, bf16[256,1024]{1,0:T(8,128)(2,1)S(1)} %collective-permute-done, bf16[1,256,1024]{2,1,0:T(8,128)(2,1)S(1)} %copy-done.2, f32[256,1024]{1,0:T(8,128)S(1)} %copy-done.3), kind=kLoop, calls=%fused_computation.13 | loop fusion | flops 3407872 | bytes 5242880 | tf_op jit(solution)/shard_map/convert_element_type | solution.py:44
  34.4 0.8 constant_dynamic-slice_fusion
  35.1 0.0 all-gather.5.cloned.1.call-update
  35.2 0.0 reduce-scatter.2.cloned.1.call-start
  35.2 52.6 %all-to-all-done = bf16[256,8,4,256]{3,1,0,2:T(8,128)(2,1)} async-done(((bf16[256,8,4,256]{3,1,0,2:T(8,128)(2,1)}), bf16[256,8,4,256]{3,1,0,2:T(8,128)(2,1)}, u32[]{:S(2)}, u32[]{:S(2)}) %all-to-all-start) | async-done | bytes 4194336 | tf_op jit(solution)/shard_map/all_to_all | solution.py:31
  87.9 6.0 %copy.22 = bf16[128,8,8,256]{3,1,2,0:T(8,128)(2,1)} copy(bf16[128,8,8,256]{3,2,1,0:T(8,128)(2,1)} %bitcast.21) | data formatting | bytes 8388608
  93.8 7.5 %multiply_convert_fusion.1 = bf16[2048,1024]{1,0:T(8,128)(2,1)S(1)} fusion(bf16[1024,2048]{1,0:T(8,128)(2,1)} %bitcast.61, bf16[1024,1024]{1,0:T(8,128)(2,1)} %all-gather.3.cloned.1.call-done), kind=kOutput, calls=%fused_computation.1 | convolution fusion | flops 4299161600 | bytes 10485760 | tf_op jit(solution)/shard_map/td,tk->dk/dot_general | solution.py:64
  101.3 0.0 copy-start
  101.3 2.0 copy-done
  103.3 1.5 dynamic-slice_bitcast_fusion
  104.8 3.0 %collective-permute-start.2 = (bf16[1024,1024]{1,0:T(8,128)(2,1)}, bf16[1024,1024]{1,0:T(8,128)(2,1)S(1)}, u32[]{:S(2)}, u32[]{:S(2)}) collective-permute-start(bf16[1024,1024]{1,0:T(8,128)(2,1)} %dynamic-slice_bitcast_fusion), channel_id=1, source_target_pairs={{0,16},{16,0},{1,17},{17,1},{2,18},{18,2},{3,19},{19,3},{4,20},{20... | collective-permute-start | bytes 6291464 | tf_op jit(solution)/shard_map/ppermute | solution.py:72
  107.8 3.9 %all-gather.5.cloned.1.call-done = bf16[2048,512]{1,0:T(8,128)(2,1)} async-done(((bf16[256,512]{1,0:T(8,128)(2,1)}), bf16[2048,512]{1,0:T(8,128)(2,1)}) %all-gather.5.cloned.1.call-update) | async-done | bytes 2097168 | tf_op jit(solution)/shard_map/all_gather | solution.py:49
  111.8 42.1 %collective-permute-done.2 = bf16[1024,1024]{1,0:T(8,128)(2,1)S(1)} collective-permute-done((bf16[1024,1024]{1,0:T(8,128)(2,1)}, bf16[1024,1024]{1,0:T(8,128)(2,1)S(1)}, u32[]{:S(2)}, u32[]{:S(2)}) %collective-permute-start.2) | collective-permute-done | bytes 2097184 | tf_op jit(solution)/shard_map/ppermute | solution.py:72
  153.8 3.9 %fusion = bf16[1024,1024]{1,0:T(8,128)(2,1)} fusion(bf16[1024,1024]{1,0:T(8,128)(2,1)S(1)} %collective-permute-done.2, bf16[2,1024,1024]{2,1,0:T(8,128)(2,1)} %bitcast.60, s32[]{:T(128)S(6)} %select_n.14), kind=kLoop, calls=%fused_computation.3 | loop fusion | flops 4194304 | bytes 6291460 | tf_op jit(solution)/shard_map/convert_element_type | solution.py:73
  157.7 0.0 reduce-scatter.2.cloned.1.call-update
  157.8 4.4 %fusion.4 = f32[1024,2048]{1,0:T(8,128)S(1)} fusion(bf16[2048,512]{1,0:T(8,128)(2,1)} %all-gather.5.cloned.1.call-done, bf16[1024,1024]{1,0:T(8,128)(2,1)} %all-gather.3.cloned.1.call-done, s32[]{:T(128)S(6)} %select_n.16), kind=kOutput, calls=%fused_computation.10 | convolution fusion | flops 2147483648 | bytes 11534340 | tf_op jit(solution)/shard_map/tk,dk->td/dot_general | solution.py:55
  162.2 4.0 %multiply_convert_fusion = bf16[1024,2048]{1,0:T(8,128)(2,1)S(1)} fusion(f32[1024,2048]{1,0:T(8,128)S(1)} %fusion.4, bf16[2048,512]{1,0:T(8,128)(2,1)} %collective-permute-done.3, bf16[1024,1024]{1,0:T(8,128)(2,1)S(1)} %copy-done.7, s32[]{:T(128)S(6)} %select_n.17), kind=kOutput, calls=%fused_computation | convolution fusion | flops 2153775104 | bytes 15728644 | tf_op jit(solution)/shard_map/tk,dk->td/dot_general | solution.py:57
  166.2 3.5 %copy.23 = bf16[128,8,8,256]{3,2,1,0:T(8,128)(2,1)} copy(bf16[128,8,8,256]{3,1,2,0:T(8,128)(2,1)S(1)} %bitcast.62) | data formatting | bytes 8388608
  169.7 5.0 %all-to-all-start.1 = ((bf16[4,256,8,1,256]{4,2,1,3,0:T(8,128)(2,1)}), bf16[4,256,8,1,256]{4,2,1,3,0:T(8,128)(2,1)}, u32[]{:S(2)}, u32[]{:S(2)}) async-start(bf16[4,256,8,1,256]{4,2,1,3,0:T(8,128)(2,1)} %bitcast.57), calls=%async_computation.2 | async-start | bytes 8388608 | tf_op jit(solution)/shard_map/all_to_all | solution.py:59
  174.7 10.1 %reduce-scatter.2.cloned.1.call-done = bf16[256,1024]{1,0:T(8,128)(2,1)} async-done(((bf16[1024,1024]{1,0:T(8,128)(2,1)}), bf16[256,1024]{1,0:T(8,128)(2,1)}) %reduce-scatter.2.cloned.1.call-update) | async-done | bytes 524304 | tf_op jit(solution)/shard_map/reduce_scatter | solution.py:74
  184.8 3.4 %fusion.7 = (f32[1,256,1024]{2,1,0:T(8,128)}, bf16[1,256,1024]{2,1,0:T(8,128)(2,1)}, f32[1,256,1024]{2,1,0:T(8,128)}) fusion(bf16[256,1024]{1,0:T(8,128)(2,1)} %reduce-scatter.2.cloned.1.call-done, f32[1,256,1024]{2,1,0:T(8,128)S(1)} %copy-done.4, f32[1,256,1024]{2,1,0:T(8,128)S(1)} %copy-done.5, bf16[256,1024]{1,0:T(8,128)(2,1)S(1)} %get-tuple-element.12), kind=kLoop, calls=%fused_computation.18 | loop fusion | flops 4456448 | bytes 5767168 | tf_op jit(solution)/shard_map/broadcast_in_dim | solution.py:89
  188.2 34.7 %all-to-all-done.1 = bf16[4,256,8,1,256]{4,2,1,3,0:T(8,128)(2,1)} async-done(((bf16[4,256,8,1,256]{4,2,1,3,0:T(8,128)(2,1)}), bf16[4,256,8,1,256]{4,2,1,3,0:T(8,128)(2,1)}, u32[]{:S(2)}, u32[]{:S(2)}) %all-to-all-start.1) | async-done | bytes 4194336 | tf_op jit(solution)/shard_map/all_to_all | solution.py:59
  222.9 7.5 %copy.20 = bf16[4,256,8,1,256]{1,4,0,2,3:T(8,128)(2,1)} copy(bf16[4,256,8,1,256]{4,2,1,3,0:T(8,128)(2,1)} %all-to-all-done.1) | data formatting | bytes 8388608 | tf_op jit(solution)/shard_map/all_to_all | solution.py:59
  230.4 6.3 %copy.21 = bf16[256,8192]{1,0:T(8,128)(2,1)} copy(bf16[256,8192]{0,1:T(8,128)(2,1)} %bitcast.58) | data formatting | bytes 8388608
  (20 shorter events, 0.0 us)
Async XLA Ops:
  7.2 86.7 %all-gather.3.cloned.1.call-start = ((), (), s32[]{:S(2)}) async-start(), calls=%async_computation.3 | async-start | bytes 2621440 | tf_op jit(solution)/shard_map/all_gather | solution.py:30
  7.9 19.6 %collective-permute-start = (bf16[256,1024]{1,0:T(8,128)(2,1)}, bf16[256,1024]{1,0:T(8,128)(2,1)S(1)}, u32[]{:S(2)}, u32[]{:S(2)}) collective-permute-start(bf16[256,1024]{1,0:T(8,128)(2,1)} %bitcast.63), channel_id=1, source_target_pairs={{0,64},{64,0},{1,65},{65,1},{2,66},{66,2},{3,67},{67,3},{4,68},{68... | collective-permute-start | bytes 1572872 | tf_op jit(solution)/shard_map/ppermute | solution.py:36
  22.1 5.5 %copy-start.2 = (bf16[1,256,1024]{2,1,0:T(8,128)(2,1)S(1)}, bf16[1,256,1024]{2,1,0:T(8,128)(2,1)}, u32[]{:S(2)}) copy-start(bf16[1,256,1024]{2,1,0:T(8,128)(2,1)} %param.8) | copy-start | bytes 1572868
  22.1 9.6 %copy-start.3 = (f32[256,1024]{1,0:T(8,128)S(1)}, f32[256,1024]{1,0:T(8,128)}, u32[]{:S(2)}) copy-start(f32[256,1024]{1,0:T(8,128)} %param.9) | copy-start | bytes 3145732
  22.1 9.6 %copy-start.6 = (bf16[256,1024]{1,0:T(8,128)(2,1)S(1)}, bf16[256,1024]{1,0:T(8,128)(2,1)}, u32[]{:S(2)}) copy-start(bf16[256,1024]{1,0:T(8,128)(2,1)} %param.7) | copy-start | bytes 1572868
  22.1 65.8 %all-to-all-start = ((bf16[256,8,4,256]{3,1,0,2:T(8,128)(2,1)}), bf16[256,8,4,256]{3,1,0,2:T(8,128)(2,1)}, u32[]{:S(2)}, u32[]{:S(2)}) async-start(bf16[256,8,4,256]{3,1,0,2:T(8,128)(2,1)} %copy.18), calls=%async_computation | async-start | bytes 8388608 | tf_op jit(solution)/shard_map/all_to_all | solution.py:31
  27.5 84.2 %all-gather.5.cloned.1.call-start = ((), (), s32[]{:S(2)}) async-start(), calls=%async_computation.5 | async-start | bytes 2359296 | tf_op jit(solution)/shard_map/all_gather | solution.py:49
  28.7 3.0 %collective-permute-start.1 = (f32[256,1024]{1,0:T(8,128)}, f32[256,1024]{1,0:T(8,128)}, u32[]{:S(2)}, u32[]{:S(2)}) collective-permute-start(f32[256,1024]{1,0:T(8,128)} %convert_add_fusion.1), channel_id=1, source_target_pairs={{0,32},{32,0},{1,33},{33,1},{2,34},{34,2},{3,35},{35,3},{4,36},{36... | collective-permute-start | bytes 3145736 | tf_op jit(solution)/shard_map/ppermute | solution.py:39
  34.4 150.4 %copy-start.1 = (bf16[256,1024]{1,0:T(8,128)(2,1)}, bf16[256,1024]{1,0:T(8,128)(2,1)S(1)}, u32[]{:S(2)}) copy-start(bf16[256,1024]{1,0:T(8,128)(2,1)S(1)} %get-tuple-element.12) | copy-start | bytes 1572868
  35.2 149.6 %reduce-scatter.2.cloned.1.call-start = ((), (), s32[]{:S(2)}) async-start(), calls=%async_computation.4 | async-start | bytes 2621440 | tf_op jit(solution)/shard_map/reduce_scatter | solution.py:74
  101.3 2.0 copy-start
  104.8 49.0 %collective-permute-start.2 = (bf16[1024,1024]{1,0:T(8,128)(2,1)}, bf16[1024,1024]{1,0:T(8,128)(2,1)S(1)}, u32[]{:S(2)}, u32[]{:S(2)}) collective-permute-start(bf16[1024,1024]{1,0:T(8,128)(2,1)} %dynamic-slice_bitcast_fusion), channel_id=1, source_target_pairs={{0,16},{16,0},{1,17},{17,1},{2,18},{18,2},{3,19},{19,3},{4,20},{20... | collective-permute-start | bytes 6291464 | tf_op jit(solution)/shard_map/ppermute | solution.py:72
  111.8 50.5 %collective-permute-start.3 = (bf16[2048,512]{1,0:T(8,128)(2,1)}, bf16[2048,512]{1,0:T(8,128)(2,1)}, u32[]{:S(2)}, u32[]{:S(2)}) collective-permute-start(bf16[2048,512]{1,0:T(8,128)(2,1)} %all-gather.5.cloned.1.call-done), channel_id=1, source_target_pairs={{0,32},{32,0},{1,33},{33,1},{2,34},{34,2},{3,35},{35,3},{4,36},{36... | collective-permute-start | bytes 6291464 | tf_op jit(solution)/shard_map/ppermute | solution.py:52
  157.8 4.5 %copy-start.7 = (bf16[1024,1024]{1,0:T(8,128)(2,1)S(1)}, bf16[1024,1024]{1,0:T(8,128)(2,1)}, u32[]{:S(2)}) copy-start(bf16[1024,1024]{1,0:T(8,128)(2,1)} %all-gather.3.cloned.1.call-done) | copy-start | bytes 6291460
  169.7 15.1 %copy-start.4 = (f32[1,256,1024]{2,1,0:T(8,128)S(1)}, f32[1,256,1024]{2,1,0:T(8,128)}, u32[]{:S(2)}) copy-start(f32[1,256,1024]{2,1,0:T(8,128)} %param.11) | copy-start | bytes 3145732
  169.7 15.1 %copy-start.5 = (f32[1,256,1024]{2,1,0:T(8,128)S(1)}, f32[1,256,1024]{2,1,0:T(8,128)}, u32[]{:S(2)}) copy-start(f32[1,256,1024]{2,1,0:T(8,128)} %param.10) | copy-start | bytes 3145732
  169.7 53.2 %all-to-all-start.1 = ((bf16[4,256,8,1,256]{4,2,1,3,0:T(8,128)(2,1)}), bf16[4,256,8,1,256]{4,2,1,3,0:T(8,128)(2,1)}, u32[]{:S(2)}, u32[]{:S(2)}) async-start(bf16[4,256,8,1,256]{4,2,1,3,0:T(8,128)(2,1)} %bitcast.57), calls=%async_computation.2 | async-start | bytes 8388608 | tf_op jit(solution)/shard_map/all_to_all | solution.py:59
Sparse Core Ops, SparseCore 0:
  9.6 44.0 all-gather.2
  56.6 55.1 all-gather.4
  157.9 26.8 reduce-scatter.1

commit v10 on v3

--- a/solution.py
+++ b/solution.py
@@ -28,8 +28,10 @@
     team = lax.axis_size(TEAM)
 
     cot_team = lax.all_gather(key_cotangent, TEAM, axis=0, tiled=True)
+    hi = lax.axis_size("y_hi")
+    cols = inputs.reshape(tok, hi, teams // hi, team, rows).transpose(0, 2, 1, 3, 4)
     inputs_part = lax.all_to_all(
-        inputs.reshape(tok, teams, team, rows), TEAM, split_axis=2, concat_axis=0, tiled=True
+        cols.reshape(tok, teams, team, rows), TEAM, split_axis=2, concat_axis=0, tiled=True
     ).reshape(team * tok, teams * rows)
 
     own = pseudo_grads[0]
@@ -63,7 +65,13 @@
     partial = (
         jnp.einsum("td,tk->dk", inputs_part, cot_team, preferred_element_type=jnp.float32) * scale
     ).astype(jnp.bfloat16)
-    grads = lax.psum_scatter(partial, TEAMS, scatter_dimension=0, tiled=True).astype(jnp.float32)
+    halves = lax.psum_scatter(partial, "x", scatter_dimension=0, tiled=True).reshape(hi, rows, kv)
+    y = lax.axis_index("y_hi")
+    kept = lax.dynamic_index_in_dim(halves, y, axis=0, keepdims=False)
+    given = lax.dynamic_index_in_dim(halves, 1 - y, axis=0, keepdims=False)
+    grads = kept.astype(jnp.float32) + lax.ppermute(
+        given, "y_hi", perm=[(0, 1), (1, 0)]
+    ).astype(jnp.float32)
 
     correct_one = 1.0 - BETA_ONE**ADAM_STEP
     correct_two = 1.0 - BETA_TWO**ADAM_STEP

time: 203 us -> 208 us (1.025)
  blocking collectives: 52.3 us -> 0 us
  waiting for transfers between devices: 66.7 us -> 104 us
  local copies, waits for them, and re-layouts: 35.8 us -> 47.7 us
  starting transfers between devices: 7.44 us -> 15.2 us
    all_to_all x1 -> x0, blocking collectives: 52.3 us -> none  [per_device(): lax.all_to_all(input_part.reshape(team, tok, teams, 1, rows), TEAM, split...]
    reduce_scatter x1, waiting for transfers between devices: 7.06 us -> 26.4 us  [per_device(): lax.psum_scatter(partial, 'x', scatter_dimension=0, tiled=True)]
    all_to_all x1 -> x2, waiting for transfers between devices: 46.6 us -> 64.3 us  [the longest x1 46.6 us: per_device(): lax.all_to_all(cols.reshape(tok, teams, team, rows), TEAM, split_axis=2,...]
    reshape x2 -> x1, local copies, waits for them, and re-layouts: 12.6 us -> 4.68 us  [per_device(): cols.reshape(tok, teams, team, rows)]
    transpose x0 -> x1, local copies, waits for them, and re-layouts: none -> 7.26 us  [per_device(): inputs.reshape(tok, hi, teams // hi, team, rows).transpose(0, 2, 1, 3, 4)]
    unnamed x17 -> x18, local copies, waits for them, and re-layouts: 14.9 us -> 21.1 us
    all_to_all x1 -> x2, starting transfers between devices: 5.43 us -> 10.2 us  [the longest x1 5.37 us: per_device(): lax.all_to_all(cols.reshape(tok, teams, team, rows), TEAM, split_axis=2,...]
    all_to_all x0 -> x1, local copies, waits for them, and re-layouts: none -> 4.61 us  [per_device(): lax.all_to_all(cols.reshape(tok, teams, team, rows), TEAM, split_axis=2,...]
  transfers between devices with their start and end apart: 7 -> 9, of which waited for: 3 -> 4; matrix products, arithmetic and copies ran while one was open for 28% -> 33% of each run, Pallas kernels for 0% -> 0%
where the time goes in v10:
time: 208 us; the launch traced here: 206 us
  waiting for transfers between devices  104 us (50%)
  local copies, waits for them, and re-layouts  47.7 us (23%)
  matrix products  17.4 us (8%)
  starting transfers between devices  15.2 us (7%)
  between operations  13.8 us (7%)
  other arithmetic  8.31 us (4%)
    all_to_all x1, waiting for transfers between devices, per_device(): lax.all_to_all(cols.reshape(tok, teams, team, rows), TEAM, split_axis=2,...  46.6 us
    reduce_scatter x1, waiting for transfers between devices, per_device(): lax.psum_scatter(partial, 'x', scatter_dimension=0, tiled=True)  26.4 us
    unnamed x18, local copies, waits for them, and re-layouts  21.1 us
    all_to_all x1, waiting for transfers between devices, per_device(): lax.all_to_all(input_part.reshape(team, tok, teams, 1, rows), TEAM, split...  17.7 us
    ppermute x1, waiting for transfers between devices, per_device(): lax.ppermute(own, 'y_lo', perm=[(0, 1), (1, 0)]).astype(jnp.float32)  12.3 us
    dot_general x1, matrix products, per_device(): jnp.einsum('td,tk->dk', inputs_part, cot_team, preferred_element_type=jnp...  9.39 us
    all_to_all x1, local copies, waits for them, and re-layouts, per_device(): lax.all_to_all(input_part.reshape(team, tok, teams, 1, rows), TEAM, split...  7.5 us
    transpose x1, local copies, waits for them, and re-layouts, per_device(): inputs.reshape(tok, hi, teams // hi, team, rows).transpose(0, 2, 1, 3, 4)  7.26 us
  transfers between devices with their start and end apart: 9, of which 4 were waited for; matrix products, arithmetic and copies ran while one was open for 33% of the time, Pallas kernels for 0%

profile of v10, /device:TPU:6, one launch (start us, length us, event | category | flops | bytes accessed | tf_op | source)
XLA Modules:
  0.0 206.3 jit_solution(3908919612842516628)
XLA Ops:
  7.2 0.0 all-gather.3.cloned.1.call-start
  7.2 0.7 all-gather.3.cloned.1.call-update
  7.9 1.7 collective-permute-start
  9.6 12.3 %collective-permute-done = bf16[256,1024]{1,0:T(8,128)(2,1)S(1)} collective-permute-done((bf16[256,1024]{1,0:T(8,128)(2,1)}, bf16[256,1024]{1,0:T(8,128)(2,1)S(1)}, u32[]{:S(2)}, u32[]{:S(2)}) %collective-permute-start) | collective-permute-done | bytes 524320 | tf_op jit(solution)/shard_map/ppermute | solution.py:38
  21.9 2.2 %convert_add_fusion.1 = f32[256,1024]{1,0:T(8,128)} fusion(bf16[256,1024]{1,0:T(8,128)(2,1)S(1)} %collective-permute-done, bf16[1,256,1024]{2,1,0:T(8,128)(2,1)} %param.8), kind=kLoop, calls=%fused_computation.13 | loop fusion | flops 786432 | bytes 2097152 | tf_op jit(solution)/shard_map/add | solution.py:38
  24.1 6.4 %copy.25 = bf16[256,8192]{0,1:T(8,128)(2,1)} copy(bf16[256,8192]{1,0:T(8,128)(2,1)} %param.12) | data formatting | bytes 8388608 | tf_op args[5]
  30.4 7.3 %copy.26 = bf16[256,4,2,4,256]{4,0,3,2,1:T(8,128)(2,1)} copy(bf16[256,4,2,4,256]{0,4,3,1,2:T(8,128)(2,1)} %bitcast.70) | data formatting | bytes 8388608 | tf_op jit(solution)/shard_map/transpose | solution.py:32
  37.7 4.7 %copy.27 = bf16[256,8,4,256]{3,0,1,2:T(8,128)(2,1)} copy(bf16[256,8,4,256]{3,0,2,1:T(8,128)(2,1)} %bitcast.67) | data formatting | bytes 8388608 | tf_op jit(solution)/shard_map/reshape | solution.py:34
  42.4 5.4 %all-to-all-start = ((bf16[256,8,4,256]{3,0,1,2:T(8,128)(2,1)}), bf16[256,8,4,256]{3,0,1,2:T(8,128)(2,1)}, u32[]{:S(2)}, u32[]{:S(2)}) async-start(bf16[256,8,4,256]{3,0,1,2:T(8,128)(2,1)} %copy.27), calls=%async_computation | async-start | bytes 8388608 | tf_op jit(solution)/shard_map/all_to_all | solution.py:33
  47.8 2.7 %subtract_convert_fusion.1 = (bf16[256,1024]{1,0:T(8,128)(2,1)S(1)}, f32[256,1024]{1,0:T(8,128)}) fusion(bf16[256,1024]{1,0:T(8,128)(2,1)S(1)} %copy-done.5, f32[256,1024]{1,0:T(8,128)} %collective-permute-done.1, bf16[256,1024]{1,0:T(8,128)(2,1)S(1)} %collective-permute-done, bf16[1,256,1024]{2,1,0:T(8,128)(2,1)S(1)} %copy-done.1, f32[256,1024]{1,0:T(8,128)S(1)} %copy-done.2), kind=kLoop, calls=%fused_computation.10 | loop fusion | flops 3407872 | bytes 5242880 | tf_op jit(solution)/shard_map/convert_element_type | solution.py:46
  50.5 0.8 constant_dynamic-slice_fusion
  51.2 0.0 all-gather.5.cloned.1.call-update
  51.2 0.0 reduce-scatter.2.cloned.1.call-start
  51.3 46.6 %all-to-all-done = bf16[256,8,4,256]{3,0,1,2:T(8,128)(2,1)} async-done(((bf16[256,8,4,256]{3,0,1,2:T(8,128)(2,1)}), bf16[256,8,4,256]{3,0,1,2:T(8,128)(2,1)}, u32[]{:S(2)}, u32[]{:S(2)}) %all-to-all-start) | async-done | bytes 4194336 | tf_op jit(solution)/shard_map/all_to_all | solution.py:33
  97.9 4.6 %copy.28 = bf16[4,256,8,1,256]{4,2,1,0,3:T(8,128)(2,1)S(1)} copy(bf16[4,256,8,1,256]{4,1,2,0,3:T(8,128)(2,1)} %bitcast.6) | data formatting | bytes 8388608 | tf_op jit(solution)/shard_map/all_to_all | solution.py:33
  102.5 3.5 %copy.32 = bf16[128,8,8,256]{3,1,2,0:T(8,128)(2,1)} copy(bf16[128,8,8,256]{3,2,1,0:T(8,128)(2,1)S(1)} %bitcast.68) | data formatting | bytes 8388608
  106.0 9.4 %multiply_convert_fusion.1 = bf16[2048,1024]{1,0:T(8,128)(2,1)} fusion(bf16[1024,2048]{1,0:T(8,128)(2,1)} %bitcast.71, bf16[1024,1024]{1,0:T(8,128)(2,1)} %all-gather.3.cloned.1.call-done), kind=kOutput, calls=%fused_computation.1 | convolution fusion | flops 4299161600 | bytes 10485760 | tf_op jit(solution)/shard_map/td,tk->dk/dot_general | solution.py:66
  115.4 0.0 reduce-scatter.2.cloned.1.call-update
  115.4 0.0 all-gather.5.cloned.1.call-done
  115.4 0.3 collective-permute-start.3
  115.7 1.3 copy-done.6
  116.9 4.0 %fusion.2 = f32[1024,2048]{1,0:T(8,128)S(1)} fusion(bf16[2048,512]{1,0:T(8,128)(2,1)} %all-gather.5.cloned.1.call-done, bf16[1024,1024]{1,0:T(8,128)(2,1)S(1)} %copy-done.6, s32[]{:T(128)S(6)} %select_n.16), kind=kOutput, calls=%fused_computation.7 | convolution fusion | flops 2147483648 | bytes 11534340 | tf_op jit(solution)/shard_map/tk,dk->td/dot_general | solution.py:57
  120.9 4.0 %multiply_convert_fusion = bf16[1024,2048]{1,0:T(8,128)(2,1)S(1)} fusion(f32[1024,2048]{1,0:T(8,128)S(1)} %fusion.2, bf16[2048,512]{1,0:T(8,128)(2,1)} %collective-permute-done.3, bf16[1024,1024]{1,0:T(8,128)(2,1)S(1)} %copy-done.6, s32[]{:T(128)S(6)} %select_n.17), kind=kOutput, calls=%fused_computation | convolution fusion | flops 2153775104 | bytes 15728644 | tf_op jit(solution)/shard_map/tk,dk->td/dot_general | solution.py:59
  124.9 3.5 %copy.33 = bf16[128,8,8,256]{3,2,1,0:T(8,128)(2,1)} copy(bf16[128,8,8,256]{3,1,2,0:T(8,128)(2,1)S(1)} %bitcast.72) | data formatting | bytes 8388608
  128.4 4.9 %all-to-all-start.1 = ((bf16[4,256,8,1,256]{4,2,1,3,0:T(8,128)(2,1)}), bf16[4,256,8,1,256]{4,2,1,3,0:T(8,128)(2,1)}, u32[]{:S(2)}, u32[]{:S(2)}) async-start(bf16[4,256,8,1,256]{4,2,1,3,0:T(8,128)(2,1)} %bitcast.66), calls=%async_computation.2 | async-start | bytes 8388608 | tf_op jit(solution)/shard_map/all_to_all | solution.py:61
  133.3 26.4 %reduce-scatter.2.cloned.1.call-done = bf16[512,1024]{1,0:T(8,128)(2,1)} async-done(((bf16[2048,1024]{1,0:T(8,128)(2,1)}), bf16[512,1024]{1,0:T(8,128)(2,1)}) %reduce-scatter.2.cloned.1.call-update) | async-done | bytes 1048592 | tf_op jit(solution)/shard_map/reduce_scatter | solution.py:68
  159.7 1.9 dynamic-slice_bitcast_fusion
  161.5 3.0 %collective-permute-start.2 = (bf16[256,1024]{1,0:T(8,128)(2,1)}, bf16[256,1024]{1,0:T(8,128)(2,1)S(1)}, u32[]{:S(2)}, u32[]{:S(2)}) collective-permute-start(bf16[256,1024]{1,0:T(8,128)(2,1)} %dynamic-slice_bitcast_fusion), channel_id=1, source_target_pairs={{0,16},{16,0},{1,17},{17,1},{2,18},{18,2},{3,19},{19,3},{4,20},{20... | collective-permute-start | bytes 1572872 | tf_op jit(solution)/shard_map/ppermute | solution.py:72
  164.6 17.7 %all-to-all-done.1 = bf16[4,256,8,1,256]{4,2,1,3,0:T(8,128)(2,1)} async-done(((bf16[4,256,8,1,256]{4,2,1,3,0:T(8,128)(2,1)}), bf16[4,256,8,1,256]{4,2,1,3,0:T(8,128)(2,1)}, u32[]{:S(2)}, u32[]{:S(2)}) %all-to-all-start.1) | async-done | bytes 4194336 | tf_op jit(solution)/shard_map/all_to_all | solution.py:61
  182.3 7.5 %copy.30 = bf16[4,256,8,1,256]{1,4,0,2,3:T(8,128)(2,1)} copy(bf16[4,256,8,1,256]{4,2,1,3,0:T(8,128)(2,1)} %all-to-all-done.1) | data formatting | bytes 8388608 | tf_op jit(solution)/shard_map/all_to_all | solution.py:61
  189.8 6.5 %copy.31 = bf16[256,8192]{1,0:T(8,128)(2,1)} copy(bf16[256,8192]{0,1:T(8,128)(2,1)} %bitcast.69) | data formatting | bytes 8388608
  196.3 3.4 %fusion.6 = (f32[1,256,1024]{2,1,0:T(8,128)}, bf16[1,256,1024]{2,1,0:T(8,128)(2,1)}, f32[1,256,1024]{2,1,0:T(8,128)}) fusion(bf16[256,1024]{1,0:T(8,128)(2,1)S(1)} %collective-permute-done.2, bf16[2,256,1024]{2,1,0:T(8,128)(2,1)} %bitcast.75, s32[]{:T(128)S(6)} %select_n.14, f32[1,256,1024]{2,1,0:T(8,128)S(1)} %copy-done.3, ...), kind=kLoop, calls=%fused_computation.17 | loop fusion | flops 4980736 | bytes 6291460 | tf_op jit(solution)/shard_map/broadcast_in_dim | solution.py:89
  (19 shorter events, 0.0 us)
Async XLA Ops:
  7.2 98.8 %all-gather.3.cloned.1.call-start = ((), (), s32[]{:S(2)}) async-start(), calls=%async_computation.3 | async-start | bytes 2621440 | tf_op jit(solution)/shard_map/all_gather | solution.py:30
  7.9 14.0 %collective-permute-start = (bf16[256,1024]{1,0:T(8,128)(2,1)}, bf16[256,1024]{1,0:T(8,128)(2,1)S(1)}, u32[]{:S(2)}, u32[]{:S(2)}) collective-permute-start(bf16[256,1024]{1,0:T(8,128)(2,1)} %bitcast.73), channel_id=1, source_target_pairs={{0,64},{64,0},{1,65},{65,1},{2,66},{66,2},{3,67},{67,3},{4,68},{68... | collective-permute-start | bytes 1572872 | tf_op jit(solution)/shard_map/ppermute | solution.py:38
  24.0 23.7 %collective-permute-start.1 = (f32[256,1024]{1,0:T(8,128)}, f32[256,1024]{1,0:T(8,128)}, u32[]{:S(2)}, u32[]{:S(2)}) collective-permute-start(f32[256,1024]{1,0:T(8,128)} %convert_add_fusion.1), channel_id=1, source_target_pairs={{0,32},{32,0},{1,33},{33,1},{2,34},{34,2},{3,35},{35,3},{4,36},{36... | collective-permute-start | bytes 3145736 | tf_op jit(solution)/shard_map/ppermute | solution.py:41
  42.4 5.4 %copy-start.1 = (bf16[1,256,1024]{2,1,0:T(8,128)(2,1)S(1)}, bf16[1,256,1024]{2,1,0:T(8,128)(2,1)}, u32[]{:S(2)}) copy-start(bf16[1,256,1024]{2,1,0:T(8,128)(2,1)} %param.8) | copy-start | bytes 1572868
  42.4 5.4 %copy-start.2 = (f32[256,1024]{1,0:T(8,128)S(1)}, f32[256,1024]{1,0:T(8,128)}, u32[]{:S(2)}) copy-start(f32[256,1024]{1,0:T(8,128)} %param.9) | copy-start | bytes 3145732
  42.4 5.4 %copy-start.5 = (bf16[256,1024]{1,0:T(8,128)(2,1)S(1)}, bf16[256,1024]{1,0:T(8,128)(2,1)}, u32[]{:S(2)}) copy-start(bf16[256,1024]{1,0:T(8,128)(2,1)} %param.7) | copy-start | bytes 1572868
  42.4 55.5 %all-to-all-start = ((bf16[256,8,4,256]{3,0,1,2:T(8,128)(2,1)}), bf16[256,8,4,256]{3,0,1,2:T(8,128)(2,1)}, u32[]{:S(2)}, u32[]{:S(2)}) async-start(bf16[256,8,4,256]{3,0,1,2:T(8,128)(2,1)} %copy.27), calls=%async_computation | async-start | bytes 8388608 | tf_op jit(solution)/shard_map/all_to_all | solution.py:33
  47.7 67.7 %all-gather.5.cloned.1.call-start = ((), (), s32[]{:S(2)}) async-start(), calls=%async_computation.5 | async-start | bytes 2359296 | tf_op jit(solution)/shard_map/all_gather | solution.py:51
  50.4 145.8 %copy-start = (bf16[256,1024]{1,0:T(8,128)(2,1)}, bf16[256,1024]{1,0:T(8,128)(2,1)S(1)}, u32[]{:S(2)}) copy-start(bf16[256,1024]{1,0:T(8,128)(2,1)S(1)} %get-tuple-element.12) | copy-start | bytes 1572868
  51.2 108.4 %reduce-scatter.2.cloned.1.call-start = ((), (), s32[]{:S(2)}) async-start(), calls=%async_computation.4 | async-start | bytes 5242880 | tf_op jit(solution)/shard_map/reduce_scatter | solution.py:68
  115.3 1.6 copy-start.6
  115.4 5.5 %collective-permute-start.3 = (bf16[2048,512]{1,0:T(8,128)(2,1)}, bf16[2048,512]{1,0:T(8,128)(2,1)}, u32[]{:S(2)}, u32[]{:S(2)}) collective-permute-start(bf16[2048,512]{1,0:T(8,128)(2,1)} %all-gather.5.cloned.1.call-done), channel_id=1, source_target_pairs={{0,32},{32,0},{1,33},{33,1},{2,34},{34,2},{3,35},{35,3},{4,36},{36... | collective-permute-start | bytes 6291464 | tf_op jit(solution)/shard_map/ppermute | solution.py:54
  128.4 53.9 %all-to-all-start.1 = ((bf16[4,256,8,1,256]{4,2,1,3,0:T(8,128)(2,1)}), bf16[4,256,8,1,256]{4,2,1,3,0:T(8,128)(2,1)}, u32[]{:S(2)}, u32[]{:S(2)}) async-start(bf16[4,256,8,1,256]{4,2,1,3,0:T(8,128)(2,1)} %bitcast.66), calls=%async_computation.2 | async-start | bytes 8388608 | tf_op jit(solution)/shard_map/all_to_all | solution.py:61
  161.5 34.7 %collective-permute-start.2 = (bf16[256,1024]{1,0:T(8,128)(2,1)}, bf16[256,1024]{1,0:T(8,128)(2,1)S(1)}, u32[]{:S(2)}, u32[]{:S(2)}) collective-permute-start(bf16[256,1024]{1,0:T(8,128)(2,1)} %dynamic-slice_bitcast_fusion), channel_id=1, source_target_pairs={{0,16},{16,0},{1,17},{17,1},{2,18},{18,2},{3,19},{19,3},{4,20},{20... | collective-permute-start | bytes 1572872 | tf_op jit(solution)/shard_map/ppermute | solution.py:72
  189.8 6.5 %copy-start.3 = (f32[1,256,1024]{2,1,0:T(8,128)S(1)}, f32[1,256,1024]{2,1,0:T(8,128)}, u32[]{:S(2)}) copy-start(f32[1,256,1024]{2,1,0:T(8,128)} %param.11) | copy-start | bytes 3145732
  189.8 6.5 %copy-start.4 = (f32[1,256,1024]{2,1,0:T(8,128)S(1)}, f32[1,256,1024]{2,1,0:T(8,128)}, u32[]{:S(2)}) copy-start(f32[1,256,1024]{2,1,0:T(8,128)} %param.10) | copy-start | bytes 3145732
Sparse Core Ops, SparseCore 0:
  9.6 33.2 all-gather.2
  51.5 56.7 all-gather.4
  115.5 44.1 reduce-scatter.1

commit v11 on v10

--- a/solution.py
+++ b/solution.py
@@ -28,10 +28,8 @@
     team = lax.axis_size(TEAM)
 
     cot_team = lax.all_gather(key_cotangent, TEAM, axis=0, tiled=True)
-    hi = lax.axis_size("y_hi")
-    cols = inputs.reshape(tok, hi, teams // hi, team, rows).transpose(0, 2, 1, 3, 4)
     inputs_part = lax.all_to_all(
-        cols.reshape(tok, teams, team, rows), TEAM, split_axis=2, concat_axis=0, tiled=True
+        inputs.reshape(tok, teams, team, rows), TEAM, split_axis=2, concat_axis=0, tiled=True
     ).reshape(team * tok, teams * rows)
 
     own = pseudo_grads[0]
@@ -65,7 +63,10 @@
     partial = (
         jnp.einsum("td,tk->dk", inputs_part, cot_team, preferred_element_type=jnp.float32) * scale
     ).astype(jnp.bfloat16)
-    halves = lax.psum_scatter(partial, "x", scatter_dimension=0, tiled=True).reshape(hi, rows, kv)
+    hi = lax.axis_size("y_hi")
+    halves = lax.psum_scatter(
+        partial.reshape(hi, -1, kv), "x", scatter_dimension=1, tiled=True
+    )
     y = lax.axis_index("y_hi")
     kept = lax.dynamic_index_in_dim(halves, y, axis=0, keepdims=False)
     given = lax.dynamic_index_in_dim(halves, 1 - y, axis=0, keepdims=False)

time: 208 us -> 199 us (0.957)
  local copies, waits for them, and re-layouts: 47.7 us -> 39.7 us
    reshape x1 -> x2, local copies, waits for them, and re-layouts: 4.68 us -> 12.6 us  [per_device(): inputs.reshape(tok, teams, team, rows)]
    transpose x1 -> x0, local copies, waits for them, and re-layouts: 7.26 us -> none  [per_device(): inputs.reshape(tok, hi, teams // hi, team, rows).transpose(0, 2, 1, 3, 4)]
    all_to_all x1 -> x0, local copies, waits for them, and re-layouts: 4.61 us -> none  [per_device(): lax.all_to_all(cols.reshape(tok, teams, team, rows), TEAM, split_axis=2,...]
    unnamed x18 -> x17, local copies, waits for them, and re-layouts: 21.1 us -> 16.9 us
  transfers between devices with their start and end apart: 9 -> 9, of which waited for: 4 -> 4; matrix products, arithmetic and copies ran while one was open for 33% -> 31% of each run, Pallas kernels for 0% -> 0%
where the time goes in v11:
time: 199 us; the launch traced here: 198 us
  waiting for transfers between devices  104 us (52%)
  local copies, waits for them, and re-layouts  39.7 us (20%)
  matrix products  17.4 us (9%)
  starting transfers between devices  15.3 us (8%)
  between operations  13.8 us (7%)
  other arithmetic  8.31 us (4%)
    all_to_all x1, waiting for transfers between devices, per_device(): lax.all_to_all(inputs.reshape(tok, teams, team, rows), TEAM, split_axis=2...  46.6 us
    reduce_scatter x1, waiting for transfers between devices, per_device(): lax.psum_scatter(partial.reshape(hi, -1, kv), 'x', scatter_dimension=1, t...  26.4 us
    all_to_all x1, waiting for transfers between devices, per_device(): lax.all_to_all(input_part.reshape(team, tok, teams, 1, rows), TEAM, split...  17.7 us
    unnamed x17, local copies, waits for them, and re-layouts  16.9 us
    reshape x2, local copies, waits for them, and re-layouts, per_device(): inputs.reshape(tok, teams, team, rows)  12.6 us
    ppermute x1, waiting for transfers between devices, per_device(): lax.ppermute(own, 'y_lo', perm=[(0, 1), (1, 0)]).astype(jnp.float32)  12.3 us
    dot_general x1, matrix products, per_device(): jnp.einsum('td,tk->dk', inputs_part, cot_team, preferred_element_type=jnp...  9.4 us
    all_to_all x1, local copies, waits for them, and re-layouts, per_device(): lax.all_to_all(input_part.reshape(team, tok, teams, 1, rows), TEAM, split...  7.5 us
  transfers between devices with their start and end apart: 9, of which 4 were waited for; matrix products, arithmetic and copies ran while one was open for 31% of the time, Pallas kernels for 0%

profile of v11, /device:TPU:6, one launch (start us, length us, event | category | flops | bytes accessed | tf_op | source)
XLA Modules:
  0.0 198.3 jit_solution(12395049609483974589)
XLA Ops:
  7.2 0.0 all-gather.3.cloned.1.call-start
  7.2 0.7 all-gather.3.cloned.1.call-update
  7.9 1.7 collective-permute-start
  9.6 12.3 %collective-permute-done = bf16[256,1024]{1,0:T(8,128)(2,1)S(1)} collective-permute-done((bf16[256,1024]{1,0:T(8,128)(2,1)}, bf16[256,1024]{1,0:T(8,128)(2,1)S(1)}, u32[]{:S(2)}, u32[]{:S(2)}) %collective-permute-start) | collective-permute-done | bytes 524320 | tf_op jit(solution)/shard_map/ppermute | solution.py:36
  21.9 2.2 %convert_add_fusion.1 = f32[256,1024]{1,0:T(8,128)} fusion(bf16[256,1024]{1,0:T(8,128)(2,1)S(1)} %collective-permute-done, bf16[1,256,1024]{2,1,0:T(8,128)(2,1)} %param.8), kind=kLoop, calls=%fused_computation.13 | loop fusion | flops 786432 | bytes 2097152 | tf_op jit(solution)/shard_map/add | solution.py:36
  24.0 0.0 collective-permute-start.1
  24.1 7.8 %reshape.35 = bf16[256,8,4,256]{3,2,1,0:T(4,128)(2,1)} reshape(bf16[256,8192]{1,0:T(8,128)(2,1)} %param.12) | data formatting | bytes 8388608 | tf_op jit(solution)/shard_map/reshape | solution.py:32
  31.9 4.8 %copy.18 = bf16[256,8,4,256]{3,1,0,2:T(8,128)(2,1)} copy(bf16[256,8,4,256]{3,2,1,0:T(4,128)(2,1)} %reshape.35) | data formatting | bytes 8388608 | tf_op jit(solution)/shard_map/reshape | solution.py:32
  36.7 5.4 %all-to-all-start = ((bf16[256,8,4,256]{3,1,0,2:T(8,128)(2,1)}), bf16[256,8,4,256]{3,1,0,2:T(8,128)(2,1)}, u32[]{:S(2)}, u32[]{:S(2)}) async-start(bf16[256,8,4,256]{3,1,0,2:T(8,128)(2,1)} %copy.18), calls=%async_computation | async-start | bytes 8388608 | tf_op jit(solution)/shard_map/all_to_all | solution.py:31
  42.1 0.0 collective-permute-done.1
  42.1 2.7 %subtract_convert_fusion.1 = (bf16[256,1024]{1,0:T(8,128)(2,1)S(1)}, f32[256,1024]{1,0:T(8,128)}) fusion(bf16[256,1024]{1,0:T(8,128)(2,1)S(1)} %copy-done.5, f32[256,1024]{1,0:T(8,128)} %collective-permute-done.1, bf16[256,1024]{1,0:T(8,128)(2,1)S(1)} %collective-permute-done, bf16[1,256,1024]{2,1,0:T(8,128)(2,1)S(1)} %copy-done.1, f32[256,1024]{1,0:T(8,128)S(1)} %copy-done.2), kind=kLoop, calls=%fused_computation.10 | loop fusion | flops 3407872 | bytes 5242880 | tf_op jit(solution)/shard_map/convert_element_type | solution.py:44
  44.8 0.8 constant_dynamic-slice_fusion
  45.6 0.0 all-gather.5.cloned.1.call-update
  45.6 0.0 reduce-scatter.2.cloned.1.call-start
  45.7 46.6 %all-to-all-done = bf16[256,8,4,256]{3,1,0,2:T(8,128)(2,1)} async-done(((bf16[256,8,4,256]{3,1,0,2:T(8,128)(2,1)}), bf16[256,8,4,256]{3,1,0,2:T(8,128)(2,1)}, u32[]{:S(2)}, u32[]{:S(2)}) %all-to-all-start) | async-done | bytes 4194336 | tf_op jit(solution)/shard_map/all_to_all | solution.py:31
  92.3 5.7 %copy.22 = bf16[128,8,8,256]{3,1,2,0:T(8,128)(2,1)} copy(bf16[128,8,8,256]{3,2,1,0:T(8,128)(2,1)} %bitcast.21) | data formatting | bytes 8388608
  98.0 9.4 %multiply_convert_fusion.1 = bf16[2048,1024]{1,0:T(8,128)(2,1)} fusion(bf16[1024,2048]{1,0:T(8,128)(2,1)} %bitcast.65, bf16[1024,1024]{1,0:T(8,128)(2,1)} %all-gather.3.cloned.1.call-done), kind=kOutput, calls=%fused_computation.1 | convolution fusion | flops 4299161600 | bytes 10485760 | tf_op jit(solution)/shard_map/td,tk->dk/dot_general | solution.py:64
  107.4 0.0 reduce-scatter.2.cloned.1.call-update
  107.4 0.0 all-gather.5.cloned.1.call-done
  107.4 0.3 collective-permute-start.3
  107.7 1.3 copy-done.6
  109.0 4.0 %fusion.2 = f32[1024,2048]{1,0:T(8,128)S(1)} fusion(bf16[2048,512]{1,0:T(8,128)(2,1)} %all-gather.5.cloned.1.call-done, bf16[1024,1024]{1,0:T(8,128)(2,1)S(1)} %copy-done.6, s32[]{:T(128)S(6)} %select_n.16), kind=kOutput, calls=%fused_computation.7 | convolution fusion | flops 2147483648 | bytes 11534340 | tf_op jit(solution)/shard_map/tk,dk->td/dot_general | solution.py:55
  112.9 4.0 %multiply_convert_fusion = bf16[1024,2048]{1,0:T(8,128)(2,1)S(1)} fusion(f32[1024,2048]{1,0:T(8,128)S(1)} %fusion.2, bf16[2048,512]{1,0:T(8,128)(2,1)} %collective-permute-done.3, bf16[1024,1024]{1,0:T(8,128)(2,1)S(1)} %copy-done.6, s32[]{:T(128)S(6)} %select_n.17), kind=kOutput, calls=%fused_computation | convolution fusion | flops 2153775104 | bytes 15728644 | tf_op jit(solution)/shard_map/tk,dk->td/dot_general | solution.py:57
  116.9 3.5 %copy.23 = bf16[128,8,8,256]{3,2,1,0:T(8,128)(2,1)} copy(bf16[128,8,8,256]{3,1,2,0:T(8,128)(2,1)S(1)} %bitcast.66) | data formatting | bytes 8388608
  120.4 4.9 %all-to-all-start.1 = ((bf16[4,256,8,1,256]{4,2,1,3,0:T(8,128)(2,1)}), bf16[4,256,8,1,256]{4,2,1,3,0:T(8,128)(2,1)}, u32[]{:S(2)}, u32[]{:S(2)}) async-start(bf16[4,256,8,1,256]{4,2,1,3,0:T(8,128)(2,1)} %bitcast.62), calls=%async_computation.2 | async-start | bytes 8388608 | tf_op jit(solution)/shard_map/all_to_all | solution.py:59
  125.3 26.4 %reduce-scatter.2.cloned.1.call-done = bf16[2,256,1024]{2,1,0:T(8,128)(2,1)} async-done(((bf16[2,1024,1024]{2,1,0:T(8,128)(2,1)}), bf16[2,256,1024]{2,1,0:T(8,128)(2,1)}) %reduce-scatter.2.cloned.1.call-update) | async-done | bytes 1048592 | tf_op jit(solution)/shard_map/reduce_scatter | solution.py:67
  151.7 1.9 dynamic-slice_bitcast_fusion
  153.6 3.0 %collective-permute-start.2 = (bf16[256,1024]{1,0:T(8,128)(2,1)}, bf16[256,1024]{1,0:T(8,128)(2,1)S(1)}, u32[]{:S(2)}, u32[]{:S(2)}) collective-permute-start(bf16[256,1024]{1,0:T(8,128)(2,1)} %dynamic-slice_bitcast_fusion), channel_id=1, source_target_pairs={{0,16},{16,0},{1,17},{17,1},{2,18},{18,2},{3,19},{19,3},{4,20},{20... | collective-permute-start | bytes 1572872 | tf_op jit(solution)/shard_map/ppermute | solution.py:73
  156.6 17.7 %all-to-all-done.1 = bf16[4,256,8,1,256]{4,2,1,3,0:T(8,128)(2,1)} async-done(((bf16[4,256,8,1,256]{4,2,1,3,0:T(8,128)(2,1)}), bf16[4,256,8,1,256]{4,2,1,3,0:T(8,128)(2,1)}, u32[]{:S(2)}, u32[]{:S(2)}) %all-to-all-start.1) | async-done | bytes 4194336 | tf_op jit(solution)/shard_map/all_to_all | solution.py:59
  174.3 7.5 %copy.20 = bf16[4,256,8,1,256]{1,4,0,2,3:T(8,128)(2,1)} copy(bf16[4,256,8,1,256]{4,2,1,3,0:T(8,128)(2,1)} %all-to-all-done.1) | data formatting | bytes 8388608 | tf_op jit(solution)/shard_map/all_to_all | solution.py:59
  181.8 6.5 %copy.21 = bf16[256,8192]{1,0:T(8,128)(2,1)} copy(bf16[256,8192]{0,1:T(8,128)(2,1)} %bitcast.63) | data formatting | bytes 8388608
  188.3 3.4 %fusion.6 = (f32[1,256,1024]{2,1,0:T(8,128)}, bf16[1,256,1024]{2,1,0:T(8,128)(2,1)}, f32[1,256,1024]{2,1,0:T(8,128)}) fusion(bf16[256,1024]{1,0:T(8,128)(2,1)S(1)} %collective-permute-done.2, bf16[2,256,1024]{2,1,0:T(8,128)(2,1)} %reduce-scatter.2.cloned.1.call-done, s32[]{:T(128)S(6)} %select_n.14, f32[1,256,1024]{2,1,0:T(8,128)S(1)} %copy-done.3, ...), kind=kLoop, calls=%fused_computation.17 | loop fusion | flops 4980736 | bytes 6291460 | tf_op jit(solution)/shard_map/broadcast_in_dim | solution.py:90
  (17 shorter events, 0.0 us)
Async XLA Ops:
  7.2 90.8 %all-gather.3.cloned.1.call-start = ((), (), s32[]{:S(2)}) async-start(), calls=%async_computation.3 | async-start | bytes 2621440 | tf_op jit(solution)/shard_map/all_gather | solution.py:30
  7.9 14.0 %collective-permute-start = (bf16[256,1024]{1,0:T(8,128)(2,1)}, bf16[256,1024]{1,0:T(8,128)(2,1)S(1)}, u32[]{:S(2)}, u32[]{:S(2)}) collective-permute-start(bf16[256,1024]{1,0:T(8,128)(2,1)} %bitcast.67), channel_id=1, source_target_pairs={{0,64},{64,0},{1,65},{65,1},{2,66},{66,2},{3,67},{67,3},{4,68},{68... | collective-permute-start | bytes 1572872 | tf_op jit(solution)/shard_map/ppermute | solution.py:36
  24.0 18.1 %collective-permute-start.1 = (f32[256,1024]{1,0:T(8,128)}, f32[256,1024]{1,0:T(8,128)}, u32[]{:S(2)}, u32[]{:S(2)}) collective-permute-start(f32[256,1024]{1,0:T(8,128)} %convert_add_fusion.1), channel_id=1, source_target_pairs={{0,32},{32,0},{1,33},{33,1},{2,34},{34,2},{3,35},{35,3},{4,36},{36... | collective-permute-start | bytes 3145736 | tf_op jit(solution)/shard_map/ppermute | solution.py:39
  36.7 5.5 %copy-start.1 = (bf16[1,256,1024]{2,1,0:T(8,128)(2,1)S(1)}, bf16[1,256,1024]{2,1,0:T(8,128)(2,1)}, u32[]{:S(2)}) copy-start(bf16[1,256,1024]{2,1,0:T(8,128)(2,1)} %param.8) | copy-start | bytes 1572868
  36.7 5.5 %copy-start.2 = (f32[256,1024]{1,0:T(8,128)S(1)}, f32[256,1024]{1,0:T(8,128)}, u32[]{:S(2)}) copy-start(f32[256,1024]{1,0:T(8,128)} %param.9) | copy-start | bytes 3145732
  36.7 5.5 %copy-start.5 = (bf16[256,1024]{1,0:T(8,128)(2,1)S(1)}, bf16[256,1024]{1,0:T(8,128)(2,1)}, u32[]{:S(2)}) copy-start(bf16[256,1024]{1,0:T(8,128)(2,1)} %param.7) | copy-start | bytes 1572868
  36.7 55.6 %all-to-all-start = ((bf16[256,8,4,256]{3,1,0,2:T(8,128)(2,1)}), bf16[256,8,4,256]{3,1,0,2:T(8,128)(2,1)}, u32[]{:S(2)}, u32[]{:S(2)}) async-start(bf16[256,8,4,256]{3,1,0,2:T(8,128)(2,1)} %copy.18), calls=%async_computation | async-start | bytes 8388608 | tf_op jit(solution)/shard_map/all_to_all | solution.py:31
  42.1 65.3 %all-gather.5.cloned.1.call-start = ((), (), s32[]{:S(2)}) async-start(), calls=%async_computation.5 | async-start | bytes 2359296 | tf_op jit(solution)/shard_map/all_gather | solution.py:49
  44.8 143.5 %copy-start = (bf16[256,1024]{1,0:T(8,128)(2,1)}, bf16[256,1024]{1,0:T(8,128)(2,1)S(1)}, u32[]{:S(2)}) copy-start(bf16[256,1024]{1,0:T(8,128)(2,1)S(1)} %get-tuple-element.12) | copy-start | bytes 1572868
  45.6 106.1 %reduce-scatter.2.cloned.1.call-start = ((), (), s32[]{:S(2)}) async-start(), calls=%async_computation.4 | async-start | bytes 5242880 | tf_op jit(solution)/shard_map/reduce_scatter | solution.py:67
  107.4 1.6 copy-start.6
  107.4 5.5 %collective-permute-start.3 = (bf16[2048,512]{1,0:T(8,128)(2,1)}, bf16[2048,512]{1,0:T(8,128)(2,1)}, u32[]{:S(2)}, u32[]{:S(2)}) collective-permute-start(bf16[2048,512]{1,0:T(8,128)(2,1)} %all-gather.5.cloned.1.call-done), channel_id=1, source_target_pairs={{0,32},{32,0},{1,33},{33,1},{2,34},{34,2},{3,35},{35,3},{4,36},{36... | collective-permute-start | bytes 6291464 | tf_op jit(solution)/shard_map/ppermute | solution.py:52
  120.4 53.9 %all-to-all-start.1 = ((bf16[4,256,8,1,256]{4,2,1,3,0:T(8,128)(2,1)}), bf16[4,256,8,1,256]{4,2,1,3,0:T(8,128)(2,1)}, u32[]{:S(2)}, u32[]{:S(2)}) async-start(bf16[4,256,8,1,256]{4,2,1,3,0:T(8,128)(2,1)} %bitcast.62), calls=%async_computation.2 | async-start | bytes 8388608 | tf_op jit(solution)/shard_map/all_to_all | solution.py:59
  153.6 34.7 %collective-permute-start.2 = (bf16[256,1024]{1,0:T(8,128)(2,1)}, bf16[256,1024]{1,0:T(8,128)(2,1)S(1)}, u32[]{:S(2)}, u32[]{:S(2)}) collective-permute-start(bf16[256,1024]{1,0:T(8,128)(2,1)} %dynamic-slice_bitcast_fusion), channel_id=1, source_target_pairs={{0,16},{16,0},{1,17},{17,1},{2,18},{18,2},{3,19},{19,3},{4,20},{20... | collective-permute-start | bytes 1572872 | tf_op jit(solution)/shard_map/ppermute | solution.py:73
  181.8 6.5 %copy-start.3 = (f32[1,256,1024]{2,1,0:T(8,128)S(1)}, f32[1,256,1024]{2,1,0:T(8,128)}, u32[]{:S(2)}) copy-start(f32[1,256,1024]{2,1,0:T(8,128)} %param.11) | copy-start | bytes 3145732
  181.8 6.5 %copy-start.4 = (f32[1,256,1024]{2,1,0:T(8,128)S(1)}, f32[1,256,1024]{2,1,0:T(8,128)}, u32[]{:S(2)}) copy-start(f32[1,256,1024]{2,1,0:T(8,128)} %param.10) | copy-start | bytes 3145732
Sparse Core Ops, SparseCore 0:
  9.6 33.2 all-gather.2
  45.9 56.6 all-gather.4
  107.5 44.1 reduce-scatter.1

commit v12 on v11

--- a/solution.py
+++ b/solution.py
@@ -46,9 +46,12 @@
 
     half = kv // 2
     core = lax.axis_index("core")
-    mine = lax.all_gather(
-        lax.dynamic_slice_in_dim(new_anchor, core * half, half, axis=1), TEAMS, axis=0, tiled=True
+    near = lax.all_gather(
+        lax.dynamic_slice_in_dim(new_anchor, core * half, half, axis=1), "x", axis=0, tiled=True
     )
+    far = lax.ppermute(near, "y_hi", perm=[(0, 1), (1, 0)])
+    low = lax.axis_index("y_hi") == 0
+    mine = jnp.concatenate([jnp.where(low, near, far), jnp.where(low, far, near)], axis=0)
     other = lax.ppermute(mine, "core", perm=[(0, 1), (1, 0)])
     cot_mine = lax.dynamic_slice_in_dim(cot_team, core * half, half, axis=1)
     cot_other = lax.dynamic_slice_in_dim(cot_team, (1 - core) * half, half, axis=1)

time: 199 us -> 227 us (1.14)
  waiting for transfers between devices: 104 us -> 130 us
  starting transfers between devices: 15.3 us -> 18.3 us
    all_to_all x1, waiting for transfers between devices: 17.7 us -> 44.6 us  [per_device(): lax.all_to_all(input_part.reshape(team, tok, teams, 1, rows), TEAM, split...]
    reduce_scatter x1, waiting for transfers between devices: 26.4 us -> 0.02 us  [per_device(): lax.psum_scatter(partial.reshape(hi, -1, kv), 'x', scatter_dimension=1, t...]
    ppermute x0 -> x1, waiting for transfers between devices: none -> 23.7 us  [per_device(): far = lax.ppermute(near, 'y_hi', perm=[(0, 1), (1, 0)])]
    all_to_all x1, waiting for transfers between devices: 46.6 us -> 41.8 us  [per_device(): lax.all_to_all(inputs.reshape(tok, teams, team, rows), TEAM, split_axis=2...]
    ppermute x1, waiting for transfers between devices: 0.01 us -> 4.5 us  [per_device(): other = lax.ppermute(mine, 'core', perm=[(0, 1), (1, 0)])]
    ppermute x0 -> x1, starting transfers between devices: none -> 3.09 us  [per_device(): far = lax.ppermute(near, 'y_hi', perm=[(0, 1), (1, 0)])]
    ppermute x1, waiting for transfers between devices: 0.01 us -> 2.77 us  [per_device(): total = pair + lax.ppermute(pair, 'core', perm=[(0, 1), (1, 0)])]
    unnamed x17 -> x15, local copies, waits for them, and re-layouts: 16.9 us -> 15.7 us
  transfers between devices with their start and end apart: 9 -> 10, of which waited for: 4 -> 6; matrix products, arithmetic and copies ran while one was open for 31% -> 27% of each run, Pallas kernels for 0% -> 0%
where the time goes in v12:
time: 227 us; the launch traced here: 226 us
  waiting for transfers between devices  130 us (57%)
  local copies, waits for them, and re-layouts  38.3 us (17%)
  starting transfers between devices  18.3 us (8%)
  matrix products  16.1 us (7%)
  between operations  13.8 us (6%)
  other arithmetic  9.58 us (4%)
    all_to_all x1, waiting for transfers between devices, per_device(): lax.all_to_all(input_part.reshape(team, tok, teams, 1, rows), TEAM, split...  44.6 us
    all_to_all x1, waiting for transfers between devices, per_device(): lax.all_to_all(inputs.reshape(tok, teams, team, rows), TEAM, split_axis=2...  41.8 us
    ppermute x1, waiting for transfers between devices, per_device(): far = lax.ppermute(near, 'y_hi', perm=[(0, 1), (1, 0)])  23.7 us
    unnamed x15, local copies, waits for them, and re-layouts  15.7 us
    reshape x2, local copies, waits for them, and re-layouts, per_device(): inputs.reshape(tok, teams, team, rows)  12.5 us
    ppermute x1, waiting for transfers between devices, per_device(): lax.ppermute(own, 'y_lo', perm=[(0, 1), (1, 0)]).astype(jnp.float32)  11.8 us
    dot_general x1, matrix products, per_device(): jnp.einsum('td,tk->dk', inputs_part, cot_team, preferred_element_type=jnp...  9.4 us
    all_to_all x1, local copies, waits for them, and re-layouts, per_device(): lax.all_to_all(input_part.reshape(team, tok, teams, 1, rows), TEAM, split...  7.5 us
  transfers between devices with their start and end apart: 10, of which 6 were waited for; matrix products, arithmetic and copies ran while one was open for 27% of the time, Pallas kernels for 0%

profile of v12, /device:TPU:6, one launch (start us, length us, event | category | flops | bytes accessed | tf_op | source)
XLA Modules:
  0.0 226.0 jit_solution(7246237461669482529)
XLA Ops:
  7.2 0.0 all-gather.3.cloned.1.call-start
  7.2 0.7 all-gather.3.cloned.1.call-update
  7.9 7.8 %reshape.35 = bf16[256,8,4,256]{3,2,1,0:T(4,128)(2,1)} reshape(bf16[256,8192]{1,0:T(8,128)(2,1)} %param.12) | data formatting | bytes 8388608 | tf_op jit(solution)/shard_map/reshape | solution.py:32
  15.7 4.7 %copy.18 = bf16[256,8,4,256]{3,1,0,2:T(8,128)(2,1)} copy(bf16[256,8,4,256]{3,2,1,0:T(4,128)(2,1)} %reshape.35) | data formatting | bytes 8388608 | tf_op jit(solution)/shard_map/reshape | solution.py:32
  20.4 5.4 %all-to-all-start = ((bf16[256,8,4,256]{3,1,0,2:T(8,128)(2,1)}), bf16[256,8,4,256]{3,1,0,2:T(8,128)(2,1)}, u32[]{:S(2)}, u32[]{:S(2)}) async-start(bf16[256,8,4,256]{3,1,0,2:T(8,128)(2,1)} %copy.18), calls=%async_computation | async-start | bytes 8388608 | tf_op jit(solution)/shard_map/all_to_all | solution.py:31
  25.9 1.7 collective-permute-start
  27.5 11.8 %collective-permute-done = bf16[256,1024]{1,0:T(8,128)(2,1)S(1)} collective-permute-done((bf16[256,1024]{1,0:T(8,128)(2,1)S(1)}, bf16[256,1024]{1,0:T(8,128)(2,1)S(1)}, u32[]{:S(2)}, u32[]{:S(2)}) %collective-permute-start) | collective-permute-done | bytes 524320 | tf_op jit(solution)/shard_map/ppermute | solution.py:36
  39.3 0.2 convert_add_fusion.1
  39.5 0.1 collective-permute-start.1
  39.6 2.8 %collective-permute-done.1 = f32[256,1024]{1,0:T(8,128)} collective-permute-done((f32[256,1024]{1,0:T(8,128)S(1)}, f32[256,1024]{1,0:T(8,128)}, u32[]{:S(2)}, u32[]{:S(2)}) %collective-permute-start.1) | collective-permute-done | bytes 1048608 | tf_op jit(solution)/shard_map/ppermute | solution.py:39
  42.4 2.8 %subtract_convert_fusion.1 = (bf16[256,1024]{1,0:T(8,128)(2,1)S(1)}, f32[256,1024]{1,0:T(8,128)}) fusion(bf16[256,1024]{1,0:T(8,128)(2,1)} %param.7, f32[256,1024]{1,0:T(8,128)} %collective-permute-done.1, bf16[256,1024]{1,0:T(8,128)(2,1)S(1)} %collective-permute-done, bf16[1,256,1024]{2,1,0:T(8,128)(2,1)S(1)} %copy-done.1, f32[256,1024]{1,0:T(8,128)S(1)} %copy-done.2), kind=kLoop, calls=%fused_computation.11 | loop fusion | flops 3407872 | bytes 5242880 | tf_op jit(solution)/shard_map/convert_element_type | solution.py:44
  45.2 0.8 constant_dynamic-slice_fusion
  46.0 0.0 reduce-scatter.2.cloned.1.call-start
  46.1 41.8 %all-to-all-done = bf16[256,8,4,256]{3,1,0,2:T(8,128)(2,1)} async-done(((bf16[256,8,4,256]{3,1,0,2:T(8,128)(2,1)}), bf16[256,8,4,256]{3,1,0,2:T(8,128)(2,1)}, u32[]{:S(2)}, u32[]{:S(2)}) %all-to-all-start) | async-done | bytes 4194336 | tf_op jit(solution)/shard_map/all_to_all | solution.py:31
  87.9 5.7 %copy.22 = bf16[128,8,8,256]{3,1,2,0:T(8,128)(2,1)} copy(bf16[128,8,8,256]{3,2,1,0:T(8,128)(2,1)} %bitcast.21) | data formatting | bytes 8388608
  93.6 9.4 %multiply_convert_fusion.1 = bf16[2048,1024]{1,0:T(8,128)(2,1)} fusion(bf16[1024,2048]{1,0:T(8,128)(2,1)} %bitcast.65, bf16[1024,1024]{1,0:T(8,128)(2,1)} %all-gather.3.cloned.1.call-done), kind=kOutput, calls=%fused_computation.1 | convolution fusion | flops 4299161600 | bytes 10485760 | tf_op jit(solution)/shard_map/td,tk->dk/dot_general | solution.py:67
  103.0 0.0 all-gather.5.cloned.1.call-done
  103.0 3.1 %collective-permute-start.3 = (bf16[1024,512]{1,0:T(8,128)(2,1)}, bf16[1024,512]{1,0:T(8,128)(2,1)}, u32[]{:S(2)}, u32[]{:S(2)}) collective-permute-start(bf16[1024,512]{1,0:T(8,128)(2,1)} %all-gather.5.cloned.1.call-done), channel_id=1, source_target_pairs={{0,16},{16,0},{1,17},{17,1},{2,18},{18,2},{3,19},{19,3},{4,20},{20... | collective-permute-start | bytes 3145736 | tf_op jit(solution)/shard_map/ppermute | solution.py:52
  106.1 23.7 %collective-permute-done.3 = bf16[1024,512]{1,0:T(8,128)(2,1)} collective-permute-done((bf16[1024,512]{1,0:T(8,128)(2,1)}, bf16[1024,512]{1,0:T(8,128)(2,1)}, u32[]{:S(2)}, u32[]{:S(2)}) %collective-permute-start.3) | collective-permute-done | bytes 1048608 | tf_op jit(solution)/shard_map/ppermute | solution.py:52
  129.8 1.7 broadcast_select_fusion.1
  131.5 1.5 pad_maximum_fusion
  132.9 4.5 %collective-permute-done.4 = bf16[2048,512]{1,0:T(8,128)(2,1)} collective-permute-done((bf16[2048,512]{1,0:T(8,128)(2,1)}, bf16[2048,512]{1,0:T(8,128)(2,1)}, u32[]{:S(2)}, u32[]{:S(2)}) %collective-permute-start.4) | collective-permute-done | bytes 2097184 | tf_op jit(solution)/shard_map/ppermute | solution.py:55
  137.4 4.3 %fusion.1 = f32[1024,2048]{1,0:T(8,128)S(1)} fusion(bf16[2048,512]{1,0:T(8,128)(2,1)} %collective-permute-done.4, bf16[1024,1024]{1,0:T(8,128)(2,1)} %all-gather.3.cloned.1.call-done, s32[]{:T(128)S(6)} %select_n.32), kind=kOutput, calls=%fused_computation.7 | convolution fusion | flops 2147483648 | bytes 11534340 | tf_op jit(solution)/shard_map/tk,dk->td/dot_general | solution.py:60
  141.7 2.4 %multiply_convert_fusion = bf16[1024,2048]{1,0:T(8,128)(2,1)S(1)} fusion(f32[1024,2048]{1,0:T(8,128)S(1)} %fusion.1, bf16[1024,1024]{1,0:T(8,128)(2,1)S(1)} %copy-done.5, s32[]{:T(128)S(6)} %select_n.28, bf16[1024,512]{1,0:T(8,128)(2,1)S(1)} %get-tuple-element.18, bf16[1024,512]{1,0:T(8,128)(2,1)S(1)} %get-tuple-element.17), kind=kOutput, calls=%fused_computation | convolution fusion | flops 2157969408 | bytes 15728644 | tf_op jit(solution)/shard_map/tk,dk->td/dot_general | solution.py:58
  144.1 3.5 %copy.23 = bf16[128,8,8,256]{3,2,1,0:T(8,128)(2,1)} copy(bf16[128,8,8,256]{3,1,2,0:T(8,128)(2,1)S(1)} %bitcast.64) | data formatting | bytes 8388608
  147.6 4.9 %all-to-all-start.1 = ((bf16[4,256,8,1,256]{4,2,1,3,0:T(8,128)(2,1)}), bf16[4,256,8,1,256]{4,2,1,3,0:T(8,128)(2,1)}, u32[]{:S(2)}, u32[]{:S(2)}) async-start(bf16[4,256,8,1,256]{4,2,1,3,0:T(8,128)(2,1)} %bitcast.61), calls=%async_computation.2 | async-start | bytes 8388608 | tf_op jit(solution)/shard_map/all_to_all | solution.py:62
  152.5 1.9 dynamic-slice_bitcast_fusion
  154.4 3.0 %collective-permute-start.2 = (bf16[256,1024]{1,0:T(8,128)(2,1)}, bf16[256,1024]{1,0:T(8,128)(2,1)S(1)}, u32[]{:S(2)}, u32[]{:S(2)}) collective-permute-start(bf16[256,1024]{1,0:T(8,128)(2,1)} %dynamic-slice_bitcast_fusion), channel_id=1, source_target_pairs={{0,16},{16,0},{1,17},{17,1},{2,18},{18,2},{3,19},{19,3},{4,20},{20... | collective-permute-start | bytes 1572872 | tf_op jit(solution)/shard_map/ppermute | solution.py:76
  157.4 44.6 %all-to-all-done.1 = bf16[4,256,8,1,256]{4,2,1,3,0:T(8,128)(2,1)} async-done(((bf16[4,256,8,1,256]{4,2,1,3,0:T(8,128)(2,1)}), bf16[4,256,8,1,256]{4,2,1,3,0:T(8,128)(2,1)}, u32[]{:S(2)}, u32[]{:S(2)}) %all-to-all-start.1) | async-done | bytes 4194336 | tf_op jit(solution)/shard_map/all_to_all | solution.py:62
  202.0 7.5 %copy.20 = bf16[4,256,8,1,256]{1,4,0,2,3:T(8,128)(2,1)} copy(bf16[4,256,8,1,256]{4,2,1,3,0:T(8,128)(2,1)} %all-to-all-done.1) | data formatting | bytes 8388608 | tf_op jit(solution)/shard_map/all_to_all | solution.py:62
  209.5 6.5 %copy.21 = bf16[256,8192]{1,0:T(8,128)(2,1)} copy(bf16[256,8192]{0,1:T(8,128)(2,1)} %bitcast.62) | data formatting | bytes 8388608
  216.0 3.4 %fusion.6 = (f32[1,256,1024]{2,1,0:T(8,128)}, bf16[1,256,1024]{2,1,0:T(8,128)(2,1)}, f32[1,256,1024]{2,1,0:T(8,128)}) fusion(bf16[256,1024]{1,0:T(8,128)(2,1)S(1)} %collective-permute-done.2, bf16[2,256,1024]{2,1,0:T(8,128)(2,1)} %reduce-scatter.2.cloned.1.call-done, s32[]{:T(128)S(6)} %select_n.26, f32[1,256,1024]{2,1,0:T(8,128)S(1)} %copy-done.3, ...), kind=kLoop, calls=%fused_computation.20 | loop fusion | flops 4980736 | bytes 6291460 | tf_op jit(solution)/shard_map/broadcast_in_dim | solution.py:93
  (19 shorter events, 0.1 us)
Async XLA Ops:
  7.2 86.4 %all-gather.3.cloned.1.call-start = ((), (), s32[]{:S(2)}) async-start(), calls=%async_computation.3 | async-start | bytes 2621440 | tf_op jit(solution)/shard_map/all_gather | solution.py:30
  20.4 5.4 %copy-start.1 = (bf16[1,256,1024]{2,1,0:T(8,128)(2,1)S(1)}, bf16[1,256,1024]{2,1,0:T(8,128)(2,1)}, u32[]{:S(2)}) copy-start(bf16[1,256,1024]{2,1,0:T(8,128)(2,1)} %param.8) | copy-start | bytes 1572868
  20.4 22.0 %copy-start.2 = (f32[256,1024]{1,0:T(8,128)S(1)}, f32[256,1024]{1,0:T(8,128)}, u32[]{:S(2)}) copy-start(f32[256,1024]{1,0:T(8,128)} %param.9) | copy-start | bytes 3145732
  20.4 67.4 %all-to-all-start = ((bf16[256,8,4,256]{3,1,0,2:T(8,128)(2,1)}), bf16[256,8,4,256]{3,1,0,2:T(8,128)(2,1)}, u32[]{:S(2)}, u32[]{:S(2)}) async-start(bf16[256,8,4,256]{3,1,0,2:T(8,128)(2,1)} %copy.18), calls=%async_computation | async-start | bytes 8388608 | tf_op jit(solution)/shard_map/all_to_all | solution.py:31
  25.9 77.1 %all-gather.5.cloned.1.call-start = ((), (), s32[]{:S(2)}) async-start(), calls=%async_computation.5 | async-start | bytes 1310720 | tf_op jit(solution)/shard_map/all_gather | solution.py:49
  25.9 13.5 %collective-permute-start = (bf16[256,1024]{1,0:T(8,128)(2,1)S(1)}, bf16[256,1024]{1,0:T(8,128)(2,1)S(1)}, u32[]{:S(2)}, u32[]{:S(2)}) collective-permute-start(bf16[256,1024]{1,0:T(8,128)(2,1)S(1)} %bitcast.66), channel_id=1, source_target_pairs={{0,64},{64,0},{1,65},{65,1},{2,66},{66,2},{3,67},{67,3},{4,68},{68... | collective-permute-start | bytes 1572872 | tf_op jit(solution)/shard_map/ppermute | solution.py:36
  39.5 2.9 %collective-permute-start.1 = (f32[256,1024]{1,0:T(8,128)S(1)}, f32[256,1024]{1,0:T(8,128)}, u32[]{:S(2)}, u32[]{:S(2)}) collective-permute-start(f32[256,1024]{1,0:T(8,128)S(1)} %convert_add_fusion.1), channel_id=1, source_target_pairs={{0,32},{32,0},{1,33},{33,1},{2,34},{34,2},{3,35},{35,3},{4,36},{36... | collective-permute-start | bytes 3145736 | tf_op jit(solution)/shard_map/ppermute | solution.py:39
  45.2 170.8 %copy-start = (bf16[256,1024]{1,0:T(8,128)(2,1)}, bf16[256,1024]{1,0:T(8,128)(2,1)S(1)}, u32[]{:S(2)}) copy-start(bf16[256,1024]{1,0:T(8,128)(2,1)S(1)} %get-tuple-element.12) | copy-start | bytes 1572868
  46.0 106.5 %reduce-scatter.2.cloned.1.call-start = ((), (), s32[]{:S(2)}) async-start(), calls=%async_computation.4 | async-start | bytes 5242880 | tf_op jit(solution)/shard_map/reduce_scatter | solution.py:70
  103.0 26.8 %collective-permute-start.3 = (bf16[1024,512]{1,0:T(8,128)(2,1)}, bf16[1024,512]{1,0:T(8,128)(2,1)}, u32[]{:S(2)}, u32[]{:S(2)}) collective-permute-start(bf16[1024,512]{1,0:T(8,128)(2,1)} %all-gather.5.cloned.1.call-done), channel_id=1, source_target_pairs={{0,16},{16,0},{1,17},{17,1},{2,18},{18,2},{3,19},{19,3},{4,20},{20... | collective-permute-start | bytes 3145736 | tf_op jit(solution)/shard_map/ppermute | solution.py:52
  132.9 4.5 %collective-permute-start.4 = (bf16[2048,512]{1,0:T(8,128)(2,1)}, bf16[2048,512]{1,0:T(8,128)(2,1)}, u32[]{:S(2)}, u32[]{:S(2)}) collective-permute-start(bf16[2048,512]{1,0:T(8,128)(2,1)} %pad_maximum_fusion), channel_id=1, source_target_pairs={{0,32},{32,0},{1,33},{33,1},{2,34},{34,2},{3,35},{35,3},{4,36},{36... | collective-permute-start | bytes 6291464 | tf_op jit(solution)/shard_map/ppermute | solution.py:55
  132.9 8.8 %copy-start.5 = (bf16[1024,1024]{1,0:T(8,128)(2,1)S(1)}, bf16[1024,1024]{1,0:T(8,128)(2,1)}, u32[]{:S(2)}) copy-start(bf16[1024,1024]{1,0:T(8,128)(2,1)} %all-gather.3.cloned.1.call-done) | copy-start | bytes 6291460
  147.6 54.4 %all-to-all-start.1 = ((bf16[4,256,8,1,256]{4,2,1,3,0:T(8,128)(2,1)}), bf16[4,256,8,1,256]{4,2,1,3,0:T(8,128)(2,1)}, u32[]{:S(2)}, u32[]{:S(2)}) async-start(bf16[4,256,8,1,256]{4,2,1,3,0:T(8,128)(2,1)} %bitcast.61), calls=%async_computation.2 | async-start | bytes 8388608 | tf_op jit(solution)/shard_map/all_to_all | solution.py:62
  154.4 61.6 %collective-permute-start.2 = (bf16[256,1024]{1,0:T(8,128)(2,1)}, bf16[256,1024]{1,0:T(8,128)(2,1)S(1)}, u32[]{:S(2)}, u32[]{:S(2)}) collective-permute-start(bf16[256,1024]{1,0:T(8,128)(2,1)} %dynamic-slice_bitcast_fusion), channel_id=1, source_target_pairs={{0,16},{16,0},{1,17},{17,1},{2,18},{18,2},{3,19},{19,3},{4,20},{20... | collective-permute-start | bytes 1572872 | tf_op jit(solution)/shard_map/ppermute | solution.py:76
  209.5 6.5 %copy-start.3 = (f32[1,256,1024]{2,1,0:T(8,128)S(1)}, f32[1,256,1024]{2,1,0:T(8,128)}, u32[]{:S(2)}) copy-start(f32[1,256,1024]{2,1,0:T(8,128)} %param.11) | copy-start | bytes 3145732
  209.5 6.5 %copy-start.4 = (f32[1,256,1024]{2,1,0:T(8,128)S(1)}, f32[1,256,1024]{2,1,0:T(8,128)}, u32[]{:S(2)}) copy-start(f32[1,256,1024]{2,1,0:T(8,128)} %param.10) | copy-start | bytes 3145732
Sparse Core Ops, SparseCore 0:
  9.6 45.5 all-gather.2
  57.5 22.5 all-gather.4
  103.1 44.4 reduce-scatter.1

commit v13 on v11

--- a/solution.py
+++ b/solution.py
@@ -28,16 +28,18 @@
     team = lax.axis_size(TEAM)
 
     cot_team = lax.all_gather(key_cotangent, TEAM, axis=0, tiled=True)
-    inputs_part = lax.all_to_all(
-        inputs.reshape(tok, teams, team, rows), TEAM, split_axis=2, concat_axis=0, tiled=True
-    ).reshape(team * tok, teams * rows)
 
     own = pseudo_grads[0]
-    pair = own.astype(jnp.float32) + lax.ppermute(own, "y_lo", perm=[(0, 1), (1, 0)]).astype(
-        jnp.float32
-    )
+    cols = inputs.reshape(tok, teams, team, rows).transpose(2, 1, 0, 3)
+    got, cols = lax.optimization_barrier((lax.ppermute(own, "y_lo", perm=[(0, 1), (1, 0)]), cols))
+    pair = own.astype(jnp.float32) + got.astype(jnp.float32)
     total = pair + lax.ppermute(pair, "core", perm=[(0, 1), (1, 0)])
     mean_delta = total / workers
+    inputs_part = (
+        lax.all_to_all(cols, TEAM, split_axis=0, concat_axis=0, tiled=True)
+        .transpose(0, 2, 1, 3)
+        .reshape(team * tok, teams * rows)
+    )
     new_moment = MOMENTUM * outer_moment + mean_delta
     new_anchor = (
         anchor.astype(jnp.float32) - OUTER_RATE * (mean_delta + MOMENTUM * new_moment)

time: 199 us -> 202 us (1.015)
  waiting for transfers between devices: 104 us -> 109 us
    ppermute x1, waiting for transfers between devices: 12.3 us -> 0.01 us  [per_device(): lax.ppermute(own, 'y_lo', perm=[(0, 1), (1, 0)])]
    all_to_all x1, waiting for transfers between devices: 46.6 us -> 55.6 us  [per_device(): lax.all_to_all(cols, TEAM, split_axis=0, concat_axis=0, tiled=True)]
    all_gather x1, waiting for transfers between devices: 0.02 us -> 7.11 us  [per_device(): lax.all_gather(lax.dynamic_slice_in_dim(new_anchor, core * half, half, ax...]
    reduce_scatter x1, waiting for transfers between devices: 26.4 us -> 29.7 us  [per_device(): lax.psum_scatter(partial.reshape(hi, -1, kv), 'x', scatter_dimension=1, t...]
    all_to_all x1, waiting for transfers between devices: 17.7 us -> 14.9 us  [per_device(): lax.all_to_all(input_part.reshape(team, tok, teams, 1, rows), TEAM, split...]
  transfers between devices with their start and end apart: 9 -> 9, of which waited for: 4 -> 5; matrix products, arithmetic and copies ran while one was open for 31% -> 30% of each run, Pallas kernels for 0% -> 0%
where the time goes in v13:
time: 202 us; the launch traced here: 200 us
  waiting for transfers between devices  109 us (54%)
  local copies, waits for them, and re-layouts  38.3 us (19%)
  matrix products  17.4 us (9%)
  starting transfers between devices  15.1 us (7%)
  between operations  13.8 us (7%)
  other arithmetic  7.26 us (4%)
    all_to_all x1, waiting for transfers between devices, per_device(): lax.all_to_all(cols, TEAM, split_axis=0, concat_axis=0, tiled=True)  55.6 us
    reduce_scatter x1, waiting for transfers between devices, per_device(): lax.psum_scatter(partial.reshape(hi, -1, kv), 'x', scatter_dimension=1, t...  29.7 us
    unnamed x17, local copies, waits for them, and re-layouts  15.7 us
    all_to_all x1, waiting for transfers between devices, per_device(): lax.all_to_all(input_part.reshape(team, tok, teams, 1, rows), TEAM, split...  14.9 us
    reshape x2, local copies, waits for them, and re-layouts, per_device(): cols = inputs.reshape(tok, teams, team, rows).transpose(2, 1, 0, 3)  12.5 us
    dot_general x1, matrix products, per_device(): jnp.einsum('td,tk->dk', inputs_part, cot_team, preferred_element_type=jnp...  9.41 us
    all_to_all x1, local copies, waits for them, and re-layouts, per_device(): lax.all_to_all(input_part.reshape(team, tok, teams, 1, rows), TEAM, split...  7.5 us
    all_gather x1, waiting for transfers between devices, per_device(): lax.all_gather(lax.dynamic_slice_in_dim(new_anchor, core * half, half, ax...  7.11 us
  transfers between devices with their start and end apart: 9, of which 5 were waited for; matrix products, arithmetic and copies ran while one was open for 30% of the time, Pallas kernels for 0%

profile of v13, /device:TPU:6, one launch (start us, length us, event | category | flops | bytes accessed | tf_op | source)
XLA Modules:
  0.0 200.3 jit_solution(11098621884716397766)
XLA Ops:
  7.2 0.0 all-gather.3.cloned.1.call-start
  7.2 0.7 all-gather.3.cloned.1.call-update
  7.9 1.7 collective-permute-start
  9.6 7.8 %reshape.34 = bf16[256,8,4,256]{3,2,1,0:T(4,128)(2,1)} reshape(bf16[256,8192]{1,0:T(8,128)(2,1)} %param.12) | data formatting | bytes 8388608 | tf_op jit(solution)/shard_map/reshape | solution.py:33
  17.4 4.7 %copy.25 = bf16[256,8,4,256]{3,1,0,2:T(8,128)(2,1)} copy(bf16[256,8,4,256]{3,2,1,0:T(4,128)(2,1)} %reshape.34) | data formatting | bytes 8388608 | tf_op jit(solution)/shard_map/reshape | solution.py:33
  22.1 0.0 collective-permute-done
  22.1 1.1 convert_add_fusion.1
  23.2 0.0 collective-permute-start.1
  23.3 5.5 %all-to-all-start = ((bf16[4,8,256,256]{3,1,2,0:T(8,128)(2,1)}), bf16[4,8,256,256]{3,1,2,0:T(8,128)(2,1)}, u32[]{:S(2)}, u32[]{:S(2)}) async-start(bf16[4,8,256,256]{3,1,2,0:T(8,128)(2,1)} %bitcast.62), calls=%async_computation | async-start | bytes 8388608 | tf_op jit(solution)/shard_map/all_to_all | solution.py:39
  28.7 0.0 collective-permute-done.1
  28.7 2.7 %subtract_convert_fusion.1 = (bf16[256,1024]{1,0:T(8,128)(2,1)S(1)}, f32[256,1024]{1,0:T(8,128)}) fusion(bf16[256,1024]{1,0:T(8,128)(2,1)S(1)} %copy-done.5, f32[256,1024]{1,0:T(8,128)} %collective-permute-done.1, bf16[256,1024]{1,0:T(8,128)(2,1)S(1)} %collective-permute-done, bf16[1,256,1024]{2,1,0:T(8,128)(2,1)S(1)} %copy-done.1, f32[256,1024]{1,0:T(8,128)S(1)} %copy-done.2), kind=kLoop, calls=%fused_computation.11 | loop fusion | flops 3407872 | bytes 5242880 | tf_op jit(solution)/shard_map/convert_element_type | solution.py:46
  31.4 0.8 constant_dynamic-slice_fusion
  32.2 0.0 all-gather.5.cloned.1.call-update
  32.2 0.0 reduce-scatter.2.cloned.1.call-start
  32.3 55.6 %all-to-all-done = bf16[4,8,256,256]{3,1,2,0:T(8,128)(2,1)} async-done(((bf16[4,8,256,256]{3,1,2,0:T(8,128)(2,1)}), bf16[4,8,256,256]{3,1,2,0:T(8,128)(2,1)}, u32[]{:S(2)}, u32[]{:S(2)}) %all-to-all-start) | async-done | bytes 4194336 | tf_op jit(solution)/shard_map/all_to_all | solution.py:39
  87.9 5.7 %copy.22 = bf16[128,8,8,256]{3,1,2,0:T(8,128)(2,1)} copy(bf16[128,8,8,256]{3,2,1,0:T(8,128)(2,1)} %bitcast.19) | data formatting | bytes 8388608
  93.6 9.4 %multiply_convert_fusion.1 = bf16[2048,1024]{1,0:T(8,128)(2,1)} fusion(bf16[1024,2048]{1,0:T(8,128)(2,1)} %bitcast.66, bf16[1024,1024]{1,0:T(8,128)(2,1)} %all-gather.3.cloned.1.call-done), kind=kOutput, calls=%fused_computation.1 | convolution fusion | flops 4299161600 | bytes 10485760 | tf_op jit(solution)/shard_map/td,tk->dk/dot_general | solution.py:66
  103.0 0.0 reduce-scatter.2.cloned.1.call-update
  103.0 7.1 %all-gather.5.cloned.1.call-done = bf16[2048,512]{1,0:T(8,128)(2,1)} async-done(((bf16[256,512]{1,0:T(8,128)(2,1)}), bf16[2048,512]{1,0:T(8,128)(2,1)}) %all-gather.5.cloned.1.call-update) | async-done | bytes 2097168 | tf_op jit(solution)/shard_map/all_gather | solution.py:51
  110.1 0.0 collective-permute-start.3
  110.1 4.0 %fusion.2 = f32[1024,2048]{1,0:T(8,128)S(1)} fusion(bf16[2048,512]{1,0:T(8,128)(2,1)} %all-gather.5.cloned.1.call-done, bf16[1024,1024]{1,0:T(8,128)(2,1)S(1)} %copy-done.6, s32[]{:T(128)S(6)} %select_n.16), kind=kOutput, calls=%fused_computation.8 | convolution fusion | flops 2147483648 | bytes 11534340 | tf_op jit(solution)/shard_map/tk,dk->td/dot_general | solution.py:57
  114.1 0.5 collective-permute-done.3
  114.6 4.0 %multiply_convert_fusion = bf16[1024,2048]{1,0:T(8,128)(2,1)S(1)} fusion(f32[1024,2048]{1,0:T(8,128)S(1)} %fusion.2, bf16[2048,512]{1,0:T(8,128)(2,1)} %collective-permute-done.3, bf16[1024,1024]{1,0:T(8,128)(2,1)S(1)} %copy-done.6, s32[]{:T(128)S(6)} %select_n.17), kind=kOutput, calls=%fused_computation | convolution fusion | flops 2153775104 | bytes 15728644 | tf_op jit(solution)/shard_map/tk,dk->td/dot_general | solution.py:59
  118.6 3.5 %copy.23 = bf16[128,8,8,256]{3,2,1,0:T(8,128)(2,1)} copy(bf16[128,8,8,256]{3,1,2,0:T(8,128)(2,1)S(1)} %bitcast.67) | data formatting | bytes 8388608
  122.1 4.9 %all-to-all-start.1 = ((bf16[4,256,8,1,256]{4,2,1,3,0:T(8,128)(2,1)}), bf16[4,256,8,1,256]{4,2,1,3,0:T(8,128)(2,1)}, u32[]{:S(2)}, u32[]{:S(2)}) async-start(bf16[4,256,8,1,256]{4,2,1,3,0:T(8,128)(2,1)} %bitcast.63), calls=%async_computation.2 | async-start | bytes 8388608 | tf_op jit(solution)/shard_map/all_to_all | solution.py:61
  127.0 29.7 %reduce-scatter.2.cloned.1.call-done = bf16[2,256,1024]{2,1,0:T(8,128)(2,1)} async-done(((bf16[2,1024,1024]{2,1,0:T(8,128)(2,1)}), bf16[2,256,1024]{2,1,0:T(8,128)(2,1)}) %reduce-scatter.2.cloned.1.call-update) | async-done | bytes 1048592 | tf_op jit(solution)/shard_map/reduce_scatter | solution.py:69
  156.6 1.9 dynamic-slice_bitcast_fusion
  158.5 3.0 %collective-permute-start.2 = (bf16[256,1024]{1,0:T(8,128)(2,1)}, bf16[256,1024]{1,0:T(8,128)(2,1)S(1)}, u32[]{:S(2)}, u32[]{:S(2)}) collective-permute-start(bf16[256,1024]{1,0:T(8,128)(2,1)} %dynamic-slice_bitcast_fusion), channel_id=1, source_target_pairs={{0,16},{16,0},{1,17},{17,1},{2,18},{18,2},{3,19},{19,3},{4,20},{20... | collective-permute-start | bytes 1572872 | tf_op jit(solution)/shard_map/ppermute | solution.py:75
  161.5 14.9 %all-to-all-done.1 = bf16[4,256,8,1,256]{4,2,1,3,0:T(8,128)(2,1)} async-done(((bf16[4,256,8,1,256]{4,2,1,3,0:T(8,128)(2,1)}), bf16[4,256,8,1,256]{4,2,1,3,0:T(8,128)(2,1)}, u32[]{:S(2)}, u32[]{:S(2)}) %all-to-all-start.1) | async-done | bytes 4194336 | tf_op jit(solution)/shard_map/all_to_all | solution.py:61
  176.4 7.5 %copy.20 = bf16[4,256,8,1,256]{1,4,0,2,3:T(8,128)(2,1)} copy(bf16[4,256,8,1,256]{4,2,1,3,0:T(8,128)(2,1)} %all-to-all-done.1) | data formatting | bytes 8388608 | tf_op jit(solution)/shard_map/all_to_all | solution.py:61
  183.9 6.5 %copy.21 = bf16[256,8192]{1,0:T(8,128)(2,1)} copy(bf16[256,8192]{0,1:T(8,128)(2,1)} %bitcast.64) | data formatting | bytes 8388608
  190.3 3.4 %fusion.6 = (f32[1,256,1024]{2,1,0:T(8,128)}, bf16[1,256,1024]{2,1,0:T(8,128)(2,1)}, f32[1,256,1024]{2,1,0:T(8,128)}) fusion(bf16[256,1024]{1,0:T(8,128)(2,1)S(1)} %collective-permute-done.2, bf16[2,256,1024]{2,1,0:T(8,128)(2,1)} %reduce-scatter.2.cloned.1.call-done, s32[]{:T(128)S(6)} %select_n.14, f32[1,256,1024]{2,1,0:T(8,128)S(1)} %copy-done.3, ...), kind=kLoop, calls=%fused_computation.18 | loop fusion | flops 4980736 | bytes 6291460 | tf_op jit(solution)/shard_map/broadcast_in_dim | solution.py:92
  (17 shorter events, 0.0 us)
Async XLA Ops:
  7.2 86.4 %all-gather.3.cloned.1.call-start = ((), (), s32[]{:S(2)}) async-start(), calls=%async_computation.3 | async-start | bytes 2621440 | tf_op jit(solution)/shard_map/all_gather | solution.py:30
  7.9 14.2 %collective-permute-start = (bf16[256,1024]{1,0:T(8,128)(2,1)}, bf16[256,1024]{1,0:T(8,128)(2,1)S(1)}, u32[]{:S(2)}, u32[]{:S(2)}) collective-permute-start(bf16[256,1024]{1,0:T(8,128)(2,1)} %bitcast.68), channel_id=1, source_target_pairs={{0,64},{64,0},{1,65},{65,1},{2,66},{66,2},{3,67},{67,3},{4,68},{68... | collective-permute-start | bytes 1572872 | tf_op jit(solution)/shard_map/ppermute | solution.py:34
  17.4 4.7 %copy-start.1 = (bf16[1,256,1024]{2,1,0:T(8,128)(2,1)S(1)}, bf16[1,256,1024]{2,1,0:T(8,128)(2,1)}, u32[]{:S(2)}) copy-start(bf16[1,256,1024]{2,1,0:T(8,128)(2,1)} %param.8) | copy-start | bytes 1572868
  23.2 5.5 %collective-permute-start.1 = (f32[256,1024]{1,0:T(8,128)}, f32[256,1024]{1,0:T(8,128)}, u32[]{:S(2)}, u32[]{:S(2)}) collective-permute-start(f32[256,1024]{1,0:T(8,128)} %convert_add_fusion.1), channel_id=1, source_target_pairs={{0,32},{32,0},{1,33},{33,1},{2,34},{34,2},{3,35},{35,3},{4,36},{36... | collective-permute-start | bytes 3145736 | tf_op jit(solution)/shard_map/ppermute | solution.py:36
  23.2 5.5 %copy-start.2 = (f32[256,1024]{1,0:T(8,128)S(1)}, f32[256,1024]{1,0:T(8,128)}, u32[]{:S(2)}) copy-start(f32[256,1024]{1,0:T(8,128)} %param.9) | copy-start | bytes 3145732
  23.2 5.5 %copy-start.5 = (bf16[256,1024]{1,0:T(8,128)(2,1)S(1)}, bf16[256,1024]{1,0:T(8,128)(2,1)}, u32[]{:S(2)}) copy-start(bf16[256,1024]{1,0:T(8,128)(2,1)} %param.7) | copy-start | bytes 1572868
  23.3 64.6 %all-to-all-start = ((bf16[4,8,256,256]{3,1,2,0:T(8,128)(2,1)}), bf16[4,8,256,256]{3,1,2,0:T(8,128)(2,1)}, u32[]{:S(2)}, u32[]{:S(2)}) async-start(bf16[4,8,256,256]{3,1,2,0:T(8,128)(2,1)} %bitcast.62), calls=%async_computation | async-start | bytes 8388608 | tf_op jit(solution)/shard_map/all_to_all | solution.py:39
  28.7 81.4 %all-gather.5.cloned.1.call-start = ((), (), s32[]{:S(2)}) async-start(), calls=%async_computation.5 | async-start | bytes 2359296 | tf_op jit(solution)/shard_map/all_gather | solution.py:51
  31.4 158.9 %copy-start = (bf16[256,1024]{1,0:T(8,128)(2,1)}, bf16[256,1024]{1,0:T(8,128)(2,1)S(1)}, u32[]{:S(2)}) copy-start(bf16[256,1024]{1,0:T(8,128)(2,1)S(1)} %get-tuple-element.16) | copy-start | bytes 1572868
  32.2 124.4 %reduce-scatter.2.cloned.1.call-start = ((), (), s32[]{:S(2)}) async-start(), calls=%async_computation.4 | async-start | bytes 5242880 | tf_op jit(solution)/shard_map/reduce_scatter | solution.py:69
  103.0 7.1 %copy-start.6 = (bf16[1024,1024]{1,0:T(8,128)(2,1)S(1)}, bf16[1024,1024]{1,0:T(8,128)(2,1)}, u32[]{:S(2)}) copy-start(bf16[1024,1024]{1,0:T(8,128)(2,1)} %all-gather.3.cloned.1.call-done) | copy-start | bytes 6291460
  110.1 4.5 %collective-permute-start.3 = (bf16[2048,512]{1,0:T(8,128)(2,1)}, bf16[2048,512]{1,0:T(8,128)(2,1)}, u32[]{:S(2)}, u32[]{:S(2)}) collective-permute-start(bf16[2048,512]{1,0:T(8,128)(2,1)} %all-gather.5.cloned.1.call-done), channel_id=1, source_target_pairs={{0,32},{32,0},{1,33},{33,1},{2,34},{34,2},{3,35},{35,3},{4,36},{36... | collective-permute-start | bytes 6291464 | tf_op jit(solution)/shard_map/ppermute | solution.py:54
  122.1 54.3 %all-to-all-start.1 = ((bf16[4,256,8,1,256]{4,2,1,3,0:T(8,128)(2,1)}), bf16[4,256,8,1,256]{4,2,1,3,0:T(8,128)(2,1)}, u32[]{:S(2)}, u32[]{:S(2)}) async-start(bf16[4,256,8,1,256]{4,2,1,3,0:T(8,128)(2,1)} %bitcast.63), calls=%async_computation.2 | async-start | bytes 8388608 | tf_op jit(solution)/shard_map/all_to_all | solution.py:61
  158.5 31.9 %collective-permute-start.2 = (bf16[256,1024]{1,0:T(8,128)(2,1)}, bf16[256,1024]{1,0:T(8,128)(2,1)S(1)}, u32[]{:S(2)}, u32[]{:S(2)}) collective-permute-start(bf16[256,1024]{1,0:T(8,128)(2,1)} %dynamic-slice_bitcast_fusion), channel_id=1, source_target_pairs={{0,16},{16,0},{1,17},{17,1},{2,18},{18,2},{3,19},{19,3},{4,20},{20... | collective-permute-start | bytes 1572872 | tf_op jit(solution)/shard_map/ppermute | solution.py:75
  183.9 6.5 %copy-start.3 = (f32[1,256,1024]{2,1,0:T(8,128)S(1)}, f32[1,256,1024]{2,1,0:T(8,128)}, u32[]{:S(2)}) copy-start(f32[1,256,1024]{2,1,0:T(8,128)} %param.11) | copy-start | bytes 3145732
  183.9 6.5 %copy-start.4 = (f32[1,256,1024]{2,1,0:T(8,128)S(1)}, f32[1,256,1024]{2,1,0:T(8,128)}, u32[]{:S(2)}) copy-start(f32[1,256,1024]{2,1,0:T(8,128)} %param.10) | copy-start | bytes 3145732
Sparse Core Ops, SparseCore 0:
  9.6 42.1 all-gather.2
  54.8 55.2 all-gather.4
  112.5 44.0 reduce-scatter.1

commit v14 on v11

--- a/solution.py
+++ b/solution.py
@@ -52,13 +52,23 @@
     other = lax.ppermute(mine, "core", perm=[(0, 1), (1, 0)])
     cot_mine = lax.dynamic_slice_in_dim(cot_team, core * half, half, axis=1)
     cot_other = lax.dynamic_slice_in_dim(cot_team, (1 - core) * half, half, axis=1)
-    product = jnp.einsum(
-        "tk,dk->td", cot_mine, mine, preferred_element_type=jnp.float32
-    ) + jnp.einsum("tk,dk->td", cot_other, other, preferred_element_type=jnp.float32)
-    input_part = (product * scale).astype(jnp.bfloat16)
-    input_grad = lax.all_to_all(
-        input_part.reshape(team, tok, teams, 1, rows), TEAM, split_axis=0, concat_axis=3, tiled=True
-    ).reshape(tok, width)
+    pieces = []
+    for h in range(2):
+        rows_h = slice(h * (teams // 2) * rows, (h + 1) * (teams // 2) * rows)
+        product = jnp.einsum(
+            "tk,dk->td", cot_mine, mine[rows_h], preferred_element_type=jnp.float32
+        ) + jnp.einsum("tk,dk->td", cot_other, other[rows_h], preferred_element_type=jnp.float32)
+        input_part = (product * scale).astype(jnp.bfloat16)
+        pieces.append(
+            lax.all_to_all(
+                input_part.reshape(team, tok, teams // 2, 1, rows),
+                TEAM,
+                split_axis=0,
+                concat_axis=3,
+                tiled=True,
+            ).reshape(tok, width // 2)
+        )
+    input_grad = jnp.concatenate(pieces, axis=1)
 
     partial = (
         jnp.einsum("td,tk->dk", inputs_part, cot_team, preferred_element_type=jnp.float32) * scale

time: 199 us -> 209 us (1.050)
  waiting for transfers between devices: 104 us -> 99 us
  matrix products: 17.4 us -> 21.5 us
  starting transfers between devices: 15.3 us -> 18.8 us
  local copies, waits for them, and re-layouts: 39.7 us -> 43 us
  other arithmetic: 8.31 us -> 11.3 us
    reduce_scatter x1, waiting for transfers between devices: 26.4 us -> 0.01 us  [per_device(): lax.psum_scatter(partial.reshape(hi, -1, kv), 'x', scatter_dimension=1, t...]
    all_to_all x1 -> x2, waiting for transfers between devices: 17.7 us -> 38.7 us  [per_device(): lax.all_to_all(input_part.reshape(team, tok, teams // 2, 1, rows), TEAM,...]
    reshape x0 -> x2, local copies, waits for them, and re-layouts: none -> 7.28 us  [per_device(): input_part.reshape(team, tok, teams // 2, 1, rows)]
    dot_general x2 -> x4, matrix products: 7.96 us -> 12.1 us  [the longest x2 6.49 us: per_device(): jnp.einsum('tk,dk->td', cot_other, other[rows_h], preferred_element_type=...]
    concatenate x0 -> x1, other arithmetic: none -> 3.81 us  [per_device(): input_grad = jnp.concatenate(pieces, axis=1)]
    all_to_all x1 -> x2, starting transfers between devices: 4.85 us -> 8.25 us  [per_device(): lax.all_to_all(input_part.reshape(team, tok, teams // 2, 1, rows), TEAM,...]
    unnamed x17 -> x20, local copies, waits for them, and re-layouts: 16.9 us -> 13.6 us
    all_to_all x1 -> x2, local copies, waits for them, and re-layouts: 7.5 us -> 6.83 us  [per_device(): lax.all_to_all(input_part.reshape(team, tok, teams // 2, 1, rows), TEAM,...]
  transfers between devices with their start and end apart: 9 -> 10, of which waited for: 4 -> 6; matrix products, arithmetic and copies ran while one was open for 31% -> 33% of each run, Pallas kernels for 0% -> 0%
where the time goes in v14:
time: 209 us; the launch traced here: 207 us
  waiting for transfers between devices  99 us (47%)
  local copies, waits for them, and re-layouts  43 us (21%)
  matrix products  21.5 us (10%)
  starting transfers between devices  18.8 us (9%)
  between operations  13.9 us (7%)
  other arithmetic  11.3 us (5%)
    all_to_all x1, waiting for transfers between devices, per_device(): lax.all_to_all(inputs.reshape(tok, teams, team, rows), TEAM, split_axis=2...  46.4 us
    all_to_all x2, waiting for transfers between devices, per_device(): lax.all_to_all(input_part.reshape(team, tok, teams // 2, 1, rows), TEAM,...  38.7 us
    unnamed x20, local copies, waits for them, and re-layouts  13.6 us
    reshape x2, local copies, waits for them, and re-layouts, per_device(): inputs.reshape(tok, teams, team, rows)  12.6 us
    ppermute x1, waiting for transfers between devices, per_device(): lax.ppermute(own, 'y_lo', perm=[(0, 1), (1, 0)]).astype(jnp.float32)  12.3 us
    dot_general x1, matrix products, per_device(): jnp.einsum('td,tk->dk', inputs_part, cot_team, preferred_element_type=jnp...  9.42 us
    all_to_all x2, starting transfers between devices, per_device(): lax.all_to_all(input_part.reshape(team, tok, teams // 2, 1, rows), TEAM,...  8.25 us
    reshape x2, local copies, waits for them, and re-layouts, per_device(): input_part.reshape(team, tok, teams // 2, 1, rows)  7.28 us
  transfers between devices with their start and end apart: 10, of which 6 were waited for; matrix products, arithmetic and copies ran while one was open for 33% of the time, Pallas kernels for 0%

profile of v14, /device:TPU:6, one launch (start us, length us, event | category | flops | bytes accessed | tf_op | source)
XLA Modules:
  0.0 207.5 jit_solution(14885805577686021356)
XLA Ops:
  7.2 0.7 all-gather.3.cloned.1.call-update
  7.9 1.7 collective-permute-start
  9.6 12.3 %collective-permute-done = bf16[256,1024]{1,0:T(8,128)(2,1)S(1)} collective-permute-done((bf16[256,1024]{1,0:T(8,128)(2,1)}, bf16[256,1024]{1,0:T(8,128)(2,1)S(1)}, u32[]{:S(2)}, u32[]{:S(2)}) %collective-permute-start) | collective-permute-done | bytes 524320 | tf_op jit(solution)/shard_map/ppermute | solution.py:36
  21.9 1.2 convert_add_fusion.1
  23.2 7.8 %reshape.42 = bf16[256,8,4,256]{3,2,1,0:T(4,128)(2,1)} reshape(bf16[256,8192]{1,0:T(8,128)(2,1)} %param.12) | data formatting | bytes 8388608 | tf_op jit(solution)/shard_map/reshape | solution.py:32
  31.0 4.8 %copy.21 = bf16[256,8,4,256]{3,1,0,2:T(8,128)(2,1)} copy(bf16[256,8,4,256]{3,2,1,0:T(4,128)(2,1)} %reshape.42) | data formatting | bytes 8388608 | tf_op jit(solution)/shard_map/reshape | solution.py:32
  35.8 5.4 %all-to-all-start = ((bf16[256,8,4,256]{3,1,0,2:T(8,128)(2,1)}), bf16[256,8,4,256]{3,1,0,2:T(8,128)(2,1)}, u32[]{:S(2)}, u32[]{:S(2)}) async-start(bf16[256,8,4,256]{3,1,0,2:T(8,128)(2,1)} %copy.21), calls=%async_computation | async-start | bytes 8388608 | tf_op jit(solution)/shard_map/all_to_all | solution.py:31
  41.2 2.8 %subtract_convert_fusion.1 = (bf16[256,1024]{1,0:T(8,128)(2,1)S(1)}, f32[256,1024]{1,0:T(8,128)}) fusion(bf16[256,1024]{1,0:T(8,128)(2,1)} %param.7, f32[256,1024]{1,0:T(8,128)} %collective-permute-done.1, bf16[256,1024]{1,0:T(8,128)(2,1)S(1)} %collective-permute-done, bf16[1,256,1024]{2,1,0:T(8,128)(2,1)S(1)} %copy-done.5, f32[256,1024]{1,0:T(8,128)S(1)} %copy-done.6), kind=kLoop, calls=%fused_computation.15 | loop fusion | flops 3407872 | bytes 5242880 | tf_op jit(solution)/shard_map/convert_element_type | solution.py:44
  44.1 0.8 constant_dynamic-slice_fusion
  44.9 46.4 %all-to-all-done = bf16[256,8,4,256]{3,1,0,2:T(8,128)(2,1)} async-done(((bf16[256,8,4,256]{3,1,0,2:T(8,128)(2,1)}), bf16[256,8,4,256]{3,1,0,2:T(8,128)(2,1)}, u32[]{:S(2)}, u32[]{:S(2)}) %all-to-all-start) | async-done | bytes 4194336 | tf_op jit(solution)/shard_map/all_to_all | solution.py:31
  91.3 5.7 %copy.27 = bf16[128,8,8,256]{3,1,2,0:T(8,128)(2,1)} copy(bf16[128,8,8,256]{3,2,1,0:T(8,128)(2,1)} %bitcast.27) | data formatting | bytes 8388608
  97.1 9.4 %multiply_convert_fusion = bf16[2048,1024]{1,0:T(8,128)(2,1)} fusion(bf16[1024,2048]{1,0:T(8,128)(2,1)} %bitcast.66, bf16[1024,1024]{1,0:T(8,128)(2,1)} %all-gather.3.cloned.1.call-done), kind=kOutput, calls=%fused_computation | convolution fusion | flops 4299161600 | bytes 10485760 | tf_op jit(solution)/shard_map/td,tk->dk/dot_general | solution.py:74
  106.6 1.4 copy-done.2
  108.1 2.7 %fusion.2 = f32[1024,1024]{1,0:T(8,128)S(1)} fusion(bf16[2048,512]{1,0:T(8,128)(2,1)} %all-gather.5.cloned.1.call-done, bf16[1024,1024]{1,0:T(8,128)(2,1)S(1)} %copy-done.2, s32[]{:T(128)S(6)} %select_n.16), kind=kOutput, calls=%fused_computation.7 | convolution fusion | flops 1073741824 | bytes 6291460 | tf_op jit(solution)/shard_map/tk,dk->td/dot_general | solution.py:58
  110.7 0.4 collective-permute-done.3
  111.1 2.5 %multiply_convert_fusion.1 = bf16[1024,1024]{1,0:T(8,128)(2,1)S(1)} fusion(f32[1024,1024]{1,0:T(8,128)S(1)} %fusion.2, bf16[2048,512]{1,0:T(8,128)(2,1)} %collective-permute-done.3, bf16[1024,1024]{1,0:T(8,128)(2,1)S(1)} %copy-done.3, s32[]{:T(128)S(6)} %select_n.17), kind=kOutput, calls=%fused_computation.2 | convolution fusion | flops 1076887552 | bytes 8388612 | tf_op jit(solution)/shard_map/tk,dk->td/dot_general | solution.py:60
  113.7 2.8 %reshape.47 = bf16[4,256,4,1,256]{4,2,1,0,3:T(4,128)(2,1)} reshape(bf16[1024,1024]{1,0:T(8,128)(2,1)S(1)} %multiply_convert_fusion.1) | data formatting | bytes 4194304 | tf_op jit(solution)/shard_map/reshape | solution.py:64
  116.4 3.8 %all-to-all-start.2 = ((bf16[4,256,4,1,256]{4,2,1,3,0:T(4,128)(2,1)}), bf16[4,256,4,1,256]{4,2,1,3,0:T(4,128)(2,1)S(1)}, u32[]{:S(2)}, u32[]{:S(2)}) async-start(bf16[4,256,4,1,256]{4,2,1,3,0:T(4,128)(2,1)} %bitcast.62), calls=%async_computation.3 | async-start | bytes 4194304 | tf_op jit(solution)/shard_map/all_to_all | solution.py:63
  120.2 3.0 %fusion.5 = f32[1024,1024]{1,0:T(8,128)S(1)} fusion(bf16[2048,512]{1,0:T(8,128)(2,1)} %all-gather.5.cloned.1.call-done, bf16[1024,1024]{1,0:T(8,128)(2,1)} %all-gather.3.cloned.1.call-done, s32[]{:T(128)S(6)} %select_n.16), kind=kOutput, calls=%fused_computation.10 | convolution fusion | flops 1073741824 | bytes 6291460 | tf_op jit(solution)/shard_map/tk,dk->td/dot_general | solution.py:58
  123.2 3.9 %multiply_convert_fusion.2 = bf16[1024,1024]{1,0:T(8,128)(2,1)} fusion(f32[1024,1024]{1,0:T(8,128)S(1)} %fusion.5, bf16[2048,512]{1,0:T(8,128)(2,1)} %collective-permute-done.3, bf16[1024,1024]{1,0:T(8,128)(2,1)S(1)} %copy-done.4, s32[]{:T(128)S(6)} %select_n.17), kind=kOutput, calls=%fused_computation.3 | convolution fusion | flops 1076887552 | bytes 8388612 | tf_op jit(solution)/shard_map/tk,dk->td/dot_general | solution.py:60
  127.2 4.5 %reshape.45 = bf16[4,256,4,1,256]{4,2,1,0,3:T(4,128)(2,1)} reshape(bf16[1024,1024]{1,0:T(8,128)(2,1)} %multiply_convert_fusion.2) | data formatting | bytes 4194304 | tf_op jit(solution)/shard_map/reshape | solution.py:64
  131.7 15.2 %all-to-all-done.2 = bf16[4,256,4,1,256]{4,2,1,3,0:T(4,128)(2,1)S(1)} async-done(((bf16[4,256,4,1,256]{4,2,1,3,0:T(4,128)(2,1)}), bf16[4,256,4,1,256]{4,2,1,3,0:T(4,128)(2,1)S(1)}, u32[]{:S(2)}, u32[]{:S(2)}) %all-to-all-start.2) | async-done | bytes 2097184 | tf_op jit(solution)/shard_map/all_to_all | solution.py:63
  146.9 4.5 %all-to-all-start.1 = ((bf16[4,256,4,1,256]{4,2,1,3,0:T(4,128)(2,1)}), bf16[4,256,4,1,256]{4,2,1,3,0:T(4,128)(2,1)}, u32[]{:S(2)}, u32[]{:S(2)}) async-start(bf16[4,256,4,1,256]{4,2,1,3,0:T(4,128)(2,1)} %bitcast.61), calls=%async_computation.2 | async-start | bytes 4194304 | tf_op jit(solution)/shard_map/all_to_all | solution.py:63
  151.4 2.6 %copy.25 = bf16[4,256,4,1,256]{1,4,0,2,3:T(8,128)(2,1)} copy(bf16[4,256,4,1,256]{4,2,1,3,0:T(4,128)(2,1)S(1)} %all-to-all-done.2) | data formatting | bytes 4194304 | tf_op jit(solution)/shard_map/all_to_all | solution.py:63
  153.9 23.5 %all-to-all-done.1 = bf16[4,256,4,1,256]{4,2,1,3,0:T(4,128)(2,1)} async-done(((bf16[4,256,4,1,256]{4,2,1,3,0:T(4,128)(2,1)}), bf16[4,256,4,1,256]{4,2,1,3,0:T(4,128)(2,1)}, u32[]{:S(2)}, u32[]{:S(2)}) %all-to-all-start.1) | async-done | bytes 2097184 | tf_op jit(solution)/shard_map/all_to_all | solution.py:63
  177.4 4.3 %copy.23 = bf16[4,256,4,1,256]{1,4,0,2,3:T(8,128)(2,1)} copy(bf16[4,256,4,1,256]{4,2,1,3,0:T(4,128)(2,1)} %all-to-all-done.1) | data formatting | bytes 4194304 | tf_op jit(solution)/shard_map/all_to_all | solution.py:63
  181.7 1.9 dynamic-slice_bitcast_fusion
  183.6 3.2 %collective-permute-start.2 = (bf16[256,1024]{1,0:T(8,128)(2,1)}, bf16[256,1024]{1,0:T(8,128)(2,1)S(1)}, u32[]{:S(2)}, u32[]{:S(2)}) collective-permute-start(bf16[256,1024]{1,0:T(8,128)(2,1)} %dynamic-slice_bitcast_fusion), channel_id=1, source_target_pairs={{0,16},{16,0},{1,17},{17,1},{2,18},{18,2},{3,19},{19,3},{4,20},{20... | collective-permute-start | bytes 1572872 | tf_op jit(solution)/shard_map/ppermute | solution.py:83
  186.8 3.8 %pad_maximum_fusion = bf16[256,8192]{0,1:T(8,128)(2,1)} fusion(bf16[256,4096]{0,1:T(8,128)(2,1)S(1)} %bitcast.63, bf16[256,4096]{0,1:T(8,128)(2,1)} %bitcast.64), kind=kLoop, calls=%fused_computation.1 | loop fusion | flops 8388608 | bytes 8388608 | tf_op jit(solution)/shard_map/concatenate | solution.py:71
  190.6 6.5 %copy.26 = bf16[256,8192]{1,0:T(8,128)(2,1)} copy(bf16[256,8192]{0,1:T(8,128)(2,1)} %pad_maximum_fusion) | data formatting | bytes 8388608
  197.1 0.4 collective-permute-done.2
  197.5 3.4 %fusion.13 = (f32[1,256,1024]{2,1,0:T(8,128)}, bf16[1,256,1024]{2,1,0:T(8,128)(2,1)}, f32[1,256,1024]{2,1,0:T(8,128)}) fusion(bf16[256,1024]{1,0:T(8,128)(2,1)S(1)} %collective-permute-done.2, bf16[2,256,1024]{2,1,0:T(8,128)(2,1)} %reduce-scatter.2.cloned.1.call-done, s32[]{:T(128)S(6)} %select_n.14, f32[1,256,1024]{2,1,0:T(8,128)S(1)} %copy-done.7, ...), kind=kLoop, calls=%fused_computation.26 | loop fusion | flops 4980736 | bytes 6291460 | tf_op jit(solution)/shard_map/broadcast_in_dim | solution.py:100
  (28 shorter events, 0.3 us)
Async XLA Ops:
  7.2 89.9 %all-gather.3.cloned.1.call-start = ((), (), s32[]{:S(2)}) async-start(), calls=%async_computation.4 | async-start | bytes 2621440 | tf_op jit(solution)/shard_map/all_gather | solution.py:30
  7.9 14.0 %collective-permute-start = (bf16[256,1024]{1,0:T(8,128)(2,1)}, bf16[256,1024]{1,0:T(8,128)(2,1)S(1)}, u32[]{:S(2)}, u32[]{:S(2)}) collective-permute-start(bf16[256,1024]{1,0:T(8,128)(2,1)} %bitcast.67), channel_id=1, source_target_pairs={{0,64},{64,0},{1,65},{65,1},{2,66},{66,2},{3,67},{67,3},{4,68},{68... | collective-permute-start | bytes 1572872 | tf_op jit(solution)/shard_map/ppermute | solution.py:36
  23.1 18.1 %collective-permute-start.1 = (f32[256,1024]{1,0:T(8,128)S(1)}, f32[256,1024]{1,0:T(8,128)}, u32[]{:S(2)}, u32[]{:S(2)}) collective-permute-start(f32[256,1024]{1,0:T(8,128)S(1)} %convert_add_fusion.1), channel_id=1, source_target_pairs={{0,32},{32,0},{1,33},{33,1},{2,34},{34,2},{3,35},{35,3},{4,36},{36... | collective-permute-start | bytes 3145736 | tf_op jit(solution)/shard_map/ppermute | solution.py:39
  35.8 5.5 %copy-start.5 = (bf16[1,256,1024]{2,1,0:T(8,128)(2,1)S(1)}, bf16[1,256,1024]{2,1,0:T(8,128)(2,1)}, u32[]{:S(2)}) copy-start(bf16[1,256,1024]{2,1,0:T(8,128)(2,1)} %param.8) | copy-start | bytes 1572868
  35.8 5.5 %copy-start.6 = (f32[256,1024]{1,0:T(8,128)S(1)}, f32[256,1024]{1,0:T(8,128)}, u32[]{:S(2)}) copy-start(f32[256,1024]{1,0:T(8,128)} %param.9) | copy-start | bytes 3145732
  35.8 55.6 %all-to-all-start = ((bf16[256,8,4,256]{3,1,0,2:T(8,128)(2,1)}), bf16[256,8,4,256]{3,1,0,2:T(8,128)(2,1)}, u32[]{:S(2)}, u32[]{:S(2)}) async-start(bf16[256,8,4,256]{3,1,0,2:T(8,128)(2,1)} %copy.21), calls=%async_computation | async-start | bytes 8388608 | tf_op jit(solution)/shard_map/all_to_all | solution.py:31
  41.2 65.3 %all-gather.5.cloned.1.call-start = ((), (), s32[]{:S(2)}) async-start(), calls=%async_computation.6 | async-start | bytes 2359296 | tf_op jit(solution)/shard_map/all_gather | solution.py:49
  44.1 153.4 %copy-start.1 = (bf16[256,1024]{1,0:T(8,128)(2,1)}, bf16[256,1024]{1,0:T(8,128)(2,1)S(1)}, u32[]{:S(2)}) copy-start(bf16[256,1024]{1,0:T(8,128)(2,1)S(1)} %get-tuple-element.12) | copy-start | bytes 1572868
  44.9 136.8 %reduce-scatter.2.cloned.1.call-start = ((), (), s32[]{:S(2)}) async-start(), calls=%async_computation.5 | async-start | bytes 5242880 | tf_op jit(solution)/shard_map/reduce_scatter | solution.py:77
  106.5 1.6 copy-start.2
  106.5 4.6 %collective-permute-start.3 = (bf16[2048,512]{1,0:T(8,128)(2,1)}, bf16[2048,512]{1,0:T(8,128)(2,1)}, u32[]{:S(2)}, u32[]{:S(2)}) collective-permute-start(bf16[2048,512]{1,0:T(8,128)(2,1)} %all-gather.5.cloned.1.call-done), channel_id=1, source_target_pairs={{0,32},{32,0},{1,33},{33,1},{2,34},{34,2},{3,35},{35,3},{4,36},{36... | collective-permute-start | bytes 6291464 | tf_op jit(solution)/shard_map/ppermute | solution.py:52
  108.1 3.0 %copy-start.3 = (bf16[1024,1024]{1,0:T(8,128)(2,1)S(1)}, bf16[1024,1024]{1,0:T(8,128)(2,1)}, u32[]{:S(2)}) copy-start(bf16[1024,1024]{1,0:T(8,128)(2,1)} %all-gather.3.cloned.1.call-done) | copy-start | bytes 6291460
  116.4 30.5 %all-to-all-start.2 = ((bf16[4,256,4,1,256]{4,2,1,3,0:T(4,128)(2,1)}), bf16[4,256,4,1,256]{4,2,1,3,0:T(4,128)(2,1)S(1)}, u32[]{:S(2)}, u32[]{:S(2)}) async-start(bf16[4,256,4,1,256]{4,2,1,3,0:T(4,128)(2,1)} %bitcast.62), calls=%async_computation.3 | async-start | bytes 4194304 | tf_op jit(solution)/shard_map/all_to_all | solution.py:63
  120.2 3.0 %copy-start.4 = (bf16[1024,1024]{1,0:T(8,128)(2,1)S(1)}, bf16[1024,1024]{1,0:T(8,128)(2,1)}, u32[]{:S(2)}) copy-start(bf16[1024,1024]{1,0:T(8,128)(2,1)} %all-gather.3.cloned.1.call-done) | copy-start | bytes 6291460
  146.9 30.5 %all-to-all-start.1 = ((bf16[4,256,4,1,256]{4,2,1,3,0:T(4,128)(2,1)}), bf16[4,256,4,1,256]{4,2,1,3,0:T(4,128)(2,1)}, u32[]{:S(2)}, u32[]{:S(2)}) async-start(bf16[4,256,4,1,256]{4,2,1,3,0:T(4,128)(2,1)} %bitcast.61), calls=%async_computation.2 | async-start | bytes 4194304 | tf_op jit(solution)/shard_map/all_to_all | solution.py:63
  153.9 32.9 %copy-start = (bf16[4,256,4,1,256]{1,4,0,2,3:T(8,128)(2,1)S(1)}, bf16[4,256,4,1,256]{1,4,0,2,3:T(8,128)(2,1)}, u32[]{:S(2)}) copy-start(bf16[4,256,4,1,256]{1,4,0,2,3:T(8,128)(2,1)} %copy.25) | copy-start | bytes 6291460
  183.6 13.9 %collective-permute-start.2 = (bf16[256,1024]{1,0:T(8,128)(2,1)}, bf16[256,1024]{1,0:T(8,128)(2,1)S(1)}, u32[]{:S(2)}, u32[]{:S(2)}) collective-permute-start(bf16[256,1024]{1,0:T(8,128)(2,1)} %dynamic-slice_bitcast_fusion), channel_id=1, source_target_pairs={{0,16},{16,0},{1,17},{17,1},{2,18},{18,2},{3,19},{19,3},{4,20},{20... | collective-permute-start | bytes 1572872 | tf_op jit(solution)/shard_map/ppermute | solution.py:83
  190.6 6.9 %copy-start.7 = (f32[1,256,1024]{2,1,0:T(8,128)S(1)}, f32[1,256,1024]{2,1,0:T(8,128)}, u32[]{:S(2)}) copy-start(f32[1,256,1024]{2,1,0:T(8,128)} %param.11) | copy-start | bytes 3145732
  190.6 6.9 %copy-start.8 = (f32[1,256,1024]{2,1,0:T(8,128)S(1)}, f32[1,256,1024]{2,1,0:T(8,128)}, u32[]{:S(2)}) copy-start(f32[1,256,1024]{2,1,0:T(8,128)} %param.10) | copy-start | bytes 3145732
Sparse Core Ops, SparseCore 0:
  9.6 33.2 all-gather.2
  45.9 55.8 all-gather.4
  106.6 44.1 reduce-scatter.1

commit v15 on v11

--- a/solution.py
+++ b/solution.py
@@ -33,10 +33,19 @@
     ).reshape(team * tok, teams * rows)
 
     own = pseudo_grads[0]
-    pair = own.astype(jnp.float32) + lax.ppermute(own, "y_lo", perm=[(0, 1), (1, 0)]).astype(
+    core = lax.axis_index("core")
+    pair = own.astype(jnp.float32) + lax.ppermute(own, "core", perm=[(0, 1), (1, 0)]).astype(
         jnp.float32
     )
-    total = pair + lax.ppermute(pair, "core", perm=[(0, 1), (1, 0)])
+    share = lax.dynamic_slice_in_dim(pair, core * (rows // 2), rows // 2, axis=0).astype(
+        jnp.bfloat16
+    )
+    done = share.astype(jnp.float32) + lax.ppermute(
+        share, "y_lo", perm=[(0, 1), (1, 0)]
+    ).astype(jnp.float32)
+    rest = lax.ppermute(done, "core", perm=[(0, 1), (1, 0)])
+    low = core == 0
+    total = jnp.concatenate([jnp.where(low, done, rest), jnp.where(low, rest, done)], axis=0)
     mean_delta = total / workers
     new_moment = MOMENTUM * outer_moment + mean_delta
     new_anchor = (

time: 199 us -> 195 us (0.980)
  other arithmetic: 8.31 us -> 5.93 us
  waiting for transfers between devices: 104 us -> 102 us
    ppermute x2 -> x3, waiting for transfers between devices: 12.3 us -> 8.87 us  [the longest x1 6.77 us: per_device(): lax.ppermute(share, 'y_lo', perm=[(0, 1), (1, 0)]).astype(jnp.float32)]
    add x1, other arithmetic: 2.19 us -> 0.06 us  [per_device(): share.astype(jnp.float32)]
    unnamed x17 -> x15, local copies, waits for them, and re-layouts: 16.9 us -> 16.9 us
  transfers between devices with their start and end apart: 9 -> 10, of which waited for: 4 -> 5; matrix products, arithmetic and copies ran while one was open for 31% -> 30% of each run, Pallas kernels for 0% -> 0%
where the time goes in v15:
time: 195 us; the launch traced here: 194 us
  waiting for transfers between devices  102 us (52%)
  local copies, waits for them, and re-layouts  39.7 us (20%)
  matrix products  17.4 us (9%)
  starting transfers between devices  15.5 us (8%)
  between operations  13.9 us (7%)
  other arithmetic  5.93 us (3%)
    all_to_all x1, waiting for transfers between devices, per_device(): lax.all_to_all(inputs.reshape(tok, teams, team, rows), TEAM, split_axis=2...  47.9 us
    reduce_scatter x1, waiting for transfers between devices, per_device(): lax.psum_scatter(partial.reshape(hi, -1, kv), 'x', scatter_dimension=1, t...  26.6 us
    all_to_all x1, waiting for transfers between devices, per_device(): lax.all_to_all(input_part.reshape(team, tok, teams, 1, rows), TEAM, split...  17.6 us
    unnamed x15, local copies, waits for them, and re-layouts  16.9 us
    reshape x2, local copies, waits for them, and re-layouts, per_device(): inputs.reshape(tok, teams, team, rows)  12.6 us
    dot_general x1, matrix products, per_device(): jnp.einsum('td,tk->dk', inputs_part, cot_team, preferred_element_type=jnp...  9.4 us
    all_to_all x1, local copies, waits for them, and re-layouts, per_device(): lax.all_to_all(input_part.reshape(team, tok, teams, 1, rows), TEAM, split...  7.5 us
    ppermute x1, waiting for transfers between devices, per_device(): lax.ppermute(share, 'y_lo', perm=[(0, 1), (1, 0)]).astype(jnp.float32)  6.77 us
  transfers between devices with their start and end apart: 10, of which 5 were waited for; matrix products, arithmetic and copies ran while one was open for 30% of the time, Pallas kernels for 0%

profile of v15, /device:TPU:6, one launch (start us, length us, event | category | flops | bytes accessed | tf_op | source)
XLA Modules:
  0.0 194.1 jit_solution(5287596152504438309)
XLA Ops:
  7.2 0.0 all-gather.3.cloned.1.call-start
  7.2 0.7 all-gather.3.cloned.1.call-update
  7.9 0.1 collective-permute-start
  8.0 2.1 %collective-permute-done = bf16[256,1024]{1,0:T(8,128)(2,1)S(1)} collective-permute-done((bf16[256,1024]{1,0:T(8,128)(2,1)}, bf16[256,1024]{1,0:T(8,128)(2,1)S(1)}, u32[]{:S(2)}, u32[]{:S(2)}) %collective-permute-start) | collective-permute-done | bytes 524320 | tf_op jit(solution)/shard_map/ppermute | solution.py:37
  10.1 1.0 add_convert_fusion
  11.1 1.7 collective-permute-start.1
  12.8 6.8 %collective-permute-done.1 = bf16[128,1024]{1,0:T(8,128)(2,1)S(1)} collective-permute-done((bf16[128,1024]{1,0:T(8,128)(2,1)S(1)}, bf16[128,1024]{1,0:T(8,128)(2,1)S(1)}, u32[]{:S(2)}, u32[]{:S(2)}) %collective-permute-start.1) | collective-permute-done | bytes 262176 | tf_op jit(solution)/shard_map/ppermute | solution.py:43
  19.5 0.1 convert_add_fusion.1
  19.6 0.1 collective-permute-start.2
  19.7 7.8 %reshape.35 = bf16[256,8,4,256]{3,2,1,0:T(4,128)(2,1)} reshape(bf16[256,8192]{1,0:T(8,128)(2,1)} %param.12) | data formatting | bytes 8388608 | tf_op jit(solution)/shard_map/reshape | solution.py:32
  27.6 4.8 %copy.18 = bf16[256,8,4,256]{3,1,0,2:T(8,128)(2,1)} copy(bf16[256,8,4,256]{3,2,1,0:T(4,128)(2,1)} %reshape.35) | data formatting | bytes 8388608 | tf_op jit(solution)/shard_map/reshape | solution.py:32
  32.3 5.4 %all-to-all-start = ((bf16[256,8,4,256]{3,1,0,2:T(8,128)(2,1)}), bf16[256,8,4,256]{3,1,0,2:T(8,128)(2,1)}, u32[]{:S(2)}, u32[]{:S(2)}) async-start(bf16[256,8,4,256]{3,1,0,2:T(8,128)(2,1)} %copy.18), calls=%async_computation | async-start | bytes 8388608 | tf_op jit(solution)/shard_map/all_to_all | solution.py:31
  37.8 0.1 broadcast_select_fusion.1
  37.9 1.3 subtract_convert_fusion.1
  39.2 0.8 constant_dynamic-slice_fusion
  40.0 0.0 reduce-scatter.2.cloned.1.call-start
  40.1 47.9 %all-to-all-done = bf16[256,8,4,256]{3,1,0,2:T(8,128)(2,1)} async-done(((bf16[256,8,4,256]{3,1,0,2:T(8,128)(2,1)}), bf16[256,8,4,256]{3,1,0,2:T(8,128)(2,1)}, u32[]{:S(2)}, u32[]{:S(2)}) %all-to-all-start) | async-done | bytes 4194336 | tf_op jit(solution)/shard_map/all_to_all | solution.py:31
  87.9 5.7 %copy.22 = bf16[128,8,8,256]{3,1,2,0:T(8,128)(2,1)} copy(bf16[128,8,8,256]{3,2,1,0:T(8,128)(2,1)} %bitcast.21) | data formatting | bytes 8388608
  93.6 9.4 %multiply_convert_fusion.1 = bf16[2048,1024]{1,0:T(8,128)(2,1)} fusion(bf16[1024,2048]{1,0:T(8,128)(2,1)} %bitcast.59, bf16[1024,1024]{1,0:T(8,128)(2,1)} %all-gather.3.cloned.1.call-done), kind=kOutput, calls=%fused_computation.1 | convolution fusion | flops 4299161600 | bytes 10485760 | tf_op jit(solution)/shard_map/td,tk->dk/dot_general | solution.py:73
  103.1 0.3 collective-permute-start.4
  103.4 1.3 copy-done.5
  104.6 4.0 %fusion.2 = f32[1024,2048]{1,0:T(8,128)S(1)} fusion(bf16[2048,512]{1,0:T(8,128)(2,1)} %all-gather.5.cloned.1.call-done, bf16[1024,1024]{1,0:T(8,128)(2,1)S(1)} %copy-done.5, s32[]{:T(128)S(6)} %select_n.35), kind=kOutput, calls=%fused_computation.8 | convolution fusion | flops 2147483648 | bytes 11534340 | tf_op jit(solution)/shard_map/tk,dk->td/dot_general | solution.py:64
  108.6 4.0 %multiply_convert_fusion = bf16[1024,2048]{1,0:T(8,128)(2,1)S(1)} fusion(f32[1024,2048]{1,0:T(8,128)S(1)} %fusion.2, bf16[2048,512]{1,0:T(8,128)(2,1)} %collective-permute-done.4, bf16[1024,1024]{1,0:T(8,128)(2,1)S(1)} %copy-done.5, s32[]{:T(128)S(6)} %select_n.36), kind=kOutput, calls=%fused_computation | convolution fusion | flops 2153775104 | bytes 15728644 | tf_op jit(solution)/shard_map/tk,dk->td/dot_general | solution.py:66
  112.6 3.5 %copy.23 = bf16[128,8,8,256]{3,2,1,0:T(8,128)(2,1)} copy(bf16[128,8,8,256]{3,1,2,0:T(8,128)(2,1)S(1)} %bitcast.60) | data formatting | bytes 8388608
  116.1 4.9 %all-to-all-start.1 = ((bf16[4,256,8,1,256]{4,2,1,3,0:T(8,128)(2,1)}), bf16[4,256,8,1,256]{4,2,1,3,0:T(8,128)(2,1)}, u32[]{:S(2)}, u32[]{:S(2)}) async-start(bf16[4,256,8,1,256]{4,2,1,3,0:T(8,128)(2,1)} %bitcast.56), calls=%async_computation.2 | async-start | bytes 8388608 | tf_op jit(solution)/shard_map/all_to_all | solution.py:68
  121.0 26.6 %reduce-scatter.2.cloned.1.call-done = bf16[2,256,1024]{2,1,0:T(8,128)(2,1)} async-done(((bf16[2,1024,1024]{2,1,0:T(8,128)(2,1)}), bf16[2,256,1024]{2,1,0:T(8,128)(2,1)}) %reduce-scatter.2.cloned.1.call-update) | async-done | bytes 1048592 | tf_op jit(solution)/shard_map/reduce_scatter | solution.py:76
  147.6 1.9 dynamic-slice_bitcast_fusion
  149.5 3.0 %collective-permute-start.3 = (bf16[256,1024]{1,0:T(8,128)(2,1)}, bf16[256,1024]{1,0:T(8,128)(2,1)S(1)}, u32[]{:S(2)}, u32[]{:S(2)}) collective-permute-start(bf16[256,1024]{1,0:T(8,128)(2,1)} %dynamic-slice_bitcast_fusion), channel_id=1, source_target_pairs={{0,16},{16,0},{1,17},{17,1},{2,18},{18,2},{3,19},{19,3},{4,20},{20... | collective-permute-start | bytes 1572872 | tf_op jit(solution)/shard_map/ppermute | solution.py:82
  152.5 17.6 %all-to-all-done.1 = bf16[4,256,8,1,256]{4,2,1,3,0:T(8,128)(2,1)} async-done(((bf16[4,256,8,1,256]{4,2,1,3,0:T(8,128)(2,1)}), bf16[4,256,8,1,256]{4,2,1,3,0:T(8,128)(2,1)}, u32[]{:S(2)}, u32[]{:S(2)}) %all-to-all-start.1) | async-done | bytes 4194336 | tf_op jit(solution)/shard_map/all_to_all | solution.py:68
  170.1 7.5 %copy.20 = bf16[4,256,8,1,256]{1,4,0,2,3:T(8,128)(2,1)} copy(bf16[4,256,8,1,256]{4,2,1,3,0:T(8,128)(2,1)} %all-to-all-done.1) | data formatting | bytes 8388608 | tf_op jit(solution)/shard_map/all_to_all | solution.py:68
  177.6 6.5 %copy.21 = bf16[256,8192]{1,0:T(8,128)(2,1)} copy(bf16[256,8192]{0,1:T(8,128)(2,1)} %bitcast.57) | data formatting | bytes 8388608
  184.1 3.4 %fusion.6 = (f32[1,256,1024]{2,1,0:T(8,128)}, bf16[1,256,1024]{2,1,0:T(8,128)(2,1)}, f32[1,256,1024]{2,1,0:T(8,128)}) fusion(bf16[256,1024]{1,0:T(8,128)(2,1)S(1)} %collective-permute-done.3, bf16[2,256,1024]{2,1,0:T(8,128)(2,1)} %reduce-scatter.2.cloned.1.call-done, s32[]{:T(128)S(6)} %select_n.33, f32[1,256,1024]{2,1,0:T(8,128)S(1)} %copy-done.1, ...), kind=kLoop, calls=%fused_computation.20 | loop fusion | flops 4980736 | bytes 6291460 | tf_op jit(solution)/shard_map/broadcast_in_dim | solution.py:99
  (19 shorter events, 0.1 us)
Async XLA Ops:
  7.2 86.5 %all-gather.3.cloned.1.call-start = ((), (), s32[]{:S(2)}) async-start(), calls=%async_computation.3 | async-start | bytes 2621440 | tf_op jit(solution)/shard_map/all_gather | solution.py:30
  7.9 2.2 %collective-permute-start = (bf16[256,1024]{1,0:T(8,128)(2,1)}, bf16[256,1024]{1,0:T(8,128)(2,1)S(1)}, u32[]{:S(2)}, u32[]{:S(2)}) collective-permute-start(bf16[256,1024]{1,0:T(8,128)(2,1)} %bitcast.61), channel_id=1, source_target_pairs={{0,32},{32,0},{1,33},{33,1},{2,34},{34,2},{3,35},{35,3},{4,36},{36... | collective-permute-start | bytes 1572872 | tf_op jit(solution)/shard_map/ppermute | solution.py:37
  11.1 8.4 %collective-permute-start.1 = (bf16[128,1024]{1,0:T(8,128)(2,1)S(1)}, bf16[128,1024]{1,0:T(8,128)(2,1)S(1)}, u32[]{:S(2)}, u32[]{:S(2)}) collective-permute-start(bf16[128,1024]{1,0:T(8,128)(2,1)S(1)} %add_convert_fusion), channel_id=1, source_target_pairs={{0,64},{64,0},{1,65},{65,1},{2,66},{66,2},{3,67},{67,3},{4,68},{68... | collective-permute-start | bytes 786440 | tf_op jit(solution)/shard_map/ppermute | solution.py:43
  19.6 18.2 %collective-permute-start.2 = (f32[128,1024]{1,0:T(8,128)S(1)}, f32[128,1024]{1,0:T(8,128)S(1)}, u32[]{:S(2)}, u32[]{:S(2)}) collective-permute-start(f32[128,1024]{1,0:T(8,128)S(1)} %convert_add_fusion.1), channel_id=1, source_target_pairs={{0,32},{32,0},{1,33},{33,1},{2,34},{34,2},{3,35},{35,3},{4,36},{36... | collective-permute-start | bytes 1572872 | tf_op jit(solution)/shard_map/ppermute | solution.py:46
  32.3 5.6 %copy-start.3 = (f32[256,1024]{1,0:T(8,128)S(1)}, f32[256,1024]{1,0:T(8,128)}, u32[]{:S(2)}) copy-start(f32[256,1024]{1,0:T(8,128)} %param.9) | copy-start | bytes 3145732
  32.3 5.6 %copy-start.4 = (bf16[256,1024]{1,0:T(8,128)(2,1)S(1)}, bf16[256,1024]{1,0:T(8,128)(2,1)}, u32[]{:S(2)}) copy-start(bf16[256,1024]{1,0:T(8,128)(2,1)} %param.7) | copy-start | bytes 1572868
  32.3 55.6 %all-to-all-start = ((bf16[256,8,4,256]{3,1,0,2:T(8,128)(2,1)}), bf16[256,8,4,256]{3,1,0,2:T(8,128)(2,1)}, u32[]{:S(2)}, u32[]{:S(2)}) async-start(bf16[256,8,4,256]{3,1,0,2:T(8,128)(2,1)} %copy.18), calls=%async_computation | async-start | bytes 8388608 | tf_op jit(solution)/shard_map/all_to_all | solution.py:31
  37.8 65.3 %all-gather.5.cloned.1.call-start = ((), (), s32[]{:S(2)}) async-start(), calls=%async_computation.5 | async-start | bytes 2359296 | tf_op jit(solution)/shard_map/all_gather | solution.py:58
  39.2 144.9 %copy-start = (bf16[256,1024]{1,0:T(8,128)(2,1)}, bf16[256,1024]{1,0:T(8,128)(2,1)S(1)}, u32[]{:S(2)}) copy-start(bf16[256,1024]{1,0:T(8,128)(2,1)S(1)} %get-tuple-element.12) | copy-start | bytes 1572868
  40.0 107.6 %reduce-scatter.2.cloned.1.call-start = ((), (), s32[]{:S(2)}) async-start(), calls=%async_computation.4 | async-start | bytes 5242880 | tf_op jit(solution)/shard_map/reduce_scatter | solution.py:76
  103.0 1.6 copy-start.5
  103.1 5.5 %collective-permute-start.4 = (bf16[2048,512]{1,0:T(8,128)(2,1)}, bf16[2048,512]{1,0:T(8,128)(2,1)}, u32[]{:S(2)}, u32[]{:S(2)}) collective-permute-start(bf16[2048,512]{1,0:T(8,128)(2,1)} %all-gather.5.cloned.1.call-done), channel_id=1, source_target_pairs={{0,32},{32,0},{1,33},{33,1},{2,34},{34,2},{3,35},{35,3},{4,36},{36... | collective-permute-start | bytes 6291464 | tf_op jit(solution)/shard_map/ppermute | solution.py:61
  116.1 54.0 %all-to-all-start.1 = ((bf16[4,256,8,1,256]{4,2,1,3,0:T(8,128)(2,1)}), bf16[4,256,8,1,256]{4,2,1,3,0:T(8,128)(2,1)}, u32[]{:S(2)}, u32[]{:S(2)}) async-start(bf16[4,256,8,1,256]{4,2,1,3,0:T(8,128)(2,1)} %bitcast.56), calls=%async_computation.2 | async-start | bytes 8388608 | tf_op jit(solution)/shard_map/all_to_all | solution.py:68
  149.5 34.6 %collective-permute-start.3 = (bf16[256,1024]{1,0:T(8,128)(2,1)}, bf16[256,1024]{1,0:T(8,128)(2,1)S(1)}, u32[]{:S(2)}, u32[]{:S(2)}) collective-permute-start(bf16[256,1024]{1,0:T(8,128)(2,1)} %dynamic-slice_bitcast_fusion), channel_id=1, source_target_pairs={{0,16},{16,0},{1,17},{17,1},{2,18},{18,2},{3,19},{19,3},{4,20},{20... | collective-permute-start | bytes 1572872 | tf_op jit(solution)/shard_map/ppermute | solution.py:82
  177.6 6.5 %copy-start.1 = (f32[1,256,1024]{2,1,0:T(8,128)S(1)}, f32[1,256,1024]{2,1,0:T(8,128)}, u32[]{:S(2)}) copy-start(f32[1,256,1024]{2,1,0:T(8,128)} %param.11) | copy-start | bytes 3145732
  177.6 6.5 %copy-start.2 = (f32[1,256,1024]{2,1,0:T(8,128)S(1)}, f32[1,256,1024]{2,1,0:T(8,128)}, u32[]{:S(2)}) copy-start(f32[1,256,1024]{2,1,0:T(8,128)} %param.10) | copy-start | bytes 3145732
Sparse Core Ops, SparseCore 0:
  9.6 33.2 all-gather.2
  45.9 54.6 all-gather.4
  103.2 44.3 reduce-scatter.1
